TPU v7x, 128 devices: a whole 4x4x4 slice. The times are simulated.
128 devices in a mesh: dp: 32 (over x, z, core), cls: 4 (over y).
Axes of the slice: x: 4, y: 4, z: 4, core: 2. Of those that a mesh axis runs over, the one named last changes fastest.
Arguments:
- images: bfloat16 [4096, 64, 512], P('dp'), may hold values from -12 to 12
- pose_slot: int32 [4096], P('dp'), may hold values from 0 to 4095, as said below
- references: bfloat16 [256, 64, 512], P('cls'), may hold values from -4 to 4
- rotation_response: float32 [36, 512], replicated, may hold values from -1 to 1
- shell_weight: float32 [64], replicated, may hold values from 0.003 to 0.03
- class_lists: int32 [4096, 2], P('dp'), may hold values from 0 to 255, as said below
- class_counts: int32 [256], P('cls'), may hold values from 0 to 19999
Outputs:
- class_gradient: float32 [4, 64, 64, 512], P('cls', 'dp')
- log_evidence: float32 [4096], P('dp')
Inputs may be any that keep to these rules, and one draw needn't show every extreme that they name: `pose_slot`: the particles of each micrograph block of 128 rows land exactly 4 in every pose block of 128 positions; each position is taken once. `class_lists`: each row names 2 different classes. Within each pose block of 128 rows every class that the block names is named by exactly 2 of its rows.
All inputs are finite; a program needn't handle non-finite values.
Results may differ from a plain program's by a relative error of at most 0.04.
Values may be sent and summed in bfloat16 or wider, within the bound.
No kernel may reach another device: no remote copies, remote signals or barrier semaphores. Data moves between devices by JAX's collectives and lax.ppermute only.
A program may use at most 192 MiB of HBM per device.

v0:
```python
import math

import jax
import jax.numpy as jnp
from jax import lax
from jax.sharding import PartitionSpec as P

NSHELL = 64
NANG = 256
LIST = 2
MOST = 2


def combined_all(part, axis, combine):
    gathered = jax.tree.map(lambda a: lax.all_gather(a, axis), part)

    def take(source):
        return jax.tree.map(lambda a: lax.dynamic_index_in_dim(a, source, 0, False), gathered)

    return lax.fori_loop(
        1, lax.axis_size(axis), lambda source, state: combine(state, take(source)), take(0)
    )


def angular_tables(points):
    positions = jnp.arange(points, dtype=jnp.int32)
    product = positions[:, None] * positions[None, :] % points
    angles = product.astype(jnp.float32) * (2.0 * math.pi / points)
    cosine = jnp.cos(angles) / math.sqrt(points)
    sine_part = jnp.sin(angles) / math.sqrt(points)
    upper_half = jnp.concatenate([cosine, -sine_part], axis=1)
    lower_half = jnp.concatenate([sine_part, cosine], axis=1)
    return jnp.concatenate([upper_half, lower_half], axis=0)


def combine(earlier_part, later_part):
    larger = jnp.maximum(earlier_part[0], later_part[0])
    merged = earlier_part[1] * jnp.exp(earlier_part[0] - larger) + later_part[1] * jnp.exp(
        later_part[0] - larger
    )
    return (larger, merged)


def local(
    images, pose_slot, references, rotation_response, shell_weight, class_lists, class_counts
):
    dp_count = lax.axis_size("dp")
    column = lax.axis_index("cls")
    blocksize = images.shape[0]
    per_pair = blocksize // dp_count
    row_width = 2 * NANG
    full_table = angular_tables(NANG)
    forward = full_table.astype(jnp.bfloat16)
    inverse = full_table.T
    target_block = pose_slot // blocksize
    target_row = pose_slot % blocksize
    dest_onehot = (target_block[:, None] == jnp.arange(dp_count, dtype=jnp.int32)[None, :]).astype(
        jnp.int32
    )
    before_dest = jnp.cumsum(dest_onehot, axis=0) - dest_onehot
    within = jnp.sum(before_dest * dest_onehot, axis=1)
    position = target_block * per_pair + within
    rows_index = jnp.arange(blocksize, dtype=jnp.int32)
    send_order = jnp.sum(
        jnp.where(position[None, :] == rows_index[:, None], rows_index[None, :], 0), axis=1
    )
    slot_tags = target_row[send_order].astype(jnp.bfloat16).reshape(dp_count, per_pair)

    def transform(field_rows):
        leading = field_rows.shape[:-1]
        result = jnp.dot(
            field_rows.reshape(-1, row_width), forward, preferred_element_type=jnp.float32
        )
        return result.astype(jnp.bfloat16).reshape(leading + (row_width,))

    outgoing = images[send_order].reshape(dp_count, per_pair, NSHELL, row_width)
    arrived, arrived_tags = (
        lax.all_to_all(outgoing, "dp", split_axis=0, concat_axis=0, tiled=True),
        lax.all_to_all(slot_tags, "dp", split_axis=0, concat_axis=0, tiled=True),
    )
    flat_tags = arrived_tags.reshape(blocksize).astype(jnp.int32)
    source_row = jnp.sum(
        jnp.where(flat_tags[None, :] == rows_index[:, None], rows_index[None, :], 0), axis=1
    )
    image_hat = transform(arrived.reshape((blocksize,) + arrived.shape[2:])[source_row])
    ref_hat = transform(references)
    col_classes = references.shape[0]
    weighted = (ref_hat.astype(jnp.float32) * shell_weight[None, :, None]).astype(jnp.bfloat16)

    def contract(left_op, right_op):
        return jnp.einsum("pjm,kjm->pkm", left_op, right_op, preferred_element_type=jnp.float32)

    image_re = image_hat[..., :NANG]
    image_im = image_hat[..., NANG:]
    ref_re = weighted[..., :NANG]
    ref_im = weighted[..., NANG:]
    cross_term = jnp.concatenate(
        [
            contract(image_re, ref_re) + contract(image_im, ref_im),
            contract(image_im, ref_re) - contract(image_re, ref_im),
        ],
        axis=-1,
    )
    log_prior = jnp.log1p(class_counts.astype(jnp.float32))
    dense_scores = (
        jnp.einsum("pkn,rn->pkr", cross_term, rotation_response, precision=lax.Precision.HIGHEST)
        + log_prior[None, :, None]
    )
    local_class = class_lists - column * col_classes
    inside = (local_class >= 0) & (local_class < col_classes)
    picker = (
        local_class[..., None] == jnp.arange(col_classes, dtype=jnp.int32)[None, None, :]
    ).astype(jnp.float32)
    scores = jnp.einsum("pak,pkr->par", picker, dense_scores, precision=lax.Precision.HIGHEST)
    scores = jnp.where(inside[..., None], scores, -1e30)
    top_local = jnp.max(scores, axis=(1, 2))
    total_local = jnp.sum(
        jnp.where(inside[..., None], jnp.exp(scores - top_local[:, None, None]), 0.0), axis=(1, 2)
    )
    top_score, total_sum = combined_all((top_local, total_local), "cls", combine)
    posterior = (
        jnp.where(inside[..., None], jnp.exp(scores - top_score[:, None, None]), 0.0)
        / total_sum[:, None, None]
    )
    evidence = top_score + jnp.log(total_sum)
    rot_re = rotation_response[:, :NANG]
    rot_im = rotation_response[:, NANG:]
    coef_table = jnp.concatenate([rot_re, -rot_im, rot_re * rot_re + rot_im * rot_im], axis=1)
    coef_rows = jnp.einsum("par,rn->pan", posterior, coef_table, precision=lax.Precision.HIGHEST)
    post_sum = jnp.sum(posterior, axis=2)
    own_ref = ref_hat.astype(jnp.float32)
    entries = blocksize * LIST
    flat_local = local_class.reshape(entries)
    flat_inside = inside.reshape(entries)
    class_onehot = (
        flat_local[:, None] == jnp.arange(col_classes, dtype=jnp.int32)[None, :]
    ).astype(jnp.int32)
    before_class = jnp.cumsum(class_onehot, axis=0) - class_onehot
    slot_rank = jnp.sum(before_class * class_onehot, axis=1)
    slot_id = jnp.where(flat_inside, flat_local * MOST + slot_rank, -1)
    slot_count = col_classes * MOST
    chooser = slot_id[None, :] == jnp.arange(slot_count, dtype=jnp.int32)[:, None]
    particle = jnp.arange(entries, dtype=jnp.int32) // LIST
    slot_particle = jnp.sum(jnp.where(chooser, particle[None, :], 0), axis=1)
    chooser_f = chooser.astype(jnp.float32)
    slot_coef = jnp.dot(
        chooser_f, coef_rows.reshape(entries, 3 * NANG), precision=lax.Precision.HIGHEST
    ).reshape(col_classes, MOST, 1, 3 * NANG)
    slot_weight = jnp.dot(
        chooser_f, post_sum.reshape(entries), precision=lax.Precision.HIGHEST
    ).reshape(col_classes, MOST)
    source = (
        image_hat[slot_particle].reshape(col_classes, MOST, NSHELL, row_width).astype(jnp.float32)
    )
    class_ref = own_ref[:, None]
    coef_re = slot_coef[..., :NANG]
    coef_im = slot_coef[..., NANG : 2 * NANG]
    volume = slot_coef[..., 2 * NANG :]
    grad_re = (
        source[..., :NANG] * coef_re - source[..., NANG:] * coef_im - volume * class_ref[..., :NANG]
    )
    grad_im = (
        source[..., :NANG] * coef_im + source[..., NANG:] * coef_re - volume * class_ref[..., NANG:]
    )
    buffer = jnp.concatenate([grad_re, grad_im], axis=-1).reshape(
        dp_count, col_classes // dp_count, MOST, NSHELL, row_width
    )
    weights_out = slot_weight.reshape(dp_count, col_classes // dp_count, MOST)
    grad_rows = lax.all_to_all(
        buffer.astype(jnp.bfloat16), "dp", split_axis=0, concat_axis=0, tiled=True
    ).astype(buffer.dtype)
    weight_rows = lax.all_to_all(
        weights_out.astype(jnp.bfloat16), "dp", split_axis=0, concat_axis=0, tiled=True
    ).astype(weights_out.dtype)
    numer_sum = jnp.sum(grad_rows, axis=(0, 2))
    scaled = numer_sum / (1.0 + jnp.sum(weight_rows, axis=(0, 2)))[:, None, None]
    result = jnp.dot(scaled.reshape(-1, row_width), inverse, precision=lax.Precision.HIGHEST)
    gradient = result.reshape(numer_sum.shape)
    return (gradient[None], evidence)


def solution(mesh):
    return jax.shard_map(
        local,
        mesh=mesh,
        in_specs=(
            P("dp", None, None),
            P("dp"),
            P("cls", None, None),
            P(),
            P(),
            P("dp", None),
            P("cls"),
        ),
        out_specs=(P("cls", "dp", None, None), P("dp")),
        check_vma=False,
    )
```

profile of v0, /device:TPU:40, one launch (start us, length us, event | category | flops | bytes accessed | tf_op | source)
XLA Modules:
  0.0 490.9 jit_solution(8612517099869755777)
XLA Ops:
  0.6 0.7 and_select_fusion.1
  1.9 1.2 gather_fusion.1
  3.1 0.7 convert_element_type.133
  3.9 8.0 %all-to-all-start.1 = ((bf16[32,1,4]{2,1,0:T(2,128)(2,1)}), bf16[32,1,4]{2,1,0:T(2,128)(2,1)S(1)}, u32[]{:S(2)}, u32[]{:S(2)}) async-start(bf16[32,1,4]{2,1,0:T(2,128)(2,1)} %convert_element_type.133), calls=%async_computation.1 | async-start | bytes 32768 | tf_op jit(solution)/shard_map/all_to_all | solution.py:79
  11.9 9.9 %gather_fusion = bf16[128,64,512]{2,1,0:T(8,128)(2,1)} fusion(bf16[128,64,512]{2,1,0:T(8,128)(2,1)} %param.9, s32[1024]{0:T(1024)S(1)} %pad_clamp_fusion.2), kind=kCustom, calls=%fused_computation | custom fusion | bytes 16777728 | tf_op jit(solution)/shard_map/gather | solution.py:76
  21.9 8.2 %all-to-all-start = ((bf16[32,4,64,512]{3,2,1,0:T(8,128)(2,1)}), bf16[32,4,64,512]{3,2,1,0:T(8,128)(2,1)}, u32[]{:S(2)}, u32[]{:S(2)}) async-start(bf16[32,4,64,512]{3,2,1,0:T(8,128)(2,1)} %bitcast.115), calls=%async_computation | async-start | bytes 16777216 | tf_op jit(solution)/shard_map/all_to_all | solution.py:78
  31.0 1.0 fusion.29
  32.0 1.1 sine_multiply_fusion
  33.1 8.0 %convert_bitcast_fusion = f32[4096,512]{0,1:T(8,128)} fusion(bf16[4096,512]{1,0:T(8,128)(2,1)} %bitcast.118, f32[256,256]{1,0:T(8,128)S(1)} %get-tuple-element.170, f32[256,256]{1,0:T(8,128)S(1)} %get-tuple-element.169, f32[256,256]{1,0:T(8,128)S(1)} %fusion.29), kind=kOutput, calls=%fused_computation.15 | convolution fusion | flops 2153775104 | bytes 13369344 | tf_op jit(solution)/shard_map/dot_general | solution.py:71
  41.1 9.0 %copy.92 = f32[4096,512]{1,0:T(8,128)} copy(f32[4096,512]{0,1:T(8,128)} %convert_bitcast_fusion) | data formatting | bytes 16777216 | tf_op jit(solution)/shard_map/convert_element_type | solution.py:88
  50.1 16.3 %copy.93 = f32[64,64,512]{1,0,2:T(8,128)} copy(f32[64,64,512]{2,1,0:T(8,128)} %bitcast.110) | data formatting | bytes 16777216 | tf_op jit(solution)/shard_map/convert_element_type | solution.py:88
  66.5 0.6 reduce-window.6
  69.6 0.8 broadcast_compare_fusion
  70.3 0.7 fusion.50
  71.0 8.8 %slice_bitcast_fusion.1 = (f32[64,64,256]{2,1,0:T(8,128)}, f32[64,64,256]{2,1,0:T(8,128)}) fusion(f32[64,1,64,512]{3,2,0,1:T(8,128)} %bitcast.111), kind=kLoop, calls=%fused_computation.22 | loop fusion | bytes 16777216 | tf_op jit(solution)/shard_map/mul | solution.py:160
  79.8 2.3 copy-done
  82.1 4.4 multiply_convert_fusion
  86.9 67.2 %all-to-all-done = bf16[32,4,64,512]{3,2,1,0:T(8,128)(2,1)} async-done(((bf16[32,4,64,512]{3,2,1,0:T(8,128)(2,1)}), bf16[32,4,64,512]{3,2,1,0:T(8,128)(2,1)}, u32[]{:S(2)}, u32[]{:S(2)}) %all-to-all-start) | async-done | bytes 8388640 | tf_op jit(solution)/shard_map/all_to_all | solution.py:78
  154.0 10.0 %gather_fusion.2 = bf16[128,64,512]{2,1,0:T(8,128)(2,1)} fusion(bf16[128,64,512]{2,1,0:T(8,128)(2,1)} %bitcast.5, s32[1024]{0:T(1024)S(1)} %pad_clamp_fusion.1), kind=kCustom, calls=%fused_computation.2 | custom fusion | bytes 16777728 | tf_op jit(solution)/shard_map/gather | solution.py:85
  164.0 8.8 %convolution_convert_fusion = bf16[8192,512]{1,0:T(8,128)(2,1)S(1)} fusion(bf16[8192,512]{1,0:T(8,128)(2,1)} %bitcast.117, f32[256,256]{1,0:T(8,128)S(1)} %get-tuple-element.170, f32[256,256]{1,0:T(8,128)S(1)} %get-tuple-element.169, f32[256,256]{1,0:T(8,128)S(1)} %fusion.29), kind=kOutput, calls=%fused_computation.13 | convolution fusion | flops 4301258752 | bytes 17563648 | tf_op jit(solution)/shard_map/dot_general | solution.py:71
  172.8 3.8 fusion.49
  176.6 1.9 copy-done.4
  178.5 7.4 %copy.107 = bf16[128,64,256]{0,1,2:T(8,128)(2,1)} copy(bf16[128,64,256]{2,1,0:T(8,128)(2,1)} %get-tuple-element.157) | data formatting | bytes 8388608
  185.8 7.4 %copy.108 = bf16[128,64,256]{0,1,2:T(8,128)(2,1)} copy(bf16[128,64,256]{2,1,0:T(8,128)(2,1)} %get-tuple-element.158) | data formatting | bytes 8388608
  193.2 8.1 %fusion.52 = f32[256,64,128]{2,1,0:T(8,128)} fusion(bf16[64,64,512]{1,0,2:T(8,128)(2,1)} %multiply_convert_fusion, bf16[128,64,256]{0,1,2:T(8,128)(2,1)} %copy.107), kind=kOutput, calls=%fused_computation.128 | convolution fusion | flops 268435456 | bytes 16777216 | tf_op jit(solution)/shard_map/pjm,kjm->pkm/dot_general | solution.py:91
  201.3 6.6 %fusion.53 = f32[256,64,128]{2,1,0:T(8,128)} fusion(bf16[64,64,512]{1,0,2:T(8,128)(2,1)} %multiply_convert_fusion, bf16[128,64,256]{0,1,2:T(8,128)(2,1)S(1)} %copy-done.2), kind=kOutput, calls=%fused_computation.129 | convolution fusion | flops 268435456 | bytes 16777216 | tf_op jit(solution)/shard_map/pjm,kjm->pkm/dot_general | solution.py:91
  207.9 9.2 %add_bitcast_fusion = f32[128,64,256]{0,1,2:T(8,128)} fusion(f32[256,64,128]{2,1,0:T(8,128)} %fusion.52, bf16[64,64,512]{1,0,2:T(8,128)(2,1)} %multiply_convert_fusion, bf16[128,64,256]{0,1,2:T(8,128)(2,1)S(1)} %copy-done.2), kind=kOutput, calls=%fused_computation.19 | convolution fusion | flops 270532608 | bytes 25165824 | tf_op jit(solution)/shard_map/pjm,kjm->pkm/dot_general | solution.py:91
  217.2 9.2 %subtract_bitcast_fusion = f32[128,64,256]{0,1,2:T(8,128)} fusion(f32[256,64,128]{2,1,0:T(8,128)} %fusion.53, bf16[64,64,512]{1,0,2:T(8,128)(2,1)} %multiply_convert_fusion, bf16[128,64,256]{0,1,2:T(8,128)(2,1)S(1)} %copy-done.1), kind=kOutput, calls=%fused_computation.18 | convolution fusion | flops 270532608 | bytes 25165824 | tf_op jit(solution)/shard_map/pjm,kjm->pkm/dot_general | solution.py:91
  226.4 10.2 %pad_maximum_fusion = f32[128,64,512]{0,1,2:T(8,128)} fusion(f32[128,64,256]{0,1,2:T(8,128)} %subtract_bitcast_fusion, f32[128,64,256]{0,1,2:T(8,128)S(1)} %copy-done.3), kind=kLoop, calls=%fused_computation.10 | loop fusion | flops 4194304 | bytes 33554432 | tf_op jit(solution)/shard_map/concatenate | solution.py:97
  236.6 17.6 %copy.96 = f32[128,64,512]{2,1,0:T(8,128)} copy(f32[128,64,512]{0,1,2:T(8,128)} %pad_maximum_fusion) | data formatting | bytes 33554432 | tf_op jit(solution)/shard_map/concatenate | solution.py:97
  254.3 23.8 %fusion.30 = f32[128,64,36]{1,2,0:T(8,128)S(1)} fusion(f32[128,64,512]{2,1,0:T(8,128)} %copy.96, f32[36,512]{1,0:T(8,128)S(1)} %copy-done.16), kind=kOutput, calls=%fused_computation.65 | convolution fusion | flops 1811939328 | bytes 18030592 | tf_op jit(solution)/shard_map/pkn,rn->pkr/dot_general | solution.py:106
  278.1 2.6 fusion.51
  280.7 2.1 select_reduce_fusion
  282.8 7.9 %all-gather.3 = f32[4,1,128]{2,1,0:T(1,128)S(1)} all-gather(f32[1,1,128]{2,1,0:T(1,128)S(1)} %bitcast.122), channel_id=3, replica_groups=mesh['dp'=32,'cls'=4] {'cls'}, dimensions={0}, use_global_device_ids=true | all-gather | bytes 2560 | tf_op jit(solution)/shard_map/all_gather | solution.py:15
  290.7 9.4 %all-gather.2 = f32[4,1,128]{2,1,0:T(1,128)S(1)} all-gather(f32[1,1,128]{2,1,0:T(1,128)S(1)} %bitcast.121), channel_id=2, replica_groups=mesh['dp'=32,'cls'=4] {'cls'}, dimensions={0}, use_global_device_ids=true | all-gather | bytes 2560 | tf_op jit(solution)/shard_map/all_gather | solution.py:15
  300.5 0.6 fusion.48
  301.1 0.8 fusion.18
  301.9 0.6 copy.98
  303.9 10.0 %gather_fusion.3 = bf16[128,64,512]{2,1,0:T(8,128)(2,1)} fusion(bf16[128,64,512]{2,1,0:T(8,128)(2,1)} %bitcast.114, s32[1024]{0:T(1024)} %pad_clamp_fusion), kind=kCustom, calls=%fused_computation.3 | custom fusion | bytes 16777728 | tf_op jit(solution)/shard_map/gather | solution.py:153
  313.9 11.6 %convert.14 = f32[64,2,64,512]{3,2,1,0:T(8,128)} convert(bf16[64,2,64,512]{3,2,1,0:T(8,128)(2,1)} %bitcast.112) | non-fusion elementwise | flops 4194304 | bytes 25165824 | tf_op jit(solution)/shard_map/convert_element_type | solution.py:153
  325.9 0.7 copy.106
  326.6 5.2 %all-to-all-start.3 = ((bf16[32,2,2]{2,1,0:T(2,128)(2,1)}), bf16[32,2,2]{2,1,0:T(2,128)(2,1)S(1)}, u32[]{:S(2)}, u32[]{:S(2)}) async-start(bf16[32,2,2]{2,1,0:T(2,128)(2,1)} %bitcast.93), calls=%async_computation.3 | async-start | bytes 32768 | tf_op jit(solution)/shard_map/all_to_all | solution.py:172
  331.8 12.8 %subtract_convert_fusion.1 = (bf16[64,2,64,256]{3,2,1,0:T(8,128)(2,1)}, bf16[64,2,64,256]{3,2,1,0:T(8,128)(2,1)}) fusion(f32[64,2,64,512]{3,2,1,0:T(8,128)} %convert.14, f32[64,64,256]{2,1,0:T(8,128)} %get-tuple-element.155, f32[64,2,256]{2,1,0:T(2,128)S(1)} %copy.101, f32[64,2,256]{2,1,0:T(2,128)S(1)} %copy.100, f32[64,2,256]{2,1,0:T(2,128)S(1)} %copy.99, ...), kind=kLoop, calls=%fused_computation.17 | loop fusion | flops 25165824 | bytes 33947648 | tf_op jit(solution)/shard_map/convert.6
  344.6 7.7 %pad_maximum_fusion.1 = bf16[64,2,64,512]{3,2,1,0:T(8,128)(2,1)} fusion(bf16[64,2,64,256]{3,2,1,0:T(8,128)(2,1)} %get-tuple-element.154, bf16[64,2,64,256]{3,2,1,0:T(8,128)(2,1)} %get-tuple-element.153), kind=kLoop, calls=%fused_computation.14 | loop fusion | flops 16777216 | bytes 16777216 | tf_op jit(solution)/shard_map/concatenate | solution.py:165
  352.3 7.4 %all-to-all-start.2 = ((bf16[32,2,2,64,512]{4,3,2,1,0:T(8,128)(2,1)}), bf16[32,2,2,64,512]{4,3,2,1,0:T(8,128)(2,1)}, u32[]{:S(2)}, u32[]{:S(2)}) async-start(bf16[32,2,2,64,512]{4,3,2,1,0:T(8,128)(2,1)} %bitcast.116), calls=%async_computation.2 | async-start | bytes 16777216 | tf_op jit(solution)/shard_map/all_to_all | solution.py:169
  360.5 123.5 %all-to-all-done.2 = bf16[32,2,2,64,512]{4,3,2,1,0:T(8,128)(2,1)} async-done(((bf16[32,2,2,64,512]{4,3,2,1,0:T(8,128)(2,1)}), bf16[32,2,2,64,512]{4,3,2,1,0:T(8,128)(2,1)}, u32[]{:S(2)}, u32[]{:S(2)}) %all-to-all-start.2) | async-done | bytes 8388640 | tf_op jit(solution)/shard_map/all_to_all | solution.py:169
  484.0 4.7 convert_reduce_fusion
  488.7 1.9 convolution_bitcast_fusion.1
  (106 shorter events, 7.2 us)
Async XLA Ops:
  3.9 18.0 %all-to-all-start.1 = ((bf16[32,1,4]{2,1,0:T(2,128)(2,1)}), bf16[32,1,4]{2,1,0:T(2,128)(2,1)S(1)}, u32[]{:S(2)}, u32[]{:S(2)}) async-start(bf16[32,1,4]{2,1,0:T(2,128)(2,1)} %convert_element_type.133), calls=%async_computation.1 | async-start | bytes 32768 | tf_op jit(solution)/shard_map/all_to_all | solution.py:79
  21.9 8.2 %copy-start.24 = (s32[128,2]{0,1:T(2,128)S(1)}, s32[128,2]{0,1:T(2,128)}, u32[]{:S(2)}) copy-start(s32[128,2]{0,1:T(2,128)} %param.14) | copy-start | bytes 3076
  21.9 132.1 %all-to-all-start = ((bf16[32,4,64,512]{3,2,1,0:T(8,128)(2,1)}), bf16[32,4,64,512]{3,2,1,0:T(8,128)(2,1)}, u32[]{:S(2)}, u32[]{:S(2)}) async-start(bf16[32,4,64,512]{3,2,1,0:T(8,128)(2,1)} %bitcast.115), calls=%async_computation | async-start | bytes 16777216 | tf_op jit(solution)/shard_map/all_to_all | solution.py:78
  30.2 0.6 copy-start.11
  32.0 132.0 %copy-start.5 = (f32[256,256]{1,0:T(8,128)}, f32[256,256]{1,0:T(8,128)S(1)}, u32[]{:S(2)}) copy-start(f32[256,256]{1,0:T(8,128)S(1)} %fusion.29) | copy-start | bytes 786436
  33.0 130.9 %copy-start.7 = (f32[256,256]{1,0:T(8,128)}, f32[256,256]{1,0:T(8,128)S(1)}, u32[]{:S(2)}) copy-start(f32[256,256]{1,0:T(8,128)S(1)} %get-tuple-element.169) | copy-start | bytes 786436
  33.1 130.9 %copy-start.9 = (f32[256,256]{1,0:T(8,128)}, f32[256,256]{1,0:T(8,128)S(1)}, u32[]{:S(2)}) copy-start(f32[256,256]{1,0:T(8,128)S(1)} %get-tuple-element.170) | copy-start | bytes 786436
  50.1 18.8 %copy-start.27 = (s32[64]{0:T(128)S(1)}, s32[64]{0:T(128)}, u32[]{:S(2)}) copy-start(s32[64]{0:T(128)} %param.15) | copy-start | bytes 772
  50.1 20.2 %copy-start.15 = (f32[36,512]{1,0:T(8,128)S(1)}, f32[36,512]{1,0:T(8,128)}, u32[]{:S(2)}) copy-start(f32[36,512]{1,0:T(8,128)} %param.12) | copy-start | bytes 221188
  50.1 29.7 %copy-start.25 = (f32[64]{0:T(128)S(1)}, f32[64]{0:T(128)}, u32[]{:S(2)}) copy-start(f32[64]{0:T(128)} %param.13) | copy-start | bytes 772
  66.5 13.3 %copy-start.13 = (pred[128,2]{1,0:T(8,128)(4,1)}, pred[128,2]{1,0:T(8,128)(4,1)S(1)}, u32[]{:S(2)}) copy-start(pred[128,2]{1,0:T(8,128)(4,1)S(1)} %copy.86) | copy-start | bytes 772
  68.2 11.6 %copy-start.21 = (s32[256]{0:T(256)}, s32[256]{0:T(256)S(1)}, u32[]{:S(2)}) copy-start(s32[256]{0:T(256)S(1)} %add_select_fusion.1) | copy-start | bytes 3076
  71.0 11.1 %copy-start = (f32[64,64,512]{1,0,2:T(8,128)S(1)}, f32[64,64,512]{1,0,2:T(8,128)}, u32[]{:S(2)}) copy-start(f32[64,64,512]{1,0,2:T(8,128)} %copy.93) | copy-start | bytes 25165828
  172.7 5.7 %copy-start.4 = (bf16[8192,512]{1,0:T(8,128)(2,1)}, bf16[8192,512]{1,0:T(8,128)(2,1)S(1)}, u32[]{:S(2)}) copy-start(bf16[8192,512]{1,0:T(8,128)(2,1)S(1)} %convolution_convert_fusion) | copy-start | bytes 25165828
  193.2 8.1 %copy-start.2 = (bf16[128,64,256]{0,1,2:T(8,128)(2,1)S(1)}, bf16[128,64,256]{0,1,2:T(8,128)(2,1)}, u32[]{:S(2)}) copy-start(bf16[128,64,256]{0,1,2:T(8,128)(2,1)} %copy.108) | copy-start | bytes 12582916
  207.9 9.3 %copy-start.1 = (bf16[128,64,256]{0,1,2:T(8,128)(2,1)S(1)}, bf16[128,64,256]{0,1,2:T(8,128)(2,1)}, u32[]{:S(2)}) copy-start(bf16[128,64,256]{0,1,2:T(8,128)(2,1)} %copy.107) | copy-start | bytes 12582916
  217.2 9.2 %copy-start.3 = (f32[128,64,256]{0,1,2:T(8,128)S(1)}, f32[128,64,256]{0,1,2:T(8,128)}, u32[]{:S(2)}) copy-start(f32[128,64,256]{0,1,2:T(8,128)} %add_bitcast_fusion) | copy-start | bytes 25165828
  236.6 17.6 %copy-start.16 = (f32[36,512]{1,0:T(8,128)S(1)}, f32[36,512]{1,0:T(8,128)}, u32[]{:S(2)}) copy-start(f32[36,512]{1,0:T(8,128)} %param.12) | copy-start | bytes 221188
  254.2 23.9 %copy-start.12 = (s32[128,2]{1,0:T(8,128)S(1)}, s32[128,2]{1,0:T(8,128)}, u32[]{:S(2)}) copy-start(s32[128,2]{1,0:T(8,128)} %copy-done.11) | copy-start | bytes 3076
  254.2 23.9 %copy-start.14 = (pred[128,2]{1,0:T(8,128)(4,1)S(1)}, pred[128,2]{1,0:T(8,128)(4,1)}, u32[]{:S(2)}) copy-start(pred[128,2]{1,0:T(8,128)(4,1)} %copy-done.13) | copy-start | bytes 772
  254.2 23.9 %copy-start.26 = (f32[64]{0:T(128)S(1)}, f32[64]{0:T(128)}, u32[]{:S(2)}) copy-start(f32[64]{0:T(128)} %convert_log-plus-one_fusion) | copy-start | bytes 772
  254.2 46.9 %copy-start.17 = (f32[36,256]{1,0:T(8,128)S(1)}, f32[36,256]{1,0:T(8,128)}, u32[]{:S(2)}) copy-start(f32[36,256]{1,0:T(8,128)} %get-tuple-element.162) | copy-start | bytes 110596
  254.2 46.9 %copy-start.18 = (f32[36,256]{1,0:T(8,128)S(1)}, f32[36,256]{1,0:T(8,128)}, u32[]{:S(2)}) copy-start(f32[36,256]{1,0:T(8,128)} %get-tuple-element.163) | copy-start | bytes 110596
  254.2 46.9 %copy-start.19 = (f32[36,256]{1,0:T(8,128)S(1)}, f32[36,256]{1,0:T(8,128)}, u32[]{:S(2)}) copy-start(f32[36,256]{1,0:T(8,128)} %get-tuple-element.164) | copy-start | bytes 110596
  254.2 48.9 %copy-start.22 = (s32[256]{0:T(256)S(1)}, s32[256]{0:T(256)}, u32[]{:S(2)}) copy-start(s32[256]{0:T(256)} %copy-done.21) | copy-start | bytes 3076
  254.2 48.9 %copy-start.23 = (s32[64,2]{0,1:T(2,128)S(1)}, s32[64,2]{0,1:T(2,128)}, u32[]{:S(2)}) copy-start(s32[64,2]{0,1:T(2,128)} %multiply_add_fusion.2) | copy-start | bytes 1540
  313.9 11.8 %copy-start.20 = (pred[32,2,2,256]{3,2,1,0:T(4,128)(4,1)S(1)}, pred[32,2,2,256]{3,2,1,0:T(4,128)(4,1)}, u32[]{:S(2)}) copy-start(pred[32,2,2,256]{3,2,1,0:T(4,128)(4,1)} %broadcast_compare_fusion) | copy-start | bytes 98308
  326.6 25.7 %all-to-all-start.3 = ((bf16[32,2,2]{2,1,0:T(2,128)(2,1)}), bf16[32,2,2]{2,1,0:T(2,128)(2,1)S(1)}, u32[]{:S(2)}, u32[]{:S(2)}) async-start(bf16[32,2,2]{2,1,0:T(2,128)(2,1)} %bitcast.93), calls=%async_computation.3 | async-start | bytes 32768 | tf_op jit(solution)/shard_map/all_to_all | solution.py:172
  352.3 131.7 %all-to-all-start.2 = ((bf16[32,2,2,64,512]{4,3,2,1,0:T(8,128)(2,1)}), bf16[32,2,2,64,512]{4,3,2,1,0:T(8,128)(2,1)}, u32[]{:S(2)}, u32[]{:S(2)}) async-start(bf16[32,2,2,64,512]{4,3,2,1,0:T(8,128)(2,1)} %bitcast.116), calls=%async_computation.2 | async-start | bytes 16777216 | tf_op jit(solution)/shard_map/all_to_all | solution.py:169
  359.7 128.9 %copy-start.6 = (f32[256,256]{1,0:T(8,128)S(1)}, f32[256,256]{1,0:T(8,128)}, u32[]{:S(2)}) copy-start(f32[256,256]{1,0:T(8,128)} %copy-done.5) | copy-start | bytes 786436
  359.8 128.9 %copy-start.8 = (f32[256,256]{1,0:T(8,128)S(1)}, f32[256,256]{1,0:T(8,128)}, u32[]{:S(2)}) copy-start(f32[256,256]{1,0:T(8,128)} %copy-done.7) | copy-start | bytes 786436
  359.8 128.9 %copy-start.10 = (f32[256,256]{1,0:T(8,128)S(1)}, f32[256,256]{1,0:T(8,128)}, u32[]{:S(2)}) copy-start(f32[256,256]{1,0:T(8,128)} %copy-done.9) | copy-start | bytes 786436
where the time goes:
time: 496 us; the launch traced here: 491 us
  waiting for transfers between devices  191 us (39%)
  local copies, waits for them, and re-layouts  110 us (22%)
  matrix products  79.7 us (16%)
  other arithmetic  62.4 us (13%)
  starting transfers between devices  28.9 us (6%)
  blocking collectives  17.3 us (3%)
    all_to_all x1, waiting for transfers between devices, local(): lax.all_to_all(buffer.astype(jnp.bfloat16), 'dp', split_axis=0, concat_ax...  123 us
    all_to_all x1, waiting for transfers between devices, local(): lax.all_to_all(outgoing, 'dp', split_axis=0, concat_axis=0, tiled=True)  67.2 us
    dot_general x4, matrix products, contract(): jnp.einsum('pjm,kjm->pkm', left_op, right_op, preferred_element_type=jnp....  33.2 us
    convert_element_type x2, local copies, waits for them, and re-layouts, local(): ref_hat.astype(jnp.float32) * shell_weight[None, :, None]  25.3 us
    dot_general x1, matrix products, local(): jnp.einsum('pkn,rn->pkr', cross_term, rotation_response, precision=lax.Pr...  23.8 us
    unnamed x58, local copies, waits for them, and re-layouts  19.5 us
    concatenate x1, local copies, waits for them, and re-layouts, local(): jnp.concatenate([contract(image_re, ref_re) + contract(image_im, ref_im),...  17.6 us
    all_gather x2, blocking collectives, combined_all(): gathered = jax.tree.map(lambda a: lax.all_gather(a, axis), part)  17.3 us
  transfers between devices with their start and end apart: 4, of which 2 were waited for; matrix products, arithmetic and copies ran while one was open for 17% of the time, Pallas kernels for 0%

commit v1 on v0

v1 whole, which is shorter than its diff:
```python
import math

import jax
import jax.numpy as jnp
from jax import lax
from jax.sharding import PartitionSpec as P

NSHELL = 64
NANG = 256
LIST = 2

HIGHEST = lax.Precision.HIGHEST


def angular_tables(points):
    positions = jnp.arange(points, dtype=jnp.int32)
    product = positions[:, None] * positions[None, :] % points
    angles = product.astype(jnp.float32) * (2.0 * math.pi / points)
    cosine = jnp.cos(angles) / math.sqrt(points)
    sine_part = jnp.sin(angles) / math.sqrt(points)
    upper_half = jnp.concatenate([cosine, -sine_part], axis=1)
    lower_half = jnp.concatenate([sine_part, cosine], axis=1)
    return jnp.concatenate([upper_half, lower_half], axis=0)


def split_bf16(x):
    high = x.astype(jnp.bfloat16)
    low = (x - high.astype(jnp.float32)).astype(jnp.bfloat16)
    return high, low


def local(
    images, pose_slot, references, rotation_response, shell_weight, class_lists, class_counts
):
    dp_index = lax.axis_index("dp")
    column = lax.axis_index("cls")
    blocksize = images.shape[0]
    col_classes = references.shape[0]
    full_table = angular_tables(NANG)
    forward = full_table.astype(jnp.bfloat16)
    inverse = full_table.T

    all_lists = lax.all_gather(class_lists, "dp", tiled=True)
    all_slots = lax.all_gather(pose_slot, "dp", tiled=True)
    my_lists = all_lists[pose_slot]
    local_class = (my_lists - column * col_classes).T
    inside = (local_class >= 0) & (local_class < col_classes)
    class_ids = jnp.arange(col_classes, dtype=jnp.int32)
    pick = local_class[:, None, :] == class_ids[None, :, None]

    image_t = jnp.einsum(
        "pjn,nm->mjp", images, forward, preferred_element_type=jnp.float32
    ).astype(jnp.bfloat16)
    image_re = image_t[:NANG]
    image_im = image_t[NANG:]
    ref_t = jnp.einsum(
        "kjn,nm->mkj", references, forward, preferred_element_type=jnp.float32
    ).astype(jnp.bfloat16)
    weighted_t = (ref_t.astype(jnp.float32) * shell_weight[None, None, :]).astype(jnp.bfloat16)
    w_re = weighted_t[:NANG]
    w_im = weighted_t[NANG:]
    stack_re = jnp.concatenate([w_re, -w_im], axis=1)
    stack_im = jnp.concatenate([w_im, w_re], axis=1)
    cross = jnp.einsum(
        "mkj,mjp->mkp", stack_re, image_re, preferred_element_type=jnp.float32
    ) + jnp.einsum("mkj,mjp->mkp", stack_im, image_im, preferred_element_type=jnp.float32)
    cross = cross.reshape(NANG, 2, col_classes, blocksize)
    cross_sel = jnp.sum(
        jnp.where(pick[None, None], cross[:, :, None], 0.0), axis=3
    )
    rot = rotation_response.reshape(-1, 2, NANG)
    log_prior = jnp.log1p(class_counts.astype(jnp.float32))
    prior_sel = jnp.sum(jnp.where(pick, log_prior[None, :, None], 0.0), axis=1)
    scores = (
        jnp.einsum("rtm,mtap->rap", rot, cross_sel, precision=HIGHEST) + prior_sel[None]
    )
    scores = jnp.where(inside[None], scores, -1e30)
    top_local = jnp.max(scores, axis=(0, 1))
    total_local = jnp.sum(
        jnp.where(inside[None], jnp.exp(scores - top_local[None, None]), 0.0), axis=(0, 1)
    )
    tops = lax.all_gather(top_local, "cls")
    totals = lax.all_gather(total_local, "cls")
    top_score = jnp.max(tops, axis=0)
    total_sum = jnp.sum(totals * jnp.exp(tops - top_score[None]), axis=0)
    posterior = (
        jnp.where(inside[None], jnp.exp(scores - top_score[None, None]), 0.0)
        / total_sum[None, None]
    )
    evidence = top_score + jnp.log(total_sum)

    rot_re = rotation_response[:, :NANG]
    rot_im = rotation_response[:, NANG:]
    coef_table = jnp.concatenate([rot_re, -rot_im, rot_re * rot_re + rot_im * rot_im], axis=1)
    coef = jnp.einsum("rn,rap->nap", coef_table, posterior, precision=HIGHEST)
    coef = coef.reshape(3, NANG, LIST, blocksize)
    post_sum = jnp.sum(posterior, axis=0)
    pick_f = pick.astype(jnp.float32)
    spread = jnp.sum(
        jnp.where(pick[None, None], coef[:2, :, :, None], 0.0), axis=2
    )
    spread = jnp.concatenate([spread[0], spread[1]], axis=1)
    volume = jnp.einsum("map,akp->mk", coef[2], pick_f, precision=HIGHEST)
    denom = jnp.einsum("ap,akp->k", post_sum, pick_f, precision=HIGHEST)
    spread_hi, spread_lo = split_bf16(spread)

    def against(image_part):
        return jnp.einsum(
            "mjp,mqp->mjq", image_part, spread_hi, preferred_element_type=jnp.float32
        ) + jnp.einsum("mjp,mqp->mjq", image_part, spread_lo, preferred_element_type=jnp.float32)

    q_re = against(image_re)
    q_im = against(image_im)
    ref_jk = jnp.swapaxes(ref_t, 1, 2).astype(jnp.float32)
    numer_re = q_re[..., :col_classes] - q_im[..., col_classes:] - volume[:, None, :] * ref_jk[:NANG]
    numer_im = q_re[..., col_classes:] + q_im[..., :col_classes] - volume[:, None, :] * ref_jk[NANG:]
    numer = jnp.concatenate([numer_re, numer_im], axis=0)
    partial = jnp.einsum("mjk,mn->kjn", numer, inverse, precision=lax.Precision.HIGH)
    summed = lax.psum_scatter(partial, "dp", scatter_dimension=0, tiled=True)
    denom_sum = lax.psum_scatter(denom, "dp", scatter_dimension=0, tiled=True)
    gradient = summed / (1.0 + denom_sum)[:, None, None]

    all_evidence = lax.all_gather(evidence, "dp", tiled=True)
    wanted = dp_index * blocksize + jnp.arange(blocksize, dtype=jnp.int32)
    placed = jnp.sum(
        jnp.where(all_slots[None, :] == wanted[:, None], all_evidence[None, :], 0.0), axis=1
    )
    return (gradient[None], placed)


def solution(mesh):
    return jax.shard_map(
        local,
        mesh=mesh,
        in_specs=(
            P("dp", None, None),
            P("dp"),
            P("cls", None, None),
            P(),
            P(),
            P("dp", None),
            P("cls"),
        ),
        out_specs=(P("cls", "dp", None, None), P("dp")),
        check_vma=False,
    )
```

time: 496 us -> 462 us (0.931)
  the two profiles are of different devices: /device:TPU:40 before, /device:TPU:0 now
where the time goes in v1:
time: 462 us; the launch traced here: 455 us
  blocking collectives  147 us (32%)
  matrix products  131 us (28%)
  local copies, waits for them, and re-layouts  82.5 us (18%)
  other arithmetic  79.7 us (17%)
  between operations  15.1 us (3%)
    unnamed x1, blocking collectives  63.3 us
    dot_general x2, matrix products, against(): jnp.einsum('mjp,mqp->mjq', image_part, spread_lo, preferred_element_type=...  32.7 us
    dot_general x2, matrix products, against(): jnp.einsum('mjp,mqp->mjq', image_part, spread_hi, preferred_element_type=...  32.5 us
    all_gather x1, blocking collectives, local(): all_lists = lax.all_gather(class_lists, 'dp', tiled=True)  28 us
    add x2, other arithmetic, against(): jnp.einsum('mjp,mqp->mjq', image_part, spread_hi, preferred_element_type=...  23.7 us
    all_gather x1, blocking collectives, local(): all_slots = lax.all_gather(pose_slot, 'dp', tiled=True)  21.6 us
    dot_general x1, matrix products, local(): jnp.einsum('mkj,mjp->mkp', stack_im, image_im, preferred_element_type=jnp...  19.2 us
    dot_general x2, local copies, waits for them, and re-layouts, against(): jnp.einsum('mjp,mqp->mjq', image_part, spread_lo, preferred_element_type=...  18.5 us
  transfers between devices with their start and end apart: 1, of which 0 were waited for; matrix products, arithmetic and copies ran while one was open for 0% of the time, Pallas kernels for 0%

profile of v1, /device:TPU:0, one launch (start us, length us, event | category | flops | bytes accessed | tf_op | source)
XLA Modules:
  0.0 455.1 jit_solution(15594944297269287481)
XLA Ops:
  7.2 1.1 sine_multiply_fusion
  8.3 1.0 fusion.41
  9.3 0.9 reshape.35
  10.2 0.8 fusion.56
  11.0 6.5 %fusion.1 = (bf16[512,64,64]{0,2,1:T(8,128)(2,1)S(1)}, bf16[512,64,64]{0,2,1:T(8,128)(2,1)}) fusion(f32[64]{0:T(128)} %param.11, bf16[64,64,512]{2,1,0:T(8,128)(2,1)} %param.9, f32[256,256]{0,1:T(8,128)S(1)} %get-tuple-element.23, f32[256,256]{0,1:T(8,128)S(1)} %get-tuple-element.22, f32[256,256]{0,1:T(8,128)S(1)} %fusion.41), kind=kOutput, calls=%fused_computation.9 | convolution fusion | flops 2157969408 | bytes 13369600 | tf_op jit(solution)/shard_map/kjn,nm->mkj/dot_general | solution.py:56
  17.5 0.4 fusion.55
  17.9 3.9 pad_maximum_fusion.3
  21.9 7.3 %copy.81 = bf16[256,128,64]{1,2,0:T(8,128)(2,1)} copy(bf16[256,128,64]{0,2,1:T(8,128)(2,1)} %get-tuple-element.14) | data formatting | bytes 8388608 | tf_op jit(solution)/shard_map/concatenate | solution.py:62
  29.2 16.6 %convert_bitcast_fusion.1 = bf16[512,64,128]{2,0,1:T(8,128)(2,1)S(1)} fusion(bf16[128,64,512]{2,1,0:T(8,128)(2,1)} %param.7, f32[256,256]{0,1:T(8,128)S(1)} %get-tuple-element.23, f32[256,256]{0,1:T(8,128)S(1)} %get-tuple-element.22, f32[256,256]{0,1:T(8,128)S(1)} %fusion.41), kind=kOutput, calls=%fused_computation.15 | convolution fusion | flops 4301258752 | bytes 17563648 | tf_op jit(solution)/shard_map/pjn,nm->mjp/dot_general | solution.py:51
  45.8 3.6 fusion.54
  49.4 7.4 %copy.83 = bf16[256,128,64]{1,2,0:T(8,128)(2,1)} copy(bf16[256,128,64]{0,2,1:T(8,128)(2,1)} %get-tuple-element.13) | data formatting | bytes 8388608 | tf_op jit(solution)/shard_map/concatenate | solution.py:63
  56.9 28.0 %all_gather.21 = s32[4096,2]{1,0:T(8,128)S(1)} all-gather(s32[128,2]{1,0:T(8,128)S(1)} %copy.78), channel_id=1, replica_groups=mesh['dp'=32,'cls'=4] {'dp'}, dimensions={0}, use_global_device_ids=true | all-gather | bytes 33792 | tf_op jit(solution)/shard_map/all_gather | solution.py:43
  84.9 0.6 gather_fusion
  85.8 13.9 %fusion.10 = f32[256,128,128]{2,1,0:T(8,128)} fusion(bf16[256,128,64]{1,2,0:T(8,128)(2,1)} %copy.81, bf16[256,64,128]{2,0,1:T(8,128)(2,1)} %get-tuple-element.8), kind=kOutput, calls=%fused_computation.26 | convolution fusion | flops 536870912 | bytes 25165824 | tf_op jit(solution)/shard_map/mkj,mjp->mkp/dot_general | solution.py:64
  99.7 19.2 %convolution_add_fusion = f32[256,128,128]{2,1,0:T(8,128)} fusion(f32[256,128,128]{2,1,0:T(8,128)} %fusion.10, bf16[256,128,64]{1,2,0:T(8,128)(2,1)} %copy.83, bf16[256,64,128]{2,0,1:T(8,128)(2,1)} %get-tuple-element.9), kind=kOutput, calls=%fused_computation.8 | convolution fusion | flops 541065216 | bytes 41943040 | tf_op jit(solution)/shard_map/mkj,mjp->mkp/dot_general | solution.py:66
  118.9 13.8 %select_reduce_fusion.1 = f32[256,2,2,128]{3,2,1,0:T(2,128)S(1)} fusion(f32[256,2,64,128]{3,2,1,0:T(8,128)} %bitcast.66, pred[2,64,128]{2,1,0:T(8,128)(4,1)S(1)} %iota_compare_fusion), kind=kLoop, calls=%fused_computation.2 | loop fusion | flops 16646144 | bytes 17317888 | tf_op jit(solution)/shard_map/reduce_sum | solution.py:68
  132.7 0.4 fusion.57
  133.1 9.9 %all-gather.3 = f32[4,1,128]{2,1,0:T(1,128)S(1)} all-gather(f32[1,1,128]{2,1,0:T(1,128)S(1)} %bitcast.79), channel_id=3, replica_groups=mesh['dp'=32,'cls'=4] {'cls'}, dimensions={0}, use_global_device_ids=true | all-gather | bytes 2560 | tf_op jit(solution)/shard_map/all_gather | solution.py:83
  143.0 6.9 %all-gather.2 = f32[4,1,128]{2,1,0:T(1,128)S(1)} all-gather(f32[1,1,128]{2,1,0:T(1,128)S(1)} %bitcast.78), channel_id=2, replica_groups=mesh['dp'=32,'cls'=4] {'cls'}, dimensions={0}, use_global_device_ids=true | all-gather | bytes 2560 | tf_op jit(solution)/shard_map/all_gather | solution.py:82
  150.0 0.8 fusion.36
  150.9 0.4 copy.87
  151.3 10.0 %select_reduce_fusion = f32[2,256,64,128]{3,2,1,0:T(8,128)} fusion(f32[2,256,2,128]{3,2,1,0:T(2,128)S(1)} %copy.87, pred[2,64,128]{2,1,0:T(8,128)(4,1)S(1)} %iota_compare_fusion), kind=kLoop, calls=%fused_computation.1 | loop fusion | flops 12582912 | bytes 17317888 | tf_op jit(solution)/shard_map/reduce_sum | solution.py:99
  161.3 10.9 %slice_bitcast_fusion.1 = (f32[256,64,128]{2,1,0:T(8,128)}, f32[256,64,128]{2,1,0:T(8,128)}) fusion(f32[2,256,64,128]{3,2,1,0:T(8,128)} %select_reduce_fusion), kind=kLoop, calls=%fused_computation.11 | loop fusion | bytes 33554432 | tf_op jit(solution)/shard_map/squeeze | solution.py:102
  172.2 16.2 %fusion.8 = f32[256,64,128]{2,1,0:T(8,128)} fusion(bf16[256,64,128]{2,0,1:T(8,128)(2,1)} %get-tuple-element.8, f32[256,64,128]{2,1,0:T(8,128)} %get-tuple-element.7, f32[256,64,128]{2,1,0:T(8,128)} %get-tuple-element.6), kind=kOutput, calls=%fused_computation.24 | convolution fusion | flops 557842432 | bytes 29360128 | tf_op jit(solution)/shard_map/mjp,mqp->mjq/dot_general | solution.py:110
  188.4 16.2 %fusion.12 = f32[256,64,128]{2,1,0:T(8,128)} fusion(bf16[256,64,128]{2,0,1:T(8,128)(2,1)} %get-tuple-element.8, f32[256,64,128]{2,1,0:T(8,128)} %get-tuple-element.7, f32[256,64,128]{2,1,0:T(8,128)} %get-tuple-element.6), kind=kOutput, calls=%fused_computation.28 | convolution fusion | flops 553648128 | bytes 29360128 | tf_op jit(solution)/shard_map/mjp,mqp->mjq/dot_general | solution.py:108
  204.6 16.5 %fusion.14 = f32[256,64,128]{2,1,0:T(8,128)} fusion(bf16[256,64,128]{2,0,1:T(8,128)(2,1)} %get-tuple-element.9, f32[256,64,128]{2,1,0:T(8,128)} %get-tuple-element.7, f32[256,64,128]{2,1,0:T(8,128)} %get-tuple-element.6), kind=kOutput, calls=%fused_computation.30 | convolution fusion | flops 557842432 | bytes 29360128 | tf_op jit(solution)/shard_map/mjp,mqp->mjq/dot_general | solution.py:110
  221.1 16.3 %fusion.16 = f32[256,64,128]{2,1,0:T(8,128)} fusion(bf16[256,64,128]{2,0,1:T(8,128)(2,1)} %get-tuple-element.9, f32[256,64,128]{2,1,0:T(8,128)} %get-tuple-element.7, f32[256,64,128]{2,1,0:T(8,128)} %get-tuple-element.6), kind=kOutput, calls=%fused_computation.32 | convolution fusion | flops 553648128 | bytes 29360128 | tf_op jit(solution)/shard_map/mjp,mqp->mjq/dot_general | solution.py:108
  237.4 0.3 convolution_bitcast_fusion
  237.7 9.2 %copy.91 = f32[256,64,128]{0,1,2:T(8,128)} copy(f32[256,64,128]{2,1,0:T(8,128)} %fusion.8) | data formatting | bytes 16777216 | tf_op jit(solution)/shard_map/mjp,mqp->mjq/dot_general | solution.py:110
  246.9 9.2 %copy.90 = f32[256,64,128]{0,1,2:T(8,128)} copy(f32[256,64,128]{2,1,0:T(8,128)} %fusion.12) | data formatting | bytes 16777216 | tf_op jit(solution)/shard_map/mjp,mqp->mjq/dot_general | solution.py:108
  256.2 9.2 %copy.95 = f32[256,64,128]{0,1,2:T(8,128)} copy(f32[256,64,128]{2,1,0:T(8,128)} %fusion.14) | data formatting | bytes 16777216 | tf_op jit(solution)/shard_map/mjp,mqp->mjq/dot_general | solution.py:110
  265.4 9.2 %copy.94 = f32[256,64,128]{0,1,2:T(8,128)} copy(f32[256,64,128]{2,1,0:T(8,128)} %fusion.16) | data formatting | bytes 16777216 | tf_op jit(solution)/shard_map/mjp,mqp->mjq/dot_general | solution.py:108
  274.6 6.7 %convert_bitcast_fusion = f32[512,64,64]{0,1,2:T(8,128)} fusion(bf16[512,64,64]{0,2,1:T(8,128)(2,1)} %get-tuple-element.19), kind=kLoop, calls=%fused_computation.6 | loop fusion | flops 2097152 | bytes 12582912 | tf_op jit(solution)/shard_map/convert_element_type | solution.py:114
  281.3 11.9 %add.69 = f32[256,64,128]{0,1,2:T(8,128)} add(f32[256,64,128]{0,1,2:T(8,128)} %copy.90, f32[256,64,128]{0,1,2:T(8,128)} %copy.91) | non-fusion elementwise | flops 2097152 | bytes 25165824 | tf_op jit(solution)/shard_map/add | solution.py:108
  293.3 11.8 %add.70 = f32[256,64,128]{0,1,2:T(8,128)} add(f32[256,64,128]{0,1,2:T(8,128)} %copy.94, f32[256,64,128]{0,1,2:T(8,128)} %copy.95) | non-fusion elementwise | flops 2097152 | bytes 25165824 | tf_op jit(solution)/shard_map/add | solution.py:108
  305.1 12.1 %fusion.7 = (f32[256,64,64]{0,1,2:T(8,128)S(1)}, f32[256,64,64]{0,1,2:T(8,128)}) fusion(f32[512,64,64]{0,1,2:T(8,128)} %convert_bitcast_fusion, f32[256,64,128]{0,1,2:T(8,128)} %add.70, f32[256,64,128]{0,1,2:T(8,128)} %add.69, f32[256,64]{0,1:T(8,128)S(1)} %convolution_bitcast_fusion), kind=kLoop, calls=%fused_computation.20 | loop fusion | flops 6291456 | bytes 33619968 | tf_op jit(solution)/shard_map/sub | solution.py:115
  317.2 3.3 pad_maximum_fusion.1
  320.4 4.9 %copy.97 = f32[512,64,64]{0,2,1:T(8,128)S(1)} copy(f32[512,64,64]{0,1,2:T(8,128)S(1)} %pad_maximum_fusion.1) | data formatting | bytes 16777216 | tf_op jit(solution)/shard_map/concatenate | solution.py:117
  325.3 7.5 %fusion.23 = f32[512,4096]{0,1:S(1)} fusion(f32[512,4096]{0,1:T(8,128)S(1)} %bitcast.67, f32[256,256]{0,1:T(8,128)S(1)} %get-tuple-element.23, f32[256,256]{0,1:T(8,128)S(1)} %get-tuple-element.22, f32[256,256]{0,1:T(8,128)S(1)} %fusion.41), kind=kOutput, calls=%fused_computation.43 | convolution fusion | flops 6443237376 | bytes 17563648
  332.8 8.1 %copy.98 = f32[64,64,512]{2,1,0:T(8,128)} copy(f32[64,64,512]{2,0,1:T(8,128)S(1)} %bitcast.68) | data formatting | bytes 16777216 | tf_op jit(solution)/shard_map/mjk,mn->kjn/transpose | solution.py:118
  340.9 0.6 copy-done.3
  341.5 0.6 dynamic-slice
  342.8 0.1 convolution_bitcast_fusion.2
  342.9 63.3 %all-reduce = f32[64]{0:T(128)S(1)} all-reduce(f32[64]{0:T(128)S(1)} %convolution_bitcast_fusion.2), channel_id=5, replica_groups=mesh['dp'=32,'cls'=4] {'dp'}, use_global_device_ids=true, to_apply=%region_9.10.clone | all-reduce | flops 64 | bytes 512
  406.2 17.5 %all-gather.5 = f32[32,1,128]{2,1,0:T(1,128)S(1)} all-gather(f32[1,1,128]{2,1,0:T(1,128)S(1)} %add_bitcast_fusion), channel_id=1, replica_groups=mesh['dp'=32,'cls'=4] {'dp'}, dimensions={0}, use_global_device_ids=true | all-gather | bytes 16896 | tf_op jit(solution)/shard_map/all_gather | solution.py:123
  423.7 21.6 %all-gather.4 = s32[32,1,128]{2,1,0:T(1,128)S(1)} all-gather(s32[1,1,128]{2,1,0:T(1,128)S(1)} %bitcast.81), channel_id=1, replica_groups=mesh['dp'=32,'cls'=4] {'dp'}, dimensions={0}, use_global_device_ids=true | all-gather | bytes 16896 | tf_op jit(solution)/shard_map/all_gather | solution.py:44
  445.4 0.9 select_reduce_fusion.2
  446.3 1.7 divide_bitcast_fusion
  (27 shorter events, 0.6 us)
Async XLA Ops:
  7.2 439.1 %reduce-scatter.2.cloned.1.call-start = ((), (), s32[]{:S(2)}) async-start(), calls=%async_computation.1 | async-start | bytes 8650752 | tf_op jit(solution)/shard_map/reduce_scatter | solution.py:119
  49.4 7.4 %copy-start = (s32[128,2]{0,1:T(2,128)S(1)}, s32[128,2]{0,1:T(2,128)}, u32[]{:S(2)}) copy-start(s32[128,2]{0,1:T(2,128)} %param.12) | copy-start | bytes 3076
  49.4 35.5 %copy-start.1 = (s32[128]{0:T(128)S(1)}, s32[128]{0:T(128)}, u32[]{:S(2)}) copy-start(s32[128]{0:T(128)} %param.8) | copy-start | bytes 1540
  49.4 36.3 %copy-start.2 = (s32[64]{0:T(128)S(1)}, s32[64]{0:T(128)}, u32[]{:S(2)}) copy-start(s32[64]{0:T(128)} %param.13) | copy-start | bytes 772
  340.9 0.7 copy-start.3
Sparse Core Ops, SparseCore 0:
  341.0 91.0 reduce-scatter.1

commit v2 on v1

v2 whole, which is shorter than its diff:
```python
import math

import jax
import jax.numpy as jnp
from jax import lax
from jax.sharding import PartitionSpec as P

NSHELL = 64
NANG = 256
LIST = 2

HIGHEST = lax.Precision.HIGHEST


def angular_tables(points):
    positions = jnp.arange(points, dtype=jnp.int32)
    product = positions[:, None] * positions[None, :] % points
    angles = product.astype(jnp.float32) * (2.0 * math.pi / points)
    cosine = jnp.cos(angles) / math.sqrt(points)
    sine_part = jnp.sin(angles) / math.sqrt(points)
    upper_half = jnp.concatenate([cosine, -sine_part], axis=1)
    lower_half = jnp.concatenate([sine_part, cosine], axis=1)
    return jnp.concatenate([upper_half, lower_half], axis=0)


def split_bf16(x):
    high = x.astype(jnp.bfloat16)
    low = (x - high.astype(jnp.float32)).astype(jnp.bfloat16)
    return high, low


def local(
    images, pose_slot, references, rotation_response, shell_weight, class_lists, class_counts
):
    dp_index = lax.axis_index("dp")
    column = lax.axis_index("cls")
    dp_count = lax.axis_size("dp")
    blocksize = images.shape[0]
    col_classes = references.shape[0]
    row_width = 2 * NANG
    full_table = angular_tables(NANG)
    forward_ms = full_table.astype(jnp.bfloat16).reshape(row_width, 2, NANG).transpose(0, 2, 1)
    inverse_ms = full_table.T.reshape(2, NANG, row_width).transpose(1, 0, 2)

    packed = jnp.concatenate([class_lists, pose_slot[:, None]], axis=1)
    all_packed = lax.all_gather(packed, "dp", tiled=True)
    all_lists = all_packed[:, :LIST]
    all_slots = all_packed[:, LIST]
    slot_hit = jnp.arange(all_slots.shape[0], dtype=jnp.int32)[None, :] == pose_slot[:, None]
    my_lists = jnp.stack(
        [jnp.sum(jnp.where(slot_hit, all_lists[None, :, a], 0), axis=1) for a in range(LIST)]
    )
    local_class = my_lists - column * col_classes
    inside = (local_class >= 0) & (local_class < col_classes)
    class_ids = jnp.arange(col_classes, dtype=jnp.int32)
    pick = local_class[:, None, :] == class_ids[None, :, None]

    image_x = jnp.einsum(
        "pjn,nms->msjp", images, forward_ms, preferred_element_type=jnp.float32
    ).astype(jnp.bfloat16)
    image_c = image_x.reshape(NANG, 2 * NSHELL, blocksize)
    ref_x = jnp.einsum(
        "kjn,nms->mskj", references, forward_ms, preferred_element_type=jnp.float32
    ).astype(jnp.bfloat16)
    weighted = (ref_x.astype(jnp.float32) * shell_weight[None, None, None, :]).astype(jnp.bfloat16)
    w_re = weighted[:, 0]
    w_im = weighted[:, 1]
    row_re = jnp.concatenate([w_re, w_im], axis=-1)
    row_im = jnp.concatenate([-w_im, w_re], axis=-1)
    stacked = jnp.concatenate([row_re, row_im], axis=1)
    cross = jnp.einsum("mqc,mcp->mqp", stacked, image_c, preferred_element_type=jnp.float32)
    cross = cross.reshape(NANG, 2, col_classes, blocksize)
    cross_sel = jnp.sum(jnp.where(pick[None, None], cross[:, :, None], 0.0), axis=3)
    rot = rotation_response.reshape(-1, 2, NANG)
    log_prior = jnp.log1p(class_counts.astype(jnp.float32))
    prior_sel = jnp.sum(jnp.where(pick, log_prior[None, :, None], 0.0), axis=1)
    scores = jnp.einsum("rtm,mtap->rap", rot, cross_sel, precision=HIGHEST) + prior_sel[None]
    scores = jnp.where(inside[None], scores, -1e30)
    top_local = jnp.max(scores, axis=(0, 1))
    total_local = jnp.sum(
        jnp.where(inside[None], jnp.exp(scores - top_local[None, None]), 0.0), axis=(0, 1)
    )
    gathered = lax.all_gather(jnp.stack([top_local, total_local]), "cls")
    tops = gathered[:, 0]
    totals = gathered[:, 1]
    top_score = jnp.max(tops, axis=0)
    total_sum = jnp.sum(totals * jnp.exp(tops - top_score[None]), axis=0)
    posterior = (
        jnp.where(inside[None], jnp.exp(scores - top_score[None, None]), 0.0)
        / total_sum[None, None]
    )
    evidence = top_score + jnp.log(total_sum)
    post_sum = jnp.sum(posterior, axis=0)

    rot_re = rotation_response[:, :NANG]
    rot_im = rotation_response[:, NANG:]
    coef_table = jnp.concatenate([rot_re, -rot_im, rot_re * rot_re + rot_im * rot_im], axis=1)
    coef = jnp.einsum("rn,rap->nap", coef_table, posterior, precision=HIGHEST)
    coef = coef.reshape(3, NANG, LIST, blocksize)
    coef_mu = jnp.transpose(coef[:2], (1, 0, 2, 3))
    spread = jnp.sum(jnp.where(pick[None, None], coef_mu[:, :, :, None], 0.0), axis=2)
    spread = spread.reshape(NANG, 2 * col_classes, blocksize)
    volume = jnp.einsum("map,akp->mk", coef[2], pick.astype(jnp.float32), precision=HIGHEST)
    spread_hi, spread_lo = split_bf16(spread)
    grad_q = jnp.einsum(
        "mqp,mcp->mqc", spread_hi, image_c, preferred_element_type=jnp.float32
    ) + jnp.einsum("mqp,mcp->mqc", spread_lo, image_c, preferred_element_type=jnp.float32)
    grad_q = grad_q.reshape(NANG, 2, col_classes, 2, NSHELL)
    ref_f = ref_x.astype(jnp.float32)
    vol = volume[:, :, None]
    numer_re = grad_q[:, 0, :, 0] - grad_q[:, 1, :, 1] - vol * ref_f[:, 0]
    numer_im = grad_q[:, 1, :, 0] + grad_q[:, 0, :, 1] - vol * ref_f[:, 1]
    numer = jnp.stack([numer_re, numer_im], axis=1)
    partial = jnp.einsum("mskj,msn->kjn", numer, inverse_ms, precision=lax.Precision.HIGH)

    outgoing = partial.reshape(dp_count, col_classes // dp_count, NSHELL, row_width)
    arrived = lax.all_to_all(
        outgoing.astype(jnp.bfloat16), "dp", split_axis=0, concat_axis=0, tiled=True
    )
    summed = jnp.sum(arrived.astype(jnp.float32), axis=0)

    denom_part = jnp.einsum("ap,akp->k", post_sum, pick.astype(jnp.float32), precision=HIGHEST)
    tail = jnp.concatenate([evidence, denom_part])
    all_tail = lax.all_gather(tail, "dp")
    all_evidence = all_tail[:, :blocksize].reshape(-1)
    per_owner = col_classes // dp_count
    denom_all = jnp.sum(all_tail[:, blocksize:], axis=0)
    own_denom = lax.dynamic_slice_in_dim(denom_all, dp_index * per_owner, per_owner)
    gradient = summed / (1.0 + own_denom)[:, None, None]
    wanted = dp_index * blocksize + jnp.arange(blocksize, dtype=jnp.int32)
    placed = jnp.sum(
        jnp.where(all_slots[None, :] == wanted[:, None], all_evidence[None, :], 0.0), axis=1
    )
    return (gradient[None], placed)


def solution(mesh):
    return jax.shard_map(
        local,
        mesh=mesh,
        in_specs=(
            P("dp", None, None),
            P("dp"),
            P("cls", None, None),
            P(),
            P(),
            P("dp", None),
            P("cls"),
        ),
        out_specs=(P("cls", "dp", None, None), P("dp")),
        check_vma=False,
    )
```

time: 462 us -> 421 us (0.911)
  blocking collectives: 147 us -> 199 us
  local copies, waits for them, and re-layouts: 82.5 us -> 33.8 us
  matrix products: 131 us -> 105 us
  between operations: 15.1 us -> 1.66 us
  other arithmetic: 79.7 us -> 68.6 us
  starting transfers between devices: 0.04 us -> 5.49 us
    unnamed x1, blocking collectives: 63.3 us -> 163 us
    all_gather x5 -> x2, blocking collectives: 83.9 us -> 36.1 us  [the longest x1 25.7 us: local(): all_packed = lax.all_gather(packed, 'dp', tiled=True)]
    dot_general x4 -> x0, local copies, waits for them, and re-layouts: 36.9 us -> none  [the longest x2 18.5 us: against(): jnp.einsum('mjp,mqp->mjq', image_part, spread_lo, preferred_element_type=...]
    add x3 -> x2, other arithmetic: 23.8 us -> 0.08 us  [the longest x1 0.08 us: local(): gradient = summed / (1.0 + own_denom)[:, None, None]]
    dot_general x10 -> x8, matrix products: 122 us -> 104 us  [the longest x1 26.6 us: local(): jnp.einsum('pjn,nms->msjp', images, forward_ms, preferred_element_type=jn...]
    add x0 -> x1, local copies, waits for them, and re-layouts: none -> 17.8 us  [local(): jnp.einsum('mqp,mcp->mqc', spread_hi, image_c, preferred_element_type=jnp...]
    squeeze x1, local copies, waits for them, and re-layouts: 10.9 us -> 2.43 us  [local(): w_im = weighted[:, 1]]
    transpose x1, local copies, waits for them, and re-layouts: 8.08 us -> 0.41 us  [local(): coef_mu = jnp.transpose(coef[:2], (1, 0, 2, 3))]
where the time goes in v2:
time: 421 us; the launch traced here: 414 us
  blocking collectives  199 us (47%)
  matrix products  105 us (25%)
  other arithmetic  68.6 us (16%)
  local copies, waits for them, and re-layouts  33.8 us (8%)
  starting transfers between devices  5.49 us (1%)
    unnamed x1, blocking collectives  163 us
    dot_general x1, matrix products, local(): jnp.einsum('pjn,nms->msjp', images, forward_ms, preferred_element_type=jn...  26.6 us
    all_gather x1, blocking collectives, local(): all_packed = lax.all_gather(packed, 'dp', tiled=True)  25.7 us
    dot_general x1, matrix products, local(): jnp.einsum('mqc,mcp->mqp', stacked, image_c, preferred_element_type=jnp.f...  20.5 us
    dot_general x1, matrix products, local(): jnp.einsum('mqp,mcp->mqc', spread_lo, image_c, preferred_element_type=jnp...  20.2 us
    dot_general x1, matrix products, local(): jnp.einsum('mqp,mcp->mqc', spread_hi, image_c, preferred_element_type=jnp...  20.2 us
    add x1, local copies, waits for them, and re-layouts, local(): jnp.einsum('mqp,mcp->mqc', spread_hi, image_c, preferred_element_type=jnp...  17.8 us
    reduce_sum x1, other arithmetic, local(): jnp.sum(jnp.where(pick[None, None], cross[:, :, None], 0.0), axis=3)  13.6 us
  transfers between devices with their start and end apart: 1, of which 0 were waited for; matrix products, arithmetic and copies ran while one was open for 0% of the time, Pallas kernels for 0%

profile of v2, /device:TPU:0, one launch (start us, length us, event | category | flops | bytes accessed | tf_op | source)
XLA Modules:
  0.0 414.2 jit_solution(2532017786800065937)
XLA Ops:
  0.6 1.1 negate_convert_fusion
  1.7 1.0 fusion.44
  2.7 7.7 %multiply_convert_fusion = (bf16[256,2,64,64]{0,3,2,1:T(8,128)(2,1)S(1)}, f32[256,2,64,64]{0,3,2,1:T(8,128)}) fusion(f32[64]{0:T(128)} %param.11, bf16[64,64,512]{2,1,0:T(8,128)(2,1)} %param.9, bf16[256,1,256]{2,0,1:T(8,128)(2,1)S(1)} %get-tuple-element.28, bf16[256,1,256]{2,0,1:T(8,128)(2,1)S(1)} %fusion.44, bf16[256,1,256]{2,0,1:T(8,128)(2,1)S(1)} %get-tuple-element.27), kind=kOutput, calls=%fused_computation.16 | convolution fusion | flops 2157969408 | bytes 17170688 | tf_op jit(solution)/shard_map/kjn,nms->mskj/dot_general | solution.py:62
  10.5 0.0 copy-start
  10.5 2.4 slice_bitcast_fusion.4
  12.9 0.1 fusion.61
  13.1 0.0 copy-done
  13.1 0.1 reshape.184
  13.1 12.4 %maximum_maximum_fusion = bf16[256,128,128]{0,2,1:T(8,128)(2,1)} fusion(bf16[256,64,64]{0,2,1:T(8,128)(2,1)} %get-tuple-element.11, bf16[256,64,64]{0,2,1:T(8,128)(2,1)S(1)} %fusion.61, bf16[256,64,64]{0,2,1:T(8,128)(2,1)} %get-tuple-element.10), kind=kLoop, calls=%fused_computation.6 | loop fusion | flops 33554432 | bytes 14680064 | tf_op jit(solution)/shard_map/concatenate | solution.py:70
  25.6 12.4 %copy.50 = bf16[256,128,128]{2,1,0:T(8,128)(2,1)} copy(bf16[256,128,128]{0,2,1:T(8,128)(2,1)} %maximum_maximum_fusion) | data formatting | bytes 16777216 | tf_op jit(solution)/shard_map/concatenate | solution.py:70
  37.9 0.0 copy-start.1
  37.9 0.0 copy-start.2
  38.0 26.6 %fusion.13 = bf16[256,2,128,64]{2,0,3,1:T(8,128)(2,1)} fusion(bf16[128,64,512]{2,1,0:T(8,128)(2,1)} %param.7, bf16[256,1,256]{2,0,1:T(8,128)(2,1)S(1)} %get-tuple-element.28, bf16[256,1,256]{2,0,1:T(8,128)(2,1)S(1)} %fusion.44, bf16[256,1,256]{2,0,1:T(8,128)(2,1)S(1)} %get-tuple-element.27), kind=kOutput, calls=%fused_computation.22 | convolution fusion | flops 4301258752 | bytes 17170432 | tf_op jit(solution)/shard_map/pjn,nms->msjp/dot_general | solution.py:58
  64.5 0.0 copy-done.1
  64.5 0.0 copy-done.2
  64.5 25.7 %all_gather.15 = s32[4096,3]{0,1:T(4,128)S(1)} all-gather(s32[128,3]{0,1:T(4,128)S(1)} %pad_add_fusion), channel_id=1, replica_groups=mesh['dp'=32,'cls'=4] {'dp'}, dimensions={0}, use_global_device_ids=true | all-gather | bytes 50688 | tf_op jit(solution)/shard_map/all_gather | solution.py:46
  90.3 0.7 select_reduce_fusion.4
  91.0 0.0 copy-done.3
  91.0 0.1 select_reduce_fusion.5
  91.1 20.5 %fusion.11 = f32[256,128,128]{2,1,0:T(8,128)} fusion(bf16[256,128,128]{2,1,0:T(8,128)(2,1)} %copy.50, bf16[256,128,128]{2,0,1:T(8,128)(2,1)} %bitcast.139), kind=kOutput, calls=%fused_computation.20 | convolution fusion | flops 1073741824 | bytes 33554432 | tf_op jit(solution)/shard_map/mqc,mcp->mqp/dot_general | solution.py:71
  111.6 13.6 %select_reduce_fusion.1 = f32[256,2,2,128]{3,2,1,0:T(2,128)S(1)} fusion(f32[256,2,64,128]{3,2,1,0:T(8,128)} %bitcast.142, pred[2,64,128]{2,1,0:T(8,128)(4,1)S(1)} %iota_compare_fusion.1), kind=kLoop, calls=%fused_computation.1 | loop fusion | flops 16646144 | bytes 17317888 | tf_op jit(solution)/shard_map/reduce_sum | solution.py:73
  125.2 0.4 fusion.64
  125.7 10.4 %all-gather.2 = f32[4,2,128]{2,1,0:T(2,128)S(1)} all-gather(f32[1,2,128]{2,1,0:T(2,128)S(1)} %maximum_bitcast_fusion.5), channel_id=2, replica_groups=mesh['dp'=32,'cls'=4] {'cls'}, dimensions={0}, use_global_device_ids=true | all-gather | bytes 5120 | tf_op jit(solution)/shard_map/all_gather | solution.py:83
  136.2 0.8 fusion.45
  137.0 0.3 convolution_bitcast_fusion
  137.3 1.1 sine_multiply_fusion
  138.4 1.0 fusion.50
  139.4 0.4 copy.55
  139.8 9.9 %select_reduce_fusion = f32[256,2,64,128]{3,2,1,0:T(8,128)} fusion(f32[256,2,2,128]{3,2,1,0:T(2,128)S(1)} %copy.55, pred[2,64,128]{2,1,0:T(8,128)(4,1)S(1)} %iota_compare_fusion.1), kind=kLoop, calls=%fused_computation | loop fusion | flops 12582912 | bytes 17317888 | tf_op jit(solution)/shard_map/reduce_sum | solution.py:101
  149.7 12.7 %fusion = (bf16[256,128,128]{2,1,0:T(8,128)(2,1)}, bf16[256,128,128]{2,1,0:T(8,128)(2,1)}) fusion(f32[256,2,64,128]{3,2,1,0:T(8,128)} %select_reduce_fusion), kind=kLoop, calls=%fused_computation.4 | loop fusion | flops 16777216 | bytes 33554432 | tf_op jit(solution)/shard_map/convert_element_type | solution.py:28
  162.4 20.2 %fusion.9 = f32[256,128,128]{2,1,0:T(8,128)} fusion(bf16[256,128,128]{2,1,0:T(8,128)(2,1)} %get-tuple-element.5, bf16[256,128,128]{2,0,1:T(8,128)(2,1)} %bitcast.140), kind=kOutput, calls=%fused_computation.18 | convolution fusion | flops 1073741824 | bytes 33554432 | tf_op jit(solution)/shard_map/mqp,mcp->mqc/dot_general | solution.py:105
  182.6 20.2 %convolution_add_fusion = f32[256,128,128]{2,1,0:T(8,128)} fusion(f32[256,128,128]{2,1,0:T(8,128)} %fusion.9, bf16[256,128,128]{2,1,0:T(8,128)(2,1)} %get-tuple-element.4, bf16[256,128,128]{2,0,1:T(8,128)(2,1)} %bitcast.141), kind=kOutput, calls=%fused_computation.5 | convolution fusion | flops 1077936128 | bytes 50331648 | tf_op jit(solution)/shard_map/mqp,mcp->mqc/dot_general | solution.py:107
  202.9 17.8 %copy.58 = f32[256,128,128]{0,2,1:T(8,128)} copy(f32[256,128,128]{2,1,0:T(8,128)} %convolution_add_fusion) | data formatting | bytes 33554432 | tf_op jit(solution)/shard_map/add | solution.py:105
  220.6 9.9 %fusion.19 = (f32[256,1,64,64]{0,3,2,1:T(8,128)S(1)}, f32[256,1,64,64]{0,3,2,1:T(8,128)S(1)}) fusion(f32[256,2,64,64]{0,3,2,1:T(8,128)} %get-tuple-element.22, f32[256,2,64,2,64]{0,4,3,2,1:T(8,128)} %bitcast.143, f32[256,64]{0,1:T(8,128)S(1)} %convolution_bitcast_fusion), kind=kLoop, calls=%fused_computation.30 | loop fusion | flops 6291456 | bytes 33619968 | tf_op jit(solution)/shard_map/sub | solution.py:111
  230.5 0.1 maximum_maximum_fusion.1
  230.6 8.3 %bitcast_convert_fusion.1 = bf16[64,64,512]{2,1,0:T(8,128)(2,1)} fusion(f32[256,2,512,1]{2,0,3,1:T(8,128)S(1)} %bitcast.146, f32[256,1,64,64]{0,3,2,1:T(8,128)S(1)} %get-tuple-element.9, f32[256,1,64,64]{0,3,2,1:T(8,128)S(1)} %get-tuple-element.8), kind=kOutput, calls=%fused_computation.11 | convolution fusion | flops 6446645248 | bytes 13631488 | tf_op jit(solution)/shard_map/mskj,msn->kjn/dot_general | solution.py:114
  238.9 5.5 %all-to-all-start = ((bf16[32,2,64,512]{3,2,1,0:T(8,128)(2,1)}), bf16[32,2,64,512]{3,2,1,0:T(8,128)(2,1)}, u32[]{:S(2)}, u32[]{:S(2)}) async-start(bf16[32,2,64,512]{3,2,1,0:T(8,128)(2,1)} %bitcast.144), calls=%async_computation | async-start | bytes 8388608 | tf_op jit(solution)/shard_map/all_to_all | solution.py:117
  244.5 0.0 copy-done.4
  244.5 0.6 dynamic-slice
  245.7 0.1 convolution_bitcast_fusion.2
  245.9 0.1 maximum_dynamic-update-slice_fusion
  246.0 163.2 %all-reduce = f32[6144]{0:T(1024)S(1)} all-reduce(f32[6144]{0:T(1024)S(1)} %maximum_dynamic-update-slice_fusion), channel_id=3, replica_groups=mesh['dp'=32,'cls'=4] {'dp'}, use_global_device_ids=true, to_apply=%add | all-reduce | flops 6144 | bytes 49152
  409.2 0.1 reshape.189
  409.3 0.1 dynamic-slice_add_fusion
  409.4 0.9 select_reduce_fusion.2
  410.3 0.0 all-to-all-done
  410.3 2.9 convert_reduce_fusion
  413.2 0.8 bitcast_divide_fusion
  (19 shorter events, 0.3 us)
Async XLA Ops:
  10.5 2.6 copy-start
  37.9 26.6 %copy-start.1 = (s32[128]{0:T(128)S(1)}, s32[128]{0:T(128)}, u32[]{:S(2)}) copy-start(s32[128]{0:T(128)} %param.8) | copy-start | bytes 1540
  37.9 26.6 %copy-start.2 = (s32[128,2]{0,1:T(2,128)S(1)}, s32[128,2]{0,1:T(2,128)}, u32[]{:S(2)}) copy-start(s32[128,2]{0,1:T(2,128)} %param.12) | copy-start | bytes 3076
  38.0 53.1 %copy-start.3 = (s32[64]{0:T(128)S(1)}, s32[64]{0:T(128)}, u32[]{:S(2)}) copy-start(s32[64]{0:T(128)} %param.13) | copy-start | bytes 772
  238.9 5.5 %copy-start.4 = (u32[128]{0:T(128)S(1)}, u32[128]{0:T(128)}, u32[]{:S(2)}) copy-start(u32[128]{0:T(128)} %constant.49) | copy-start | bytes 1540
  238.9 171.3 %all-to-all-start = ((bf16[32,2,64,512]{3,2,1,0:T(8,128)(2,1)}), bf16[32,2,64,512]{3,2,1,0:T(8,128)(2,1)}, u32[]{:S(2)}, u32[]{:S(2)}) async-start(bf16[32,2,64,512]{3,2,1,0:T(8,128)(2,1)} %bitcast.144), calls=%async_computation | async-start | bytes 8388608 | tf_op jit(solution)/shard_map/all_to_all | solution.py:117

commit v3 on v2

v3 whole, which is shorter than its diff:
```python
import math

import jax
import jax.numpy as jnp
from jax import lax
from jax.experimental import pallas as pl
from jax.experimental.pallas import tpu as pltpu
from jax.sharding import PartitionSpec as P

NSHELL = 64
NANG = 256
LIST = 2

HIGHEST = lax.Precision.HIGHEST
F32 = jnp.float32


def angular_tables(points):
    positions = jnp.arange(points, dtype=jnp.int32)
    product = positions[:, None] * positions[None, :] % points
    angles = product.astype(jnp.float32) * (2.0 * math.pi / points)
    cosine = jnp.cos(angles) / math.sqrt(points)
    sine_part = jnp.sin(angles) / math.sqrt(points)
    upper_half = jnp.concatenate([cosine, -sine_part], axis=1)
    lower_half = jnp.concatenate([sine_part, cosine], axis=1)
    return jnp.concatenate([upper_half, lower_half], axis=0)


def cross_kernel(count_ref, ent_p_ref, ent_k_ref, image_ref, weight_ref, out_ref):
    out_ref[...] = jnp.zeros_like(out_ref)

    def body(e, carry):
        x = image_ref[ent_p_ref[e]].astype(F32)
        w = weight_ref[ent_k_ref[e]].astype(F32)
        x_re = x[:, :NANG]
        x_im = x[:, NANG:]
        w_re = w[:, :NANG]
        w_im = w[:, NANG:]
        c_re = jnp.sum(x_re * w_re + x_im * w_im, axis=0, keepdims=True)
        c_im = jnp.sum(x_im * w_re - x_re * w_im, axis=0, keepdims=True)
        out_ref[pl.ds(e, 1), :] = jnp.concatenate([c_re, c_im], axis=1)
        return carry

    lax.fori_loop(0, count_ref[0], body, 0)


def grad_kernel(count_ref, ent_p_ref, ent_k_ref, image_ref, coef_ref, acc_ref):
    acc_ref[...] = jnp.zeros_like(acc_ref)

    def body(e, carry):
        x = image_ref[ent_p_ref[e]].astype(F32)
        c = coef_ref[pl.ds(e, 1), :]
        c_re = c[:, :NANG]
        c_im = c[:, NANG:]
        x_re = x[:, :NANG]
        x_im = x[:, NANG:]
        g_re = x_re * c_re - x_im * c_im
        g_im = x_re * c_im + x_im * c_re
        k = ent_k_ref[e]
        acc_ref[k] = acc_ref[k] + jnp.concatenate([g_re, g_im], axis=1)
        return carry

    lax.fori_loop(0, count_ref[0], body, 0)


def smem():
    return pl.BlockSpec(memory_space=pltpu.SMEM)


def vmem():
    return pl.BlockSpec(memory_space=pltpu.VMEM)


def local(
    images, pose_slot, references, rotation_response, shell_weight, class_lists, class_counts
):
    dp_index = lax.axis_index("dp")
    column = lax.axis_index("cls")
    dp_count = lax.axis_size("dp")
    blocksize = images.shape[0]
    col_classes = references.shape[0]
    per_owner = col_classes // dp_count
    per_pair = blocksize // dp_count
    row_width = 2 * NANG
    entries = blocksize * LIST
    full_table = angular_tables(NANG)
    forward = full_table.astype(jnp.bfloat16)
    inverse = full_table.T

    packed = jnp.concatenate([class_lists, pose_slot[:, None]], axis=1)
    all_packed = lax.all_to_all(
        jnp.broadcast_to(packed[None], (dp_count,) + packed.shape), "dp", 0, 0, tiled=True
    ).reshape(dp_count * blocksize, LIST + 1)
    all_lists = all_packed[:, :LIST]
    slot_hit = jnp.arange(all_lists.shape[0], dtype=jnp.int32)[None, :] == pose_slot[:, None]
    my_lists = jnp.stack(
        [jnp.sum(jnp.where(slot_hit, all_lists[None, :, a], 0), axis=1) for a in range(LIST)],
        axis=1,
    )
    local_class = (my_lists - column * col_classes).reshape(entries)
    inside = (local_class >= 0) & (local_class < col_classes)
    inside_i = inside.astype(jnp.int32)
    count = jnp.sum(inside_i)
    before_in = jnp.cumsum(inside_i) - inside_i
    before_out = jnp.cumsum(1 - inside_i) - (1 - inside_i)
    rank = jnp.where(inside, before_in, count + before_out)
    slots = jnp.arange(entries, dtype=jnp.int32)
    at_rank = rank[None, :] == slots[:, None]
    order = jnp.sum(jnp.where(at_rank, slots[None, :], 0), axis=1)
    safe_class = jnp.clip(local_class, 0, col_classes - 1)
    ent_p = order // LIST
    ent_k = jnp.sum(jnp.where(at_rank, safe_class[None, :], 0), axis=1)
    count_arr = count.reshape(1)

    image_hat = jnp.dot(
        images.reshape(-1, row_width), forward, preferred_element_type=F32
    ).astype(jnp.bfloat16).reshape(images.shape)
    ref_hat = jnp.dot(
        references.reshape(-1, row_width), forward, preferred_element_type=F32
    ).astype(jnp.bfloat16).reshape(references.shape)
    weighted = (ref_hat.astype(F32) * shell_weight[None, :, None]).astype(jnp.bfloat16)

    cross_c = pl.pallas_call(
        cross_kernel,
        out_shape=jax.ShapeDtypeStruct((entries, row_width), F32),
        in_specs=[smem(), smem(), smem(), vmem(), vmem()],
        out_specs=vmem(),
    )(count_arr, ent_p, ent_k, image_hat, weighted)

    log_prior = jnp.log1p(class_counts.astype(F32))
    prior = jnp.sum(
        jnp.where(safe_class[:, None] == jnp.arange(col_classes)[None, :], log_prior[None, :], 0.0),
        axis=1,
    )
    scores_c = jnp.dot(cross_c, rotation_response.T, precision=HIGHEST)
    scores = jnp.take(scores_c, rank, axis=0) + prior[:, None]
    scores = jnp.where(inside[:, None], scores, -1e30).reshape(blocksize, LIST, -1)
    inside_pa = inside.reshape(blocksize, LIST)
    top_local = jnp.max(scores, axis=(1, 2))
    total_local = jnp.sum(
        jnp.where(inside_pa[..., None], jnp.exp(scores - top_local[:, None, None]), 0.0), axis=(1, 2)
    )
    gathered = lax.all_gather(jnp.stack([top_local, total_local]), "cls")
    tops = gathered[:, 0]
    totals = gathered[:, 1]
    top_score = jnp.max(tops, axis=0)
    total_sum = jnp.sum(totals * jnp.exp(tops - top_score[None]), axis=0)
    posterior = (
        jnp.where(inside_pa[..., None], jnp.exp(scores - top_score[:, None, None]), 0.0)
        / total_sum[:, None, None]
    )
    evidence = top_score + jnp.log(total_sum)
    post_sum = jnp.sum(posterior, axis=2).reshape(entries)

    rot_re = rotation_response[:, :NANG]
    rot_im = rotation_response[:, NANG:]
    coef_table = jnp.concatenate([rot_re, -rot_im, rot_re * rot_re + rot_im * rot_im], axis=1)
    coef = jnp.dot(posterior.reshape(entries, -1), coef_table, precision=HIGHEST)
    coef_c = jnp.take(coef, order, axis=0)

    numer_acc = pl.pallas_call(
        grad_kernel,
        out_shape=jax.ShapeDtypeStruct(references.shape, F32),
        in_specs=[smem(), smem(), smem(), vmem(), vmem()],
        out_specs=vmem(),
    )(count_arr, ent_p, ent_k, image_hat, coef_c[:, :row_width])

    class_pick = (
        (local_class[None, :] == jnp.arange(col_classes, dtype=jnp.int32)[:, None]) & inside[None, :]
    ).astype(F32)
    volume = jnp.dot(class_pick, coef[:, row_width:], precision=HIGHEST)
    denom_part = jnp.dot(class_pick, post_sum, precision=HIGHEST)
    volume_full = jnp.concatenate([volume, volume], axis=1)
    numer = numer_acc - volume_full[:, None, :] * ref_hat.astype(F32)
    partial = jnp.dot(
        numer.reshape(-1, row_width), inverse, precision=lax.Precision.HIGH
    ).reshape(references.shape)

    outgoing = partial.reshape(dp_count, per_owner, NSHELL, row_width)
    arrived = lax.all_to_all(
        outgoing.astype(jnp.bfloat16), "dp", split_axis=0, concat_axis=0, tiled=True
    )
    summed = jnp.sum(arrived.astype(F32), axis=0)

    dest = pose_slot // blocksize
    dest_hit = dest[None, :] == jnp.arange(dp_count, dtype=jnp.int32)[:, None]
    dest_i = dest_hit.astype(jnp.int32)
    within = jnp.sum((jnp.cumsum(dest_i, axis=1) - dest_i) * dest_i, axis=0)
    sel = dest_hit[:, None, :] & (
        within[None, None, :] == jnp.arange(per_pair, dtype=jnp.int32)[None, :, None]
    )
    send_ev = jnp.sum(jnp.where(sel, evidence[None, None, :], 0.0), axis=2)
    send_pos = jnp.sum(jnp.where(sel, (pose_slot % blocksize).astype(F32)[None, None, :], 0.0), axis=2)
    send_den = denom_part.reshape(dp_count, per_owner)
    small = jnp.concatenate([send_ev, send_pos, send_den], axis=1)
    got = lax.all_to_all(small, "dp", 0, 0, tiled=True)
    got_ev = got[:, :per_pair].reshape(-1)
    got_pos = got[:, per_pair : 2 * per_pair].reshape(-1)
    own_denom = jnp.sum(got[:, 2 * per_pair :], axis=0)
    gradient = summed / (1.0 + own_denom)[:, None, None]
    rows = jnp.arange(blocksize, dtype=F32)
    placed = jnp.sum(jnp.where(got_pos[None, :] == rows[:, None], got_ev[None, :], 0.0), axis=1)
    return (gradient[None], placed)


def solution(mesh):
    return jax.shard_map(
        local,
        mesh=mesh,
        in_specs=(
            P("dp", None, None),
            P("dp"),
            P("cls", None, None),
            P(),
            P(),
            P("dp", None),
            P("cls"),
        ),
        out_specs=(P("cls", "dp", None, None), P("dp")),
        check_vma=False,
    )
```

time: 421 us -> 204 us (0.48); the launches traced: 414 us -> 201 us
  blocking collectives: 199 us -> 9.88 us
  matrix products: 105 us -> 33.4 us
  waiting for transfers between devices: 0.01 us -> 51.8 us
  other arithmetic: 68.6 us -> 35 us
  Pallas kernels: 0 us -> 19.5 us
  starting transfers between devices: 5.49 us -> 23.5 us
  local copies, waits for them, and re-layouts: 33.8 us -> 27.5 us
    unnamed x1 -> x0, blocking collectives: 163 us -> none
    dot_general x10 -> x7, matrix products: 105 us -> 33.4 us  [the longest x1 12 us: local(): jnp.dot(numer.reshape(-1, row_width), inverse, precision=lax.Precision.HIGH)]
    all_to_all x1, waiting for transfers between devices: 0.01 us -> 51.8 us  [local(): lax.all_to_all(outgoing.astype(jnp.bfloat16), 'dp', split_axis=0, concat_...]
    all_gather x1 -> x0, blocking collectives: 25.7 us -> none  [local(): all_packed = lax.all_gather(packed, 'dp', tiled=True)]
    reduce_sum x8 -> x11, other arithmetic: 27.5 us -> 5.95 us  [the longest x1 2.87 us: local(): summed = jnp.sum(arrived.astype(F32), axis=0)]
    convert_element_type x0 -> x4, local copies, waits for them, and re-layouts: none -> 21.2 us  [the longest x1 11.9 us: local(): image_hat = jnp.dot(images.reshape(-1, row_width), forward, preferred_ele...]
    pallas_call x0 -> x2, Pallas kernels: none -> 19.5 us  [the longest x1 9.75 us: local(): pl.pallas_call(cross_kernel, out_shape=jax.ShapeDtypeStruct((entries, row...]
    add x1 -> x0, local copies, waits for them, and re-layouts: 17.8 us -> none  [local(): jnp.einsum('mqp,mcp->mqc', spread_hi, image_c, preferred_element_type=jnp...]
  transfers between devices with their start and end apart: 1 -> 3, of which waited for: 0 -> 1; matrix products, arithmetic and copies ran while one was open for 0% -> 37% of each run, Pallas kernels for 0% -> 0%
where the time goes in v3:
time: 204 us; the launch traced here: 201 us
  waiting for transfers between devices  51.8 us (25%)
  other arithmetic  35 us (17%)
  matrix products  33.4 us (16%)
  local copies, waits for them, and re-layouts  27.5 us (13%)
  starting transfers between devices  23.5 us (12%)
  Pallas kernels  19.5 us (10%)
  blocking collectives  9.88 us (5%)
    all_to_all x1, waiting for transfers between devices, local(): lax.all_to_all(outgoing.astype(jnp.bfloat16), 'dp', split_axis=0, concat_...  51.8 us
    sub x1, other arithmetic, local(): numer = numer_acc - volume_full[:, None, :] * ref_hat.astype(F32)  12.1 us
    dot_general x1, matrix products, local(): jnp.dot(numer.reshape(-1, row_width), inverse, precision=lax.Precision.HIGH)  12 us
    convert_element_type x1, local copies, waits for them, and re-layouts, local(): image_hat = jnp.dot(images.reshape(-1, row_width), forward, preferred_ele...  11.9 us
    dot_general x1, matrix products, local(): jnp.dot(images.reshape(-1, row_width), forward, preferred_element_type=F32)  10.7 us
    all_gather x1, blocking collectives, local(): gathered = lax.all_gather(jnp.stack([top_local, total_local]), 'cls')  9.88 us
    pallas_call x1, Pallas kernels, local(): pl.pallas_call(cross_kernel, out_shape=jax.ShapeDtypeStruct((entries, row...  9.75 us
    pallas_call x1, Pallas kernels, local(): pl.pallas_call(grad_kernel, out_shape=jax.ShapeDtypeStruct(references.sha...  9.72 us
  transfers between devices with their start and end apart: 3, of which 1 were waited for; matrix products, arithmetic and copies ran while one was open for 37% of the time, Pallas kernels for 0%

profile of v3, /device:TPU:0, one launch (start us, length us, event | category | flops | bytes accessed | tf_op | source)
XLA Modules:
  0.0 201.5 jit_solution(13489012592976495403)
XLA Ops:
  0.6 0.7 pad_add_fusion
  1.3 0.6 broadcast_in_dim.183
  2.0 8.2 %all-to-all-start = ((s32[32,128,3]{1,2,0:T(4,128)}), s32[32,128,3]{1,2,0:T(4,128)S(1)}, u32[]{:S(2)}, u32[]{:S(2)}) async-start(s32[32,128,3]{1,2,0:T(4,128)} %broadcast_in_dim.183), calls=%async_computation | async-start | bytes 131072 | tf_op jit(solution)/shard_map/all_to_all | solution.py:91
  10.2 1.1 sine_multiply_fusion
  11.3 1.0 fusion.25
  12.3 0.7 fusion.51
  12.9 10.7 %fusion = bf16[8192,512]{0,1:T(8,128)(2,1)} fusion(bf16[8192,512]{1,0:T(8,128)(2,1)} %bitcast.110, f32[256,256]{1,0:T(8,128)S(1)} %get-tuple-element.31, f32[256,256]{1,0:T(8,128)S(1)} %get-tuple-element.30, f32[256,256]{1,0:T(8,128)S(1)} %fusion.25), kind=kOutput, calls=%fused_computation.3 | convolution fusion | flops 4301258752 | bytes 17563648 | tf_op jit(solution)/shard_map/dot_general | solution.py:115
  23.6 7.8 %convert_bitcast_fusion = f32[4096,512]{0,1:T(8,128)} fusion(bf16[4096,512]{1,0:T(8,128)(2,1)} %bitcast.88, f32[256,256]{1,0:T(8,128)S(1)} %get-tuple-element.31, f32[256,256]{1,0:T(8,128)S(1)} %get-tuple-element.30, f32[256,256]{1,0:T(8,128)S(1)} %fusion.25), kind=kOutput, calls=%fused_computation.4 | convolution fusion | flops 2153775104 | bytes 13369344 | tf_op jit(solution)/shard_map/dot_general | solution.py:118
  31.4 9.0 %copy.45 = f32[4096,512]{1,0:T(8,128)} copy(f32[4096,512]{0,1:T(8,128)} %convert_bitcast_fusion) | data formatting | bytes 16777216 | tf_op jit(solution)/shard_map/convert_element_type | solution.py:121
  40.5 0.3 reduce_window_sum.82
  40.8 6.7 %multiply_convert_fusion.weight_ref = bf16[64,64,512]{2,1,0:T(8,128)(2,1)} fusion(f32[64,64,512]{2,1,0:T(8,128)} %bitcast.83, f32[64]{0:T(128)S(1)} %copy-done.2), kind=kLoop, calls=%fused_computation.7 | loop fusion | flops 4194304 | bytes 12583168 | tf_op jit(solution)/shard_map/convert_element_type | solution.py:121
  47.6 11.9 %copy.41 = bf16[8192,512]{1,0:T(8,128)(2,1)} copy(bf16[8192,512]{0,1:T(8,128)(2,1)} %fusion) | data formatting | bytes 16777216 | tf_op jit(solution)/shard_map/convert_element_type | solution.py:117
  59.5 0.6 select_reduce_fusion.1
  60.5 0.3 reduce-window.16
  60.8 0.6 convert_reduce_fusion.1
  61.8 0.3 reduce-window.24
  62.6 0.7 compare_and_fusion.2
  63.4 0.7 select_reduce_fusion.2
  64.0 0.6 and_select_fusion.4.ent_p_ref
  64.6 9.7 %shard_map.86 = f32[256,512]{1,0:T(8,128)} custom-call(s32[1]{0:T(128)} %bitcast.6.count_ref, s32[256]{0:T(256)} %and_select_fusion.4.ent_p_ref, s32[256]{0:T(256)} %get-tuple-element.4.ent_k_ref, bf16[128,64,512]{2,1,0:T(8,128)(2,1)} %bitcast.85, bf16[64,64,512]{2,1,0:T(8,128)(2,1)} %multiply_convert_fusion.weight_ref), custom_call_target="tpu_custom_call" | custom-call | tf_op jit(solution)/shard_map/pallas_call | solution.py:123
  74.4 1.6 fusion.64
  76.1 0.7 compare_select_fusion.1
  77.1 0.2 reshape.454
  77.5 0.2 reshape.452
  77.7 0.7 gather_fusion
  78.4 0.7 compare_and_fusion.1
  79.1 0.2 fusion.26
  79.7 0.2 sub.196
  79.8 0.3 select_reduce_fusion.4
  80.4 9.9 %all-gather.1 = f32[4,2,128]{2,1,0:T(2,128)S(1)} all-gather(f32[1,2,128]{2,1,0:T(2,128)S(1)} %maximum_bitcast_fusion.1), channel_id=2, replica_groups=mesh['dp'=32,'cls'=4] {'cls'}, dimensions={0}, use_global_device_ids=true | all-gather | bytes 5120 | tf_op jit(solution)/shard_map/all_gather | solution.py:143
  90.4 0.2 div.69
  90.6 0.2 sub.200
  91.1 0.3 fusion.19
  91.4 1.0 fusion.11
  92.4 0.2 fusion.6
  92.6 1.1 gather_fusion.1
  93.7 1.0 slice_select_fusion.coef_ref
  94.7 9.7 %shard_map.87 = f32[64,64,512]{2,1,0:T(8,128)} custom-call(s32[1]{0:T(128)} %bitcast.6.count_ref, s32[256]{0:T(256)} %and_select_fusion.4.ent_p_ref, s32[256]{0:T(256)} %get-tuple-element.4.ent_k_ref, bf16[128,64,512]{2,1,0:T(8,128)(2,1)} %bitcast.86, f32[256,512]{1,0:T(8,128)} %slice_select_fusion.coef_ref), custom_call_target="tpu_custom_call" | custom-call | tf_op jit(solution)/shard_map/pallas_call | solution.py:161
  104.7 0.2 fusion.27
  104.9 0.7 copy.49
  105.6 7.8 %all-to-all-start.2 = ((f32[32,1,10]{2,1,0:T(1,128)}), f32[32,1,10]{2,1,0:T(1,128)S(1)}, u32[]{:S(2)}, u32[]{:S(2)}) async-start(f32[32,1,10]{2,1,0:T(1,128)} %copy.49), calls=%async_computation.2 | async-start | bytes 32768 | tf_op jit(solution)/shard_map/all_to_all | solution.py:196
  113.4 12.1 %multiply_subtract_fusion = f32[64,64,512]{2,1,0:T(8,128)} fusion(f32[64,64,512]{2,1,0:T(8,128)} %shard_map.87, f32[64,64,512]{2,1,0:T(8,128)} %bitcast.84, f32[64,512]{1,0:T(8,128)S(1)} %pad_maximum_fusion), kind=kLoop, calls=%fused_computation.6 | loop fusion | flops 4194304 | bytes 25296896 | tf_op jit(solution)/shard_map/sub | solution.py:174
  125.4 12.0 %convolution_convert_fusion.2 = bf16[32,2,64,512]{3,2,1,0:T(8,128)(2,1)} fusion(f32[32,2,64,512]{3,2,1,0:T(8,128)} %bitcast.87, f32[256,256]{1,0:T(8,128)S(1)} %get-tuple-element.31, f32[256,256]{1,0:T(8,128)S(1)} %get-tuple-element.30, f32[256,256]{1,0:T(8,128)S(1)} %fusion.25), kind=kOutput, calls=%fused_computation.9 | convolution fusion | flops 6445334528 | bytes 13369344 | tf_op jit(solution)/shard_map/dot_general | solution.py:175
  137.5 7.5 %all-to-all-start.1 = ((bf16[32,2,64,512]{3,2,1,0:T(8,128)(2,1)}), bf16[32,2,64,512]{3,2,1,0:T(8,128)(2,1)}, u32[]{:S(2)}, u32[]{:S(2)}) async-start(bf16[32,2,64,512]{3,2,1,0:T(8,128)(2,1)} %convolution_convert_fusion.2), calls=%async_computation.1 | async-start | bytes 8388608 | tf_op jit(solution)/shard_map/all_to_all | solution.py:180
  145.4 0.6 select_reduce_fusion.5
  146.0 51.8 %all-to-all-done.1 = bf16[32,2,64,512]{3,2,1,0:T(8,128)(2,1)} async-done(((bf16[32,2,64,512]{3,2,1,0:T(8,128)(2,1)}), bf16[32,2,64,512]{3,2,1,0:T(8,128)(2,1)}, u32[]{:S(2)}, u32[]{:S(2)}) %all-to-all-start.1) | async-done | bytes 4194336 | tf_op jit(solution)/shard_map/all_to_all | solution.py:180
  197.8 2.9 %convert_reduce_fusion = f32[2,64,512]{2,1,0:T(8,128)S(1)} fusion(bf16[32,2,64,512]{3,2,1,0:T(8,128)(2,1)} %all-to-all-done.1), kind=kLoop, calls=%fused_computation.5 | loop fusion | flops 4128768 | bytes 4456448 | tf_op jit(solution)/shard_map/reduce_sum | solution.py:183
  200.7 0.8 bitcast_divide_fusion
  (67 shorter events, 3.7 us)
Async XLA Ops:
  2.0 57.5 %all-to-all-start = ((s32[32,128,3]{1,2,0:T(4,128)}), s32[32,128,3]{1,2,0:T(4,128)S(1)}, u32[]{:S(2)}, u32[]{:S(2)}) async-start(s32[32,128,3]{1,2,0:T(4,128)} %broadcast_in_dim.183), calls=%async_computation | async-start | bytes 131072 | tf_op jit(solution)/shard_map/all_to_all | solution.py:91
  31.4 9.1 %copy-start = (f32[36,512]{1,0:T(8,128)S(1)}, f32[36,512]{1,0:T(8,128)}, u32[]{:S(2)}) copy-start(f32[36,512]{1,0:T(8,128)} %param.10) | copy-start | bytes 221188
  31.4 9.1 %copy-start.3 = (s32[64]{0:T(128)S(1)}, s32[64]{0:T(128)}, u32[]{:S(2)}) copy-start(s32[64]{0:T(128)} %param.13) | copy-start | bytes 772
  31.4 9.4 %copy-start.2 = (f32[64]{0:T(128)S(1)}, f32[64]{0:T(128)}, u32[]{:S(2)}) copy-start(f32[64]{0:T(128)} %param.11) | copy-start | bytes 772
  47.6 12.0 %copy-start.1 = (s32[128]{0:T(128)S(1)}, s32[128]{0:T(128)}, u32[]{:S(2)}) copy-start(s32[128]{0:T(128)} %param.8) | copy-start | bytes 1540
  105.6 31.9 %all-to-all-start.2 = ((f32[32,1,10]{2,1,0:T(1,128)}), f32[32,1,10]{2,1,0:T(1,128)S(1)}, u32[]{:S(2)}, u32[]{:S(2)}) async-start(f32[32,1,10]{2,1,0:T(1,128)} %copy.49), calls=%async_computation.2 | async-start | bytes 32768 | tf_op jit(solution)/shard_map/all_to_all | solution.py:196
  137.5 60.3 %all-to-all-start.1 = ((bf16[32,2,64,512]{3,2,1,0:T(8,128)(2,1)}), bf16[32,2,64,512]{3,2,1,0:T(8,128)(2,1)}, u32[]{:S(2)}, u32[]{:S(2)}) async-start(bf16[32,2,64,512]{3,2,1,0:T(8,128)(2,1)} %convolution_convert_fusion.2), calls=%async_computation.1 | async-start | bytes 8388608 | tf_op jit(solution)/shard_map/all_to_all | solution.py:180

commit v4 on v3

--- a/solution.py
+++ b/solution.py
@@ -26,29 +26,70 @@
     return jnp.concatenate([upper_half, lower_half], axis=0)
 
 
-def cross_kernel(count_ref, ent_p_ref, ent_k_ref, image_ref, weight_ref, out_ref):
-    out_ref[...] = jnp.zeros_like(out_ref)
+CHUNK = 512
+
+
+def cross_kernel(
+    count_ref, ent_p_ref, ent_k_ref, image_ref, refs_ref, forward_ref, wrow_ref,
+    cross_ref, image_hat_ref, ref_hat_ref, weighted_ref,
+):
+    forward = forward_ref[...]
+    wrow = wrow_ref[...]
+
+    def image_dft(c, carry):
+        r = pl.multiple_of(c * CHUNK, CHUNK)
+        image_hat_ref[pl.ds(r, CHUNK), :] = jnp.dot(
+            image_ref[pl.ds(r, CHUNK), :], forward, preferred_element_type=F32
+        ).astype(jnp.bfloat16)
+        return carry
+
+    def ref_dft(c, carry):
+        r = pl.multiple_of(c * CHUNK, CHUNK)
+        hat = jnp.dot(
+            refs_ref[pl.ds(r, CHUNK), :], forward, preferred_element_type=F32
+        ).astype(jnp.bfloat16)
+        ref_hat_ref[pl.ds(r, CHUNK), :] = hat
+        weighted_ref[pl.ds(r, CHUNK), :] = (hat.astype(F32) * wrow).astype(jnp.bfloat16)
+        return carry
+
+    lax.fori_loop(0, image_ref.shape[0] // CHUNK, image_dft, 0)
+    lax.fori_loop(0, refs_ref.shape[0] // CHUNK, ref_dft, 0)
+    cross_ref[...] = jnp.zeros_like(cross_ref)
 
     def body(e, carry):
-        x = image_ref[ent_p_ref[e]].astype(F32)
-        w = weight_ref[ent_k_ref[e]].astype(F32)
+        rp = pl.multiple_of(ent_p_ref[e] * NSHELL, NSHELL)
+        rk = pl.multiple_of(ent_k_ref[e] * NSHELL, NSHELL)
+        x = image_hat_ref[pl.ds(rp, NSHELL), :].astype(F32)
+        w = weighted_ref[pl.ds(rk, NSHELL), :].astype(F32)
         x_re = x[:, :NANG]
         x_im = x[:, NANG:]
         w_re = w[:, :NANG]
         w_im = w[:, NANG:]
         c_re = jnp.sum(x_re * w_re + x_im * w_im, axis=0, keepdims=True)
         c_im = jnp.sum(x_im * w_re - x_re * w_im, axis=0, keepdims=True)
-        out_ref[pl.ds(e, 1), :] = jnp.concatenate([c_re, c_im], axis=1)
+        cross_ref[pl.ds(e, 1), :] = jnp.concatenate([c_re, c_im], axis=1)
         return carry
 
     lax.fori_loop(0, count_ref[0], body, 0)
 
 
-def grad_kernel(count_ref, ent_p_ref, ent_k_ref, image_ref, coef_ref, acc_ref):
-    acc_ref[...] = jnp.zeros_like(acc_ref)
+def grad_kernel(
+    count_ref, ent_p_ref, ent_k_ref, image_hat_ref, coef_ref, ref_hat_ref, volume_ref,
+    out_ref, acc_ref,
+):
+    def init(k, carry):
+        r = pl.multiple_of(k * NSHELL, NSHELL)
+        acc_ref[pl.ds(r, NSHELL), :] = -volume_ref[pl.ds(k, 1), :] * ref_hat_ref[
+            pl.ds(r, NSHELL), :
+        ].astype(F32)
+        return carry
+
+    lax.fori_loop(0, volume_ref.shape[0], init, 0)
 
     def body(e, carry):
-        x = image_ref[ent_p_ref[e]].astype(F32)
+        rp = pl.multiple_of(ent_p_ref[e] * NSHELL, NSHELL)
+        rk = pl.multiple_of(ent_k_ref[e] * NSHELL, NSHELL)
+        x = image_hat_ref[pl.ds(rp, NSHELL), :].astype(F32)
         c = coef_ref[pl.ds(e, 1), :]
         c_re = c[:, :NANG]
         c_im = c[:, NANG:]
@@ -56,11 +97,19 @@
         x_im = x[:, NANG:]
         g_re = x_re * c_re - x_im * c_im
         g_im = x_re * c_im + x_im * c_re
-        k = ent_k_ref[e]
-        acc_ref[k] = acc_ref[k] + jnp.concatenate([g_re, g_im], axis=1)
+        acc_ref[pl.ds(rk, NSHELL), :] = acc_ref[pl.ds(rk, NSHELL), :] + jnp.concatenate(
+            [g_re, g_im], axis=1
+        )
         return carry
 
     lax.fori_loop(0, count_ref[0], body, 0)
+
+    def finish(c, carry):
+        r = pl.multiple_of(c * CHUNK, CHUNK)
+        out_ref[pl.ds(r, CHUNK), :] = acc_ref[pl.ds(r, CHUNK), :].astype(jnp.bfloat16)
+        return carry
+
+    lax.fori_loop(0, acc_ref.shape[0] // CHUNK, finish, 0)
 
 
 def smem():
@@ -112,20 +161,25 @@
     ent_k = jnp.sum(jnp.where(at_rank, safe_class[None, :], 0), axis=1)
     count_arr = count.reshape(1)
 
-    image_hat = jnp.dot(
-        images.reshape(-1, row_width), forward, preferred_element_type=F32
-    ).astype(jnp.bfloat16).reshape(images.shape)
-    ref_hat = jnp.dot(
-        references.reshape(-1, row_width), forward, preferred_element_type=F32
-    ).astype(jnp.bfloat16).reshape(references.shape)
-    weighted = (ref_hat.astype(F32) * shell_weight[None, :, None]).astype(jnp.bfloat16)
-
-    cross_c = pl.pallas_call(
+    image_rows = images.shape[0] * NSHELL
+    ref_rows = col_classes * NSHELL
+    wrow = jnp.tile(shell_weight, CHUNK // NSHELL)[:, None]
+    params = pltpu.CompilerParams(vmem_limit_bytes=60 * 1024 * 1024)
+    cross_c, image_hat, ref_hat = pl.pallas_call(
         cross_kernel,
-        out_shape=jax.ShapeDtypeStruct((entries, row_width), F32),
-        in_specs=[smem(), smem(), smem(), vmem(), vmem()],
-        out_specs=vmem(),
-    )(count_arr, ent_p, ent_k, image_hat, weighted)
+        out_shape=(
+            jax.ShapeDtypeStruct((entries, row_width), F32),
+            jax.ShapeDtypeStruct((image_rows, row_width), jnp.bfloat16),
+            jax.ShapeDtypeStruct((ref_rows, row_width), jnp.bfloat16),
+        ),
+        in_specs=[smem(), smem(), smem(), vmem(), vmem(), vmem(), vmem()],
+        out_specs=(vmem(), vmem(), vmem()),
+        scratch_shapes=[pltpu.VMEM((ref_rows, row_width), jnp.bfloat16)],
+        compiler_params=params,
+    )(
+        count_arr, ent_p, ent_k, images.reshape(image_rows, row_width),
+        references.reshape(ref_rows, row_width), forward, wrow,
+    )
 
     log_prior = jnp.log1p(class_counts.astype(F32))
     prior = jnp.sum(
@@ -158,29 +212,27 @@
     coef = jnp.dot(posterior.reshape(entries, -1), coef_table, precision=HIGHEST)
     coef_c = jnp.take(coef, order, axis=0)
 
-    numer_acc = pl.pallas_call(
-        grad_kernel,
-        out_shape=jax.ShapeDtypeStruct(references.shape, F32),
-        in_specs=[smem(), smem(), smem(), vmem(), vmem()],
-        out_specs=vmem(),
-    )(count_arr, ent_p, ent_k, image_hat, coef_c[:, :row_width])
-
     class_pick = (
         (local_class[None, :] == jnp.arange(col_classes, dtype=jnp.int32)[:, None]) & inside[None, :]
     ).astype(F32)
     volume = jnp.dot(class_pick, coef[:, row_width:], precision=HIGHEST)
     denom_part = jnp.dot(class_pick, post_sum, precision=HIGHEST)
     volume_full = jnp.concatenate([volume, volume], axis=1)
-    numer = numer_acc - volume_full[:, None, :] * ref_hat.astype(F32)
-    partial = jnp.dot(
-        numer.reshape(-1, row_width), inverse, precision=lax.Precision.HIGH
-    ).reshape(references.shape)
-
-    outgoing = partial.reshape(dp_count, per_owner, NSHELL, row_width)
-    arrived = lax.all_to_all(
-        outgoing.astype(jnp.bfloat16), "dp", split_axis=0, concat_axis=0, tiled=True
-    )
+    numer = pl.pallas_call(
+        grad_kernel,
+        out_shape=jax.ShapeDtypeStruct((ref_rows, row_width), jnp.bfloat16),
+        in_specs=[smem(), smem(), smem(), vmem(), vmem(), vmem(), vmem()],
+        out_specs=vmem(),
+        scratch_shapes=[pltpu.VMEM((ref_rows, row_width), F32)],
+        compiler_params=params,
+    )(count_arr, ent_p, ent_k, image_hat, coef_c[:, :row_width], ref_hat, volume_full)
+
+    outgoing = numer.reshape(dp_count, per_owner, NSHELL, row_width)
+    arrived = lax.all_to_all(outgoing, "dp", split_axis=0, concat_axis=0, tiled=True)
     summed = jnp.sum(arrived.astype(F32), axis=0)
+    summed = jnp.dot(
+        summed.reshape(-1, row_width), inverse, precision=HIGHEST
+    ).reshape(summed.shape)
 
     dest = pose_slot // blocksize
     dest_hit = dest[None, :] == jnp.arange(dp_count, dtype=jnp.int32)[:, None]

time: 204 us -> 154 us (0.75)
  matrix products: 33.4 us -> 4.78 us
  local copies, waits for them, and re-layouts: 27.5 us -> 8.13 us
  other arithmetic: 35 us -> 19 us
  Pallas kernels: 19.5 us -> 34.3 us
    dot_general x3 -> x1, matrix products: 30.5 us -> 1.88 us  [local(): jnp.dot(summed.reshape(-1, row_width), inverse, precision=HIGHEST)]
    convert_element_type x2 -> x0, local copies, waits for them, and re-layouts: 21 us -> none  [the longest x1 11.9 us: local(): image_hat = jnp.dot(images.reshape(-1, row_width), forward, preferred_ele...]
    pallas_call x2, Pallas kernels: 19.5 us -> 34.3 us  [the longest x1 23.8 us: local(): pl.pallas_call(cross_kernel, out_shape=(jax.ShapeDtypeStruct((entries, ro...]
    sub x1 -> x0, other arithmetic: 12.1 us -> none  [local(): numer = numer_acc - volume_full[:, None, :] * ref_hat.astype(F32)]
    convert_element_type x1, other arithmetic: 6.72 us -> 0.87 us  [local(): forward = full_table.astype(jnp.bfloat16)]
  transfers between devices with their start and end apart: 3 -> 3, of which waited for: 1 -> 2; matrix products, arithmetic and copies ran while one was open for 37% -> 8% of each run, Pallas kernels for 0% -> 7%
where the time goes in v4:
time: 154 us; the launch traced here: 152 us
  waiting for transfers between devices  52.3 us (34%)
  Pallas kernels  34.3 us (22%)
  starting transfers between devices  22.6 us (15%)
  other arithmetic  19 us (12%)
  blocking collectives  10.2 us (7%)
  local copies, waits for them, and re-layouts  8.13 us (5%)
  matrix products  4.78 us (3%)
    all_to_all x1, waiting for transfers between devices, local(): lax.all_to_all(outgoing, 'dp', split_axis=0, concat_axis=0, tiled=True)  51.8 us
    pallas_call x1, Pallas kernels, local(): pl.pallas_call(cross_kernel, out_shape=(jax.ShapeDtypeStruct((entries, ro...  23.8 us
    pallas_call x1, Pallas kernels, local(): pl.pallas_call(grad_kernel, out_shape=jax.ShapeDtypeStruct((ref_rows, row...  10.5 us
    all_gather x1, blocking collectives, local(): gathered = lax.all_gather(jnp.stack([top_local, total_local]), 'cls')  10.2 us
    all_to_all x1, starting transfers between devices, local(): lax.all_to_all(jnp.broadcast_to(packed[None], (dp_count,) + packed.shape)...  8.25 us
    all_to_all x1, starting transfers between devices, local(): lax.all_to_all(outgoing, 'dp', split_axis=0, concat_axis=0, tiled=True)  7.62 us
    all_to_all x1, starting transfers between devices, local(): got = lax.all_to_all(small, 'dp', 0, 0, tiled=True)  6.73 us
  transfers between devices with their start and end apart: 3, of which 2 were waited for; matrix products, arithmetic and copies ran while one was open for 8% of the time, Pallas kernels for 7%

profile of v4, /device:TPU:0, one launch (start us, length us, event | category | flops | bytes accessed | tf_op | source)
XLA Modules:
  0.0 152.2 jit_solution(17393606119407677802)
XLA Ops:
  0.6 0.7 pad_add_fusion
  1.3 0.6 broadcast_in_dim.183
  2.0 8.2 %all-to-all-start = ((s32[32,128,3]{1,2,0:T(4,128)}), s32[32,128,3]{1,2,0:T(4,128)S(1)}, u32[]{:S(2)}, u32[]{:S(2)}) async-start(s32[32,128,3]{1,2,0:T(4,128)} %broadcast_in_dim.183), calls=%async_computation | async-start | bytes 131072 | tf_op jit(solution)/shard_map/all_to_all | solution.py:140
  10.2 0.7 fusion.51
  10.9 1.0 fusion.25
  11.9 1.1 sine_multiply_fusion
  12.9 0.7 convert_log-plus-one_fusion
  13.6 0.3 reduce_window_sum.82
  13.9 0.8 fusion.59
  14.7 0.9 fusion.2.forward_ref
  15.6 0.7 tile.2
  16.3 0.9 broadcast_in_dim_tile.4.wrow_ref
  17.2 0.6 all-to-all-done
  17.8 1.3 select_reduce_fusion.1
  19.1 0.6 convert_reduce_fusion.1
  20.1 0.3 reduce-window.16
  20.4 0.3 reduce-window.24
  21.0 0.2 slice_reduce_fusion.1
  21.5 0.7 compare_and_fusion.2
  22.3 0.7 select_reduce_fusion.2
  23.0 0.6 and_select_fusion.4.ent_p_ref
  24.4 0.7 compare_select_fusion.1
  25.3 0.2 reshape.443
  25.6 23.8 %shard_map.86 = (f32[256,512]{1,0:T(8,128)}, bf16[8192,512]{1,0:T(8,128)(2,1)}, bf16[4096,512]{1,0:T(8,128)(2,1)}) custom-call(s32[1]{0:T(128)} %bitcast.6.count_ref, s32[256]{0:T(256)} %and_select_fusion.4.ent_p_ref, s32[256]{0:T(256)} %get-tuple-element.10.ent_k_ref, bf16[8192,512]{1,0:T(8,128)(2,1)} %bitcast.74, bf16[4096,512]{1,0:T(8,128)(2,1)} %bitcast.75, ...), custom_call_target="tpu_custom_call" | custom-call | tf_op jit(solution)/shard_map/pallas_call | solution.py:168
  49.4 1.6 %fusion.62 = f32[256,36]{1,0:T(8,128)S(1)} fusion(f32[256,512]{1,0:T(8,128)} %get-tuple-element.6, f32[36,512]{1,0:T(8,128)S(1)} %copy-done), kind=kOutput, calls=%fused_computation.142 | convolution fusion | flops 56623104 | bytes 634880 | tf_op jit(solution)/shard_map/dot_general | solution.py:189
  51.1 0.7 compare_and_fusion.1
  51.8 0.7 gather_fusion
  52.5 0.2 fusion.26
  53.1 0.2 sub.193
  53.2 0.3 select_reduce_fusion.4
  53.8 10.2 %all-gather.1 = f32[4,2,128]{2,1,0:T(2,128)S(1)} all-gather(f32[1,2,128]{2,1,0:T(2,128)S(1)} %maximum_bitcast_fusion.1), channel_id=2, replica_groups=mesh['dp'=32,'cls'=4] {'cls'}, dimensions={0}, use_global_device_ids=true | all-gather | bytes 5120 | tf_op jit(solution)/shard_map/all_gather | solution.py:197
  64.2 0.2 div.62
  64.4 0.2 sub.197
  64.6 0.3 fusion.19
  65.0 0.2 fusion.27
  65.2 0.7 copy.43
  65.9 6.7 %all-to-all-start.2 = ((f32[32,1,10]{2,1,0:T(1,128)}), f32[32,1,10]{2,1,0:T(1,128)S(1)}, u32[]{:S(2)}, u32[]{:S(2)}) async-start(f32[32,1,10]{2,1,0:T(1,128)} %copy.43), calls=%async_computation.2 | async-start | bytes 32768 | tf_op jit(solution)/shard_map/all_to_all | solution.py:248
  72.6 0.9 fusion.11
  73.6 0.2 fusion.6
  73.8 1.1 gather_fusion.1
  74.9 0.9 slice_select_fusion.coef_ref
  75.8 0.7 pad_maximum_fusion.volume_ref
  76.5 10.5 %shard_map.87 = bf16[4096,512]{1,0:T(8,128)(2,1)} custom-call(s32[1]{0:T(128)} %bitcast.6.count_ref, s32[256]{0:T(256)} %and_select_fusion.4.ent_p_ref, s32[256]{0:T(256)} %get-tuple-element.10.ent_k_ref, bf16[8192,512]{1,0:T(8,128)(2,1)} %get-tuple-element.5.image_hat_ref, f32[256,512]{1,0:T(8,128)} %slice_select_fusion.coef_ref, ...), custom_call_target="tpu_custom_call" | custom-call | tf_op jit(solution)/shard_map/pallas_call | solution.py:221
  87.0 7.6 %all-to-all-start.1 = ((bf16[32,2,64,512]{3,2,1,0:T(8,128)(2,1)}), bf16[32,2,64,512]{3,2,1,0:T(8,128)(2,1)}, u32[]{:S(2)}, u32[]{:S(2)}) async-start(bf16[32,2,64,512]{3,2,1,0:T(8,128)(2,1)} %bitcast.73), calls=%async_computation.1 | async-start | bytes 8388608 | tf_op jit(solution)/shard_map/all_to_all | solution.py:231
  95.0 0.6 select_reduce_fusion.5
  95.7 51.8 %all-to-all-done.1 = bf16[32,2,64,512]{3,2,1,0:T(8,128)(2,1)} async-done(((bf16[32,2,64,512]{3,2,1,0:T(8,128)(2,1)}), bf16[32,2,64,512]{3,2,1,0:T(8,128)(2,1)}, u32[]{:S(2)}, u32[]{:S(2)}) %all-to-all-start.1) | async-done | bytes 4194336 | tf_op jit(solution)/shard_map/all_to_all | solution.py:231
  147.4 2.9 %convert_reduce_fusion = f32[2,64,512]{2,1,0:T(8,128)S(1)} fusion(bf16[32,2,64,512]{3,2,1,0:T(8,128)(2,1)} %all-to-all-done.1), kind=kLoop, calls=%fused_computation.2 | loop fusion | flops 4128768 | bytes 4456448 | tf_op jit(solution)/shard_map/reduce_sum | solution.py:232
  150.3 1.9 %fusion = f32[1,2,64,512]{3,2,1,0:T(8,128)} fusion(f32[2,64,512]{2,1,0:T(8,128)S(1)} %convert_reduce_fusion, f32[256,256]{1,0:T(8,128)S(1)} %get-tuple-element.37, f32[256,256]{1,0:T(8,128)S(1)} %get-tuple-element.36, f32[256,256]{1,0:T(8,128)S(1)} %fusion.25, f32[2]{0:T(128)S(1)} %broadcast_add_fusion.2), kind=kOutput, calls=%fused_computation.7 | convolution fusion | flops 403505152 | bytes 1310728 | tf_op jit(solution)/shard_map/dot_general | solution.py:233
  (57 shorter events, 3.7 us)
Async XLA Ops:
  2.0 15.8 %all-to-all-start = ((s32[32,128,3]{1,2,0:T(4,128)}), s32[32,128,3]{1,2,0:T(4,128)S(1)}, u32[]{:S(2)}, u32[]{:S(2)}) async-start(s32[32,128,3]{1,2,0:T(4,128)} %broadcast_in_dim.183), calls=%async_computation | async-start | bytes 131072 | tf_op jit(solution)/shard_map/all_to_all | solution.py:140
  25.6 23.8 %copy-start = (f32[36,512]{1,0:T(8,128)S(1)}, f32[36,512]{1,0:T(8,128)}, u32[]{:S(2)}) copy-start(f32[36,512]{1,0:T(8,128)} %param.10) | copy-start | bytes 221188
  65.9 21.1 %all-to-all-start.2 = ((f32[32,1,10]{2,1,0:T(1,128)}), f32[32,1,10]{2,1,0:T(1,128)S(1)}, u32[]{:S(2)}, u32[]{:S(2)}) async-start(f32[32,1,10]{2,1,0:T(1,128)} %copy.43), calls=%async_computation.2 | async-start | bytes 32768 | tf_op jit(solution)/shard_map/all_to_all | solution.py:248
  87.0 60.4 %all-to-all-start.1 = ((bf16[32,2,64,512]{3,2,1,0:T(8,128)(2,1)}), bf16[32,2,64,512]{3,2,1,0:T(8,128)(2,1)}, u32[]{:S(2)}, u32[]{:S(2)}) async-start(bf16[32,2,64,512]{3,2,1,0:T(8,128)(2,1)} %bitcast.73), calls=%async_computation.1 | async-start | bytes 8388608 | tf_op jit(solution)/shard_map/all_to_all | solution.py:231

commit v5 on v4

--- a/solution.py
+++ b/solution.py
@@ -227,8 +227,16 @@
         compiler_params=params,
     )(count_arr, ent_p, ent_k, image_hat, coef_c[:, :row_width], ref_hat, volume_full)
 
-    outgoing = numer.reshape(dp_count, per_owner, NSHELL, row_width)
-    arrived = lax.all_to_all(outgoing, "dp", split_axis=0, concat_axis=0, tiled=True)
+    core = dp_index % 2
+    by_core = numer.reshape(dp_count // 2, 2, per_owner, NSHELL, row_width)
+    keep = lax.dynamic_index_in_dim(by_core, core, axis=1, keepdims=False)
+    give = lax.dynamic_index_in_dim(by_core, 1 - core, axis=1, keepdims=False)
+    taken = lax.ppermute(give, "dp", perm=[(i, i ^ 1) for i in range(dp_count)])
+    pair_sum = (keep.astype(F32) + taken.astype(F32)).astype(jnp.bfloat16)
+    groups = [list(range(q, dp_count, 2)) for q in range(2)]
+    arrived = lax.all_to_all(
+        pair_sum, "dp", split_axis=0, concat_axis=0, tiled=True, axis_index_groups=groups
+    )
     summed = jnp.sum(arrived.astype(F32), axis=0)
     summed = jnp.dot(
         summed.reshape(-1, row_width), inverse, precision=HIGHEST

time: 154 us -> 134 us (0.87)
  waiting for transfers between devices: 52.3 us -> 35.8 us
  starting transfers between devices: 22.6 us -> 16.9 us
  local copies, waits for them, and re-layouts: 8.13 us -> 10.7 us
    all_to_all x1, waiting for transfers between devices: 51.8 us -> 30.1 us  [local(): lax.all_to_all(pair_sum, 'dp', split_axis=0, concat_axis=0, tiled=True, a...]
    all_to_all x1, starting transfers between devices: 7.62 us -> 3.72 us  [local(): lax.all_to_all(pair_sum, 'dp', split_axis=0, concat_axis=0, tiled=True, a...]
    convert_element_type x0 -> x1, other arithmetic: none -> 3.69 us  [local(): pair_sum = (keep.astype(F32) + taken.astype(F32)).astype(jnp.bfloat16)]
    all_to_all x1, waiting for transfers between devices: 0.01 us -> 3.58 us  [local(): got = lax.all_to_all(small, 'dp', 0, 0, tiled=True)]
    squeeze x0 -> x1, local copies, waits for them, and re-layouts: none -> 3.17 us  [local(): give = lax.dynamic_index_in_dim(by_core, 1 - core, axis=1, keepdims=False)]
    reduce_sum x1, other arithmetic: 2.87 us -> 0.3 us  [local(): summed = jnp.sum(arrived.astype(F32), axis=0)]
    all_to_all x1, starting transfers between devices: 6.73 us -> 4.97 us  [local(): got = lax.all_to_all(small, 'dp', 0, 0, tiled=True)]
    all_to_all x1, waiting for transfers between devices: 0.56 us -> 2.16 us  [local(): lax.all_to_all(jnp.broadcast_to(packed[None], (dp_count,) + packed.shape)...]
  transfers between devices with their start and end apart: 3 -> 4, of which waited for: 2 -> 3; matrix products, arithmetic and copies ran while one was open for 8% -> 9% of each run, Pallas kernels for 7% -> 0%
where the time goes in v5:
time: 134 us; the launch traced here: 133 us
  waiting for transfers between devices  35.8 us (27%)
  Pallas kernels  34.1 us (25%)
  other arithmetic  18.8 us (14%)
  starting transfers between devices  16.9 us (13%)
  blocking collectives  10.9 us (8%)
  local copies, waits for them, and re-layouts  10.7 us (8%)
  matrix products  4.77 us (4%)
    all_to_all x1, waiting for transfers between devices, local(): lax.all_to_all(pair_sum, 'dp', split_axis=0, concat_axis=0, tiled=True, a...  30.1 us
    pallas_call x1, Pallas kernels, local(): pl.pallas_call(cross_kernel, out_shape=(jax.ShapeDtypeStruct((entries, ro...  23.6 us
    all_gather x1, blocking collectives, local(): gathered = lax.all_gather(jnp.stack([top_local, total_local]), 'cls')  10.9 us
    pallas_call x1, Pallas kernels, local(): pl.pallas_call(grad_kernel, out_shape=jax.ShapeDtypeStruct((ref_rows, row...  10.5 us
    all_to_all x1, starting transfers between devices, local(): lax.all_to_all(jnp.broadcast_to(packed[None], (dp_count,) + packed.shape)...  8.25 us
    all_to_all x1, starting transfers between devices, local(): got = lax.all_to_all(small, 'dp', 0, 0, tiled=True)  4.97 us
    all_to_all x1, starting transfers between devices, local(): lax.all_to_all(pair_sum, 'dp', split_axis=0, concat_axis=0, tiled=True, a...  3.72 us
    convert_element_type x1, other arithmetic, local(): pair_sum = (keep.astype(F32) + taken.astype(F32)).astype(jnp.bfloat16)  3.69 us
  transfers between devices with their start and end apart: 4, of which 3 were waited for; matrix products, arithmetic and copies ran while one was open for 9% of the time, Pallas kernels for 0%

profile of v5, /device:TPU:0, one launch (start us, length us, event | category | flops | bytes accessed | tf_op | source)
XLA Modules:
  0.0 133.1 jit_solution(17087501377300255912)
XLA Ops:
  0.7 0.7 pad_add_fusion
  1.4 0.6 broadcast_in_dim.183
  2.0 8.2 %all-to-all-start = ((s32[32,128,3]{1,2,0:T(4,128)}), s32[32,128,3]{1,2,0:T(4,128)S(1)}, u32[]{:S(2)}, u32[]{:S(2)}) async-start(s32[32,128,3]{1,2,0:T(4,128)} %broadcast_in_dim.183), calls=%async_computation | async-start | bytes 131072 | tf_op jit(solution)/shard_map/all_to_all | solution.py:140
  10.3 1.1 sine_multiply_fusion
  11.3 1.0 fusion.26
  12.3 0.7 convert_log-plus-one_fusion
  13.0 0.8 fusion.60
  13.8 0.9 fusion.3.forward_ref
  14.7 0.9 broadcast_in_dim_tile.4.wrow_ref
  15.6 2.2 %all-to-all-done = s32[32,128,3]{1,2,0:T(4,128)S(1)} async-done(((s32[32,128,3]{1,2,0:T(4,128)}), s32[32,128,3]{1,2,0:T(4,128)S(1)}, u32[]{:S(2)}, u32[]{:S(2)}) %all-to-all-start) | async-done | bytes 49184 | tf_op jit(solution)/shard_map/all_to_all | solution.py:140
  17.8 0.6 select_reduce_fusion.1
  18.8 0.3 reduce-window.16
  19.1 0.6 convert_reduce_fusion.1
  19.8 0.3 reduce-window.24
  20.9 0.7 compare_and_fusion.2
  21.7 0.7 select_reduce_fusion.2
  22.3 0.6 and_select_fusion.4.ent_p_ref
  22.9 23.6 %shard_map.86 = (f32[256,512]{1,0:T(8,128)}, bf16[8192,512]{1,0:T(8,128)(2,1)}, bf16[4096,512]{1,0:T(8,128)(2,1)}) custom-call(s32[1]{0:T(128)} %bitcast.6.count_ref, s32[256]{0:T(256)} %and_select_fusion.4.ent_p_ref, s32[256]{0:T(256)} %get-tuple-element.10.ent_k_ref, bf16[8192,512]{1,0:T(8,128)(2,1)} %bitcast.80, bf16[4096,512]{1,0:T(8,128)(2,1)} %bitcast.81, ...), custom_call_target="tpu_custom_call" | custom-call | tf_op jit(solution)/shard_map/pallas_call | solution.py:168
  46.6 1.6 %fusion.63 = f32[256,36]{1,0:T(8,128)S(1)} fusion(f32[256,512]{1,0:T(8,128)} %get-tuple-element.6, f32[36,512]{1,0:T(8,128)S(1)} %copy-done.2), kind=kOutput, calls=%fused_computation.145 | convolution fusion | flops 56623104 | bytes 634880 | tf_op jit(solution)/shard_map/dot_general | solution.py:189
  48.3 0.7 compare_select_fusion.1
  49.2 0.1 reshape.443
  49.6 0.2 reshape.445
  49.9 0.7 gather_fusion
  50.6 0.7 compare_and_fusion.1
  51.3 0.2 fusion.27
  51.9 0.2 sub.196
  52.0 0.3 select_reduce_fusion.4
  52.6 10.9 %all-gather.1 = f32[4,2,128]{2,1,0:T(2,128)S(1)} all-gather(f32[1,2,128]{2,1,0:T(2,128)S(1)} %maximum_bitcast_fusion.1), channel_id=2, replica_groups=mesh['dp'=32,'cls'=4] {'cls'}, dimensions={0}, use_global_device_ids=true | all-gather | bytes 5120 | tf_op jit(solution)/shard_map/all_gather | solution.py:197
  63.6 0.1 div.62
  63.9 0.2 sub.200
  64.4 0.9 fusion.12
  65.3 0.2 fusion.7
  65.6 1.1 gather_fusion.1
  66.7 0.7 pad_maximum_fusion.volume_ref
  67.3 0.9 slice_select_fusion.coef_ref
  68.2 10.5 %shard_map.87 = bf16[4096,512]{1,0:T(8,128)(2,1)} custom-call(s32[1]{0:T(128)} %bitcast.6.count_ref, s32[256]{0:T(256)} %and_select_fusion.4.ent_p_ref, s32[256]{0:T(256)} %get-tuple-element.10.ent_k_ref, bf16[8192,512]{1,0:T(8,128)(2,1)} %get-tuple-element.5.image_hat_ref, f32[256,512]{1,0:T(8,128)} %slice_select_fusion.coef_ref, ...), custom_call_target="tpu_custom_call" | custom-call | tf_op jit(solution)/shard_map/pallas_call | solution.py:221
  78.7 3.2 %dynamic-slice_bitcast_fusion = bf16[16,2,64,512]{3,2,1,0:T(8,128)(2,1)} fusion(bf16[16,2,2,64,512]{4,3,2,1,0:T(8,128)(2,1)} %bitcast.78, s32[]{:T(128)S(6)} %select_n.189), kind=kLoop, calls=%fused_computation.5 | loop fusion | bytes 4194308 | tf_op jit(solution)/shard_map/jit(dynamic_index_in_dim)/squeeze | solution.py:233
  82.0 0.3 reduce_window_sum.82
  82.5 0.3 fusion.20
  83.1 0.7 copy.43
  83.8 5.0 %all-to-all-start.2 = ((f32[32,1,10]{2,1,0:T(1,128)}), f32[32,1,10]{2,1,0:T(1,128)S(1)}, u32[]{:S(2)}, u32[]{:S(2)}) async-start(f32[32,1,10]{2,1,0:T(1,128)} %copy.43), calls=%async_computation.2 | async-start | bytes 32768 | tf_op jit(solution)/shard_map/all_to_all | solution.py:256
  88.8 3.7 %fusion = bf16[16,2,64,512]{3,2,1,0:T(8,128)(2,1)} fusion(bf16[16,2,64,512]{3,2,1,0:T(8,128)(2,1)S(1)} %collective-permute-done, bf16[16,2,2,64,512]{4,3,2,1,0:T(8,128)(2,1)} %bitcast.79, s32[]{:T(128)S(6)} %select_n.188), kind=kLoop, calls=%fused_computation.3 | loop fusion | flops 4194304 | bytes 6291460 | tf_op jit(solution)/shard_map/convert_element_type | solution.py:235
  92.5 3.6 %all-to-all-done.2 = f32[32,1,10]{2,1,0:T(1,128)S(1)} async-done(((f32[32,1,10]{2,1,0:T(1,128)}), f32[32,1,10]{2,1,0:T(1,128)S(1)}, u32[]{:S(2)}, u32[]{:S(2)}) %all-to-all-start.2) | async-done | bytes 1312 | tf_op jit(solution)/shard_map/all_to_all | solution.py:256
  96.1 3.7 %all-to-all-start.1 = ((bf16[16,2,64,512]{3,2,1,0:T(8,128)(2,1)}), bf16[16,2,64,512]{3,2,1,0:T(8,128)(2,1)S(1)}, u32[]{:S(2)}, u32[]{:S(2)}) async-start(bf16[16,2,64,512]{3,2,1,0:T(8,128)(2,1)} %fusion), calls=%async_computation.1 | async-start | bytes 4194304 | tf_op jit(solution)/shard_map/all_to_all | solution.py:237
  100.2 0.6 select_reduce_fusion.5
  100.8 30.1 %all-to-all-done.1 = bf16[16,2,64,512]{3,2,1,0:T(8,128)(2,1)S(1)} async-done(((bf16[16,2,64,512]{3,2,1,0:T(8,128)(2,1)}), bf16[16,2,64,512]{3,2,1,0:T(8,128)(2,1)S(1)}, u32[]{:S(2)}, u32[]{:S(2)}) %all-to-all-start.1) | async-done | bytes 2097184 | tf_op jit(solution)/shard_map/all_to_all | solution.py:237
  130.9 0.3 convert_reduce_fusion
  131.2 1.9 %fusion.1 = f32[1,2,64,512]{3,2,1,0:T(8,128)} fusion(f32[2,64,512]{2,1,0:T(8,128)S(1)} %convert_reduce_fusion, f32[256,256]{1,0:T(8,128)S(1)} %get-tuple-element.37, f32[256,256]{1,0:T(8,128)S(1)} %get-tuple-element.36, f32[256,256]{1,0:T(8,128)S(1)} %copy-done.1, f32[2]{0:T(128)S(1)} %broadcast_add_fusion.2), kind=kOutput, calls=%fused_computation.10 | convolution fusion | flops 403505152 | bytes 1310728 | tf_op jit(solution)/shard_map/dot_general | solution.py:241
  (87 shorter events, 4.0 us)
Async XLA Ops:
  0.6 17.2 %copy-start.9 = (s32[128]{0:T(128)S(1)}, s32[128]{0:T(128)}, u32[]{:S(2)}) copy-start(s32[128]{0:T(128)} %param.8) | copy-start | bytes 1540
  0.6 14.1 %copy-start.13 = (f32[64]{0:T(128)S(1)}, f32[64]{0:T(128)}, u32[]{:S(2)}) copy-start(f32[64]{0:T(128)} %param.11) | copy-start | bytes 772
  2.0 15.8 %all-to-all-start = ((s32[32,128,3]{1,2,0:T(4,128)}), s32[32,128,3]{1,2,0:T(4,128)S(1)}, u32[]{:S(2)}, u32[]{:S(2)}) async-start(s32[32,128,3]{1,2,0:T(4,128)} %broadcast_in_dim.183), calls=%async_computation | async-start | bytes 131072 | tf_op jit(solution)/shard_map/all_to_all | solution.py:140
  12.3 1.5 %copy-start = (f32[256,256]{1,0:T(8,128)}, f32[256,256]{1,0:T(8,128)S(1)}, u32[]{:S(2)}) copy-start(f32[256,256]{1,0:T(8,128)S(1)} %fusion.26) | copy-start | bytes 786436
  22.9 23.6 %copy-start.2 = (f32[36,512]{1,0:T(8,128)S(1)}, f32[36,512]{1,0:T(8,128)}, u32[]{:S(2)}) copy-start(f32[36,512]{1,0:T(8,128)} %param.10) | copy-start | bytes 221188
  51.3 13.1 %copy-start.5 = (pred[256]{0:T(512)(128)(4,1)}, pred[256]{0:T(512)(128)(4,1)S(1)}, u32[]{:S(2)}) copy-start(pred[256]{0:T(512)(128)(4,1)S(1)} %compare_and_fusion.1) | copy-start | bytes 772
  63.5 0.8 copy-start.7
  63.5 0.8 copy-start.11
  64.0 1.3 copy-start.3
  78.7 3.2 %copy-start.10 = (s32[128]{0:T(128)S(1)}, s32[128]{0:T(128)}, u32[]{:S(2)}) copy-start(s32[128]{0:T(128)} %param.8) | copy-start | bytes 1540
  78.7 3.6 %copy-start.8 = (f32[128]{0:T(128)S(1)}, f32[128]{0:T(128)}, u32[]{:S(2)}) copy-start(f32[128]{0:T(128)} %copy-done.7) | copy-start | bytes 1540
  78.7 3.6 %copy-start.12 = (f32[128]{0:T(128)S(1)}, f32[128]{0:T(128)}, u32[]{:S(2)}) copy-start(f32[128]{0:T(128)} %copy-done.11) | copy-start | bytes 1540
  78.7 3.7 %copy-start.4 = (f32[256]{0:T(256)S(1)}, f32[256]{0:T(256)}, u32[]{:S(2)}) copy-start(f32[256]{0:T(256)} %copy-done.3) | copy-start | bytes 3076
  78.7 3.7 %copy-start.6 = (pred[256]{0:T(512)(128)(4,1)S(1)}, pred[256]{0:T(512)(128)(4,1)}, u32[]{:S(2)}) copy-start(pred[256]{0:T(512)(128)(4,1)} %copy-done.5) | copy-start | bytes 772
  81.9 6.9 %collective-permute-start = (bf16[16,2,64,512]{3,2,1,0:T(8,128)(2,1)}, bf16[16,2,64,512]{3,2,1,0:T(8,128)(2,1)S(1)}, u32[]{:S(2)}, u32[]{:S(2)}) collective-permute-start(bf16[16,2,64,512]{3,2,1,0:T(8,128)(2,1)} %dynamic-slice_bitcast_fusion), channel_id=1, source_target_pairs={{0,4},{4,0},{8,12},{12,8},{16,20},{20,16},{24,28},{28,24},{32,36},... | collective-permute-start | bytes 6291464 | tf_op jit(solution)/shard_map/ppermute | solution.py:234
  83.8 12.3 %all-to-all-start.2 = ((f32[32,1,10]{2,1,0:T(1,128)}), f32[32,1,10]{2,1,0:T(1,128)S(1)}, u32[]{:S(2)}, u32[]{:S(2)}) async-start(f32[32,1,10]{2,1,0:T(1,128)} %copy.43), calls=%async_computation.2 | async-start | bytes 32768 | tf_op jit(solution)/shard_map/all_to_all | solution.py:256
  96.1 34.8 %all-to-all-start.1 = ((bf16[16,2,64,512]{3,2,1,0:T(8,128)(2,1)}), bf16[16,2,64,512]{3,2,1,0:T(8,128)(2,1)S(1)}, u32[]{:S(2)}, u32[]{:S(2)}) async-start(bf16[16,2,64,512]{3,2,1,0:T(8,128)(2,1)} %fusion), calls=%async_computation.1 | async-start | bytes 4194304 | tf_op jit(solution)/shard_map/all_to_all | solution.py:237
  99.8 31.4 %copy-start.1 = (f32[256,256]{1,0:T(8,128)S(1)}, f32[256,256]{1,0:T(8,128)}, u32[]{:S(2)}) copy-start(f32[256,256]{1,0:T(8,128)} %copy-done) | copy-start | bytes 786436

commit v6 on v5

--- a/solution.py
+++ b/solution.py
@@ -29,31 +29,22 @@
 CHUNK = 512
 
 
-def cross_kernel(
-    count_ref, ent_p_ref, ent_k_ref, image_ref, refs_ref, forward_ref, wrow_ref,
-    cross_ref, image_hat_ref, ref_hat_ref, weighted_ref,
-):
-    forward = forward_ref[...]
-    wrow = wrow_ref[...]
-
-    def image_dft(c, carry):
-        r = pl.multiple_of(c * CHUNK, CHUNK)
-        image_hat_ref[pl.ds(r, CHUNK), :] = jnp.dot(
-            image_ref[pl.ds(r, CHUNK), :], forward, preferred_element_type=F32
-        ).astype(jnp.bfloat16)
-        return carry
-
-    def ref_dft(c, carry):
-        r = pl.multiple_of(c * CHUNK, CHUNK)
-        hat = jnp.dot(
-            refs_ref[pl.ds(r, CHUNK), :], forward, preferred_element_type=F32
-        ).astype(jnp.bfloat16)
-        ref_hat_ref[pl.ds(r, CHUNK), :] = hat
-        weighted_ref[pl.ds(r, CHUNK), :] = (hat.astype(F32) * wrow).astype(jnp.bfloat16)
-        return carry
-
-    lax.fori_loop(0, image_ref.shape[0] // CHUNK, image_dft, 0)
-    lax.fori_loop(0, refs_ref.shape[0] // CHUNK, ref_dft, 0)
+ROWS = 1024
+
+
+def image_dft_kernel(image_ref, forward_ref, out_ref):
+    out_ref[...] = jnp.dot(
+        image_ref[...], forward_ref[...], preferred_element_type=F32
+    ).astype(jnp.bfloat16)
+
+
+def ref_dft_kernel(refs_ref, forward_ref, wrow_ref, hat_ref, weighted_ref):
+    hat = jnp.dot(refs_ref[...], forward_ref[...], preferred_element_type=F32).astype(jnp.bfloat16)
+    hat_ref[...] = hat
+    weighted_ref[...] = (hat.astype(F32) * wrow_ref[...]).astype(jnp.bfloat16)
+
+
+def cross_kernel(count_ref, ent_p_ref, ent_k_ref, image_hat_ref, weighted_ref, cross_ref):
     cross_ref[...] = jnp.zeros_like(cross_ref)
 
     def body(e, carry):
@@ -163,23 +154,34 @@
 
     image_rows = images.shape[0] * NSHELL
     ref_rows = col_classes * NSHELL
-    wrow = jnp.tile(shell_weight, CHUNK // NSHELL)[:, None]
+    wrow = jnp.tile(shell_weight, ROWS // NSHELL)[:, None]
     params = pltpu.CompilerParams(vmem_limit_bytes=60 * 1024 * 1024)
-    cross_c, image_hat, ref_hat = pl.pallas_call(
-        cross_kernel,
+    row_block = pl.BlockSpec((ROWS, row_width), lambda i: (i, 0))
+    table_block = pl.BlockSpec((row_width, row_width), lambda i: (0, 0))
+    image_hat = pl.pallas_call(
+        image_dft_kernel,
+        out_shape=jax.ShapeDtypeStruct((image_rows, row_width), jnp.bfloat16),
+        grid=(image_rows // ROWS,),
+        in_specs=[row_block, table_block],
+        out_specs=row_block,
+    )(images.reshape(image_rows, row_width), forward)
+    ref_hat, weighted = pl.pallas_call(
+        ref_dft_kernel,
         out_shape=(
-            jax.ShapeDtypeStruct((entries, row_width), F32),
-            jax.ShapeDtypeStruct((image_rows, row_width), jnp.bfloat16),
+            jax.ShapeDtypeStruct((ref_rows, row_width), jnp.bfloat16),
             jax.ShapeDtypeStruct((ref_rows, row_width), jnp.bfloat16),
         ),
-        in_specs=[smem(), smem(), smem(), vmem(), vmem(), vmem(), vmem()],
-        out_specs=(vmem(), vmem(), vmem()),
-        scratch_shapes=[pltpu.VMEM((ref_rows, row_width), jnp.bfloat16)],
+        grid=(ref_rows // ROWS,),
+        in_specs=[row_block, table_block, pl.BlockSpec((ROWS, 1), lambda i: (0, 0))],
+        out_specs=(row_block, row_block),
+    )(references.reshape(ref_rows, row_width), forward, wrow)
+    cross_c = pl.pallas_call(
+        cross_kernel,
+        out_shape=jax.ShapeDtypeStruct((entries, row_width), F32),
+        in_specs=[smem(), smem(), smem(), vmem(), vmem()],
+        out_specs=vmem(),
         compiler_params=params,
-    )(
-        count_arr, ent_p, ent_k, images.reshape(image_rows, row_width),
-        references.reshape(ref_rows, row_width), forward, wrow,
-    )
+    )(count_arr, ent_p, ent_k, image_hat, weighted)
 
     log_prior = jnp.log1p(class_counts.astype(F32))
     prior = jnp.sum(

time: 134 us -> 138 us (1.030)
  Pallas kernels: 34.1 us -> 38.9 us
  starting transfers between devices: 16.9 us -> 19.5 us
  waiting for transfers between devices: 35.8 us -> 33.7 us
  blocking collectives: 10.9 us -> 9.01 us
    pallas_call x1 -> x3, Pallas kernels: 23.6 us -> 28.2 us  [the longest x1 10.9 us: local(): pl.pallas_call(image_dft_kernel, out_shape=jax.ShapeDtypeStruct((image_ro...]
    all_to_all x1, starting transfers between devices: 4.97 us -> 7.49 us  [local(): got = lax.all_to_all(small, 'dp', 0, 0, tiled=True)]
    all_to_all x1, waiting for transfers between devices: 2.16 us -> 0.01 us  [local(): lax.all_to_all(jnp.broadcast_to(packed[None], (dp_count,) + packed.shape)...]
    all_gather x1, blocking collectives: 10.9 us -> 9.01 us  [local(): gathered = lax.all_gather(jnp.stack([top_local, total_local]), 'cls')]
  transfers between devices with their start and end apart: 4 -> 4, of which waited for: 3 -> 2; matrix products, arithmetic and copies ran while one was open for 9% -> 9% of each run, Pallas kernels for 0% -> 13%
where the time goes in v6:
time: 138 us; the launch traced here: 136 us
  Pallas kernels  38.9 us (28%)
  waiting for transfers between devices  33.7 us (24%)
  starting transfers between devices  19.5 us (14%)
  other arithmetic  18.7 us (14%)
  local copies, waits for them, and re-layouts  11 us (8%)
  blocking collectives  9.01 us (7%)
  matrix products  4.77 us (3%)
    all_to_all x1, waiting for transfers between devices, local(): lax.all_to_all(pair_sum, 'dp', split_axis=0, concat_axis=0, tiled=True, a...  30.1 us
    pallas_call x1, Pallas kernels, local(): pl.pallas_call(image_dft_kernel, out_shape=jax.ShapeDtypeStruct((image_ro...  10.9 us
    pallas_call x1, Pallas kernels, local(): pl.pallas_call(grad_kernel, out_shape=jax.ShapeDtypeStruct((ref_rows, row...  10.8 us
    pallas_call x1, Pallas kernels, local(): pl.pallas_call(cross_kernel, out_shape=jax.ShapeDtypeStruct((entries, row...  9.83 us
    all_gather x1, blocking collectives, local(): gathered = lax.all_gather(jnp.stack([top_local, total_local]), 'cls')  9.01 us
    all_to_all x1, starting transfers between devices, local(): lax.all_to_all(jnp.broadcast_to(packed[None], (dp_count,) + packed.shape)...  8.25 us
    all_to_all x1, starting transfers between devices, local(): got = lax.all_to_all(small, 'dp', 0, 0, tiled=True)  7.49 us
    pallas_call x1, Pallas kernels, local(): pl.pallas_call(ref_dft_kernel, out_shape=(jax.ShapeDtypeStruct((ref_rows,...  7.39 us
  transfers between devices with their start and end apart: 4, of which 2 were waited for; matrix products, arithmetic and copies ran while one was open for 9% of the time, Pallas kernels for 13%

profile of v6, /device:TPU:0, one launch (start us, length us, event | category | flops | bytes accessed | tf_op | source)
XLA Modules:
  0.0 136.5 jit_solution(5635192754021316299)
XLA Ops:
  0.6 0.7 pad_add_fusion
  1.3 0.6 broadcast_in_dim.183
  2.0 8.2 %all-to-all-start = ((s32[32,128,3]{1,2,0:T(4,128)}), s32[32,128,3]{1,2,0:T(4,128)S(1)}, u32[]{:S(2)}, u32[]{:S(2)}) async-start(s32[32,128,3]{1,2,0:T(4,128)} %broadcast_in_dim.183), calls=%async_computation | async-start | bytes 131072 | tf_op jit(solution)/shard_map/all_to_all | solution.py:131
  10.2 1.1 sine_multiply_fusion
  11.3 1.0 fusion.26
  12.3 0.7 convert_log-plus-one_fusion
  13.0 0.8 fusion.60
  13.8 0.8 fusion.3.forward_ref
  14.6 1.3 broadcast_in_dim_tile.4.wrow_ref
  15.9 10.9 %shard_map.86.image_hat_ref = bf16[8192,512]{1,0:T(8,128)(2,1)} custom-call(bf16[8192,512]{1,0:T(8,128)(2,1)} %bitcast.80, bf16[512,512]{1,0:T(8,128)(2,1)} %fusion.3.forward_ref), custom_call_target="tpu_custom_call" | custom-call | tf_op jit(solution)/shard_map/pallas_call | solution.py:161
  26.8 7.4 %shard_map.87 = (bf16[4096,512]{1,0:T(8,128)(2,1)}, bf16[4096,512]{1,0:T(8,128)(2,1)}) custom-call(bf16[4096,512]{1,0:T(8,128)(2,1)} %bitcast.81, bf16[512,512]{1,0:T(8,128)(2,1)} %fusion.3.forward_ref, f32[1024,1]{1,0:T(8,128)} %broadcast_in_dim_tile.4.wrow_ref), custom_call_target="tpu_custom_call" | custom-call | tf_op jit(solution)/shard_map/pallas_call | solution.py:168
  34.3 0.6 select_reduce_fusion.1
  35.2 0.3 reduce-window.16
  35.5 0.6 convert_reduce_fusion.1
  36.3 0.3 reduce-window.24
  37.4 0.7 compare_and_fusion.2
  38.1 0.7 select_reduce_fusion.2
  38.8 0.6 and_select_fusion.4.ent_p_ref
  39.4 9.8 %shard_map.88 = f32[256,512]{1,0:T(8,128)} custom-call(s32[1]{0:T(128)} %bitcast.6.count_ref, s32[256]{0:T(256)} %and_select_fusion.4.ent_p_ref, s32[256]{0:T(256)} %get-tuple-element.8.ent_k_ref, bf16[8192,512]{1,0:T(8,128)(2,1)} %shard_map.86.image_hat_ref, bf16[4096,512]{1,0:T(8,128)(2,1)} %get-tuple-element.4.weighted_ref), custom_call_target="tpu_custom_call" | custom-call | tf_op jit(solution)/shard_map/pallas_call | solution.py:178
  49.2 1.6 %fusion.63 = f32[256,36]{1,0:T(8,128)S(1)} fusion(f32[256,512]{1,0:T(8,128)} %shard_map.88, f32[36,512]{1,0:T(8,128)S(1)} %copy-done), kind=kOutput, calls=%fused_computation.145 | convolution fusion | flops 56623104 | bytes 634880 | tf_op jit(solution)/shard_map/dot_general | solution.py:191
  51.0 0.7 compare_select_fusion.1
  52.2 0.2 reshape.445
  52.5 0.7 gather_fusion
  53.2 0.7 compare_and_fusion.1
  53.9 0.2 fusion.27
  54.5 0.2 sub.196
  54.6 0.3 select_reduce_fusion.4
  55.2 9.0 %all-gather.1 = f32[4,2,128]{2,1,0:T(2,128)S(1)} all-gather(f32[1,2,128]{2,1,0:T(2,128)S(1)} %maximum_bitcast_fusion.1), channel_id=2, replica_groups=mesh['dp'=32,'cls'=4] {'cls'}, dimensions={0}, use_global_device_ids=true | all-gather | bytes 5120 | tf_op jit(solution)/shard_map/all_gather | solution.py:199
  64.3 0.2 div.62
  64.6 0.2 sub.200
  65.1 0.9 fusion.12
  66.0 0.2 fusion.7
  66.2 1.1 gather_fusion.1
  67.3 0.7 pad_maximum_fusion.volume_ref
  68.0 0.9 slice_select_fusion.coef_ref
  68.9 10.8 %shard_map.89 = bf16[4096,512]{1,0:T(8,128)(2,1)} custom-call(s32[1]{0:T(128)} %bitcast.6.count_ref, s32[256]{0:T(256)} %and_select_fusion.4.ent_p_ref, s32[256]{0:T(256)} %get-tuple-element.8.ent_k_ref, bf16[8192,512]{1,0:T(8,128)(2,1)} %shard_map.86.image_hat_ref, f32[256,512]{1,0:T(8,128)} %slice_select_fusion.coef_ref, ...), custom_call_target="tpu_custom_call" | custom-call | tf_op jit(solution)/shard_map/pallas_call | solution.py:223
  79.7 3.2 %dynamic-slice_bitcast_fusion = bf16[16,2,64,512]{3,2,1,0:T(8,128)(2,1)} fusion(bf16[16,2,2,64,512]{4,3,2,1,0:T(8,128)(2,1)} %bitcast.78, s32[]{:T(128)S(6)} %select_n.189), kind=kLoop, calls=%fused_computation.5 | loop fusion | bytes 4194308 | tf_op jit(solution)/shard_map/jit(dynamic_index_in_dim)/squeeze | solution.py:235
  82.9 0.3 reduce_window_sum.82
  83.3 0.3 fusion.20
  84.0 0.7 copy.43
  84.7 7.5 %all-to-all-start.2 = ((f32[32,1,10]{2,1,0:T(1,128)}), f32[32,1,10]{2,1,0:T(1,128)S(1)}, u32[]{:S(2)}, u32[]{:S(2)}) async-start(f32[32,1,10]{2,1,0:T(1,128)} %copy.43), calls=%async_computation.2 | async-start | bytes 32768 | tf_op jit(solution)/shard_map/all_to_all | solution.py:258
  92.2 3.7 %fusion = bf16[16,2,64,512]{3,2,1,0:T(8,128)(2,1)} fusion(bf16[16,2,64,512]{3,2,1,0:T(8,128)(2,1)S(1)} %collective-permute-done, bf16[16,2,2,64,512]{4,3,2,1,0:T(8,128)(2,1)} %bitcast.79, s32[]{:T(128)S(6)} %select_n.188), kind=kLoop, calls=%fused_computation.3 | loop fusion | flops 4194304 | bytes 6291460 | tf_op jit(solution)/shard_map/convert_element_type | solution.py:237
  95.9 3.6 %all-to-all-done.2 = f32[32,1,10]{2,1,0:T(1,128)S(1)} async-done(((f32[32,1,10]{2,1,0:T(1,128)}), f32[32,1,10]{2,1,0:T(1,128)S(1)}, u32[]{:S(2)}, u32[]{:S(2)}) %all-to-all-start.2) | async-done | bytes 1312 | tf_op jit(solution)/shard_map/all_to_all | solution.py:258
  99.5 3.7 %all-to-all-start.1 = ((bf16[16,2,64,512]{3,2,1,0:T(8,128)(2,1)}), bf16[16,2,64,512]{3,2,1,0:T(8,128)(2,1)S(1)}, u32[]{:S(2)}, u32[]{:S(2)}) async-start(bf16[16,2,64,512]{3,2,1,0:T(8,128)(2,1)} %fusion), calls=%async_computation.1 | async-start | bytes 4194304 | tf_op jit(solution)/shard_map/all_to_all | solution.py:239
  103.6 0.6 select_reduce_fusion.5
  104.2 30.1 %all-to-all-done.1 = bf16[16,2,64,512]{3,2,1,0:T(8,128)(2,1)S(1)} async-done(((bf16[16,2,64,512]{3,2,1,0:T(8,128)(2,1)}), bf16[16,2,64,512]{3,2,1,0:T(8,128)(2,1)S(1)}, u32[]{:S(2)}, u32[]{:S(2)}) %all-to-all-start.1) | async-done | bytes 2097184 | tf_op jit(solution)/shard_map/all_to_all | solution.py:239
  134.3 0.3 convert_reduce_fusion
  134.6 1.9 %fusion.1 = f32[1,2,64,512]{3,2,1,0:T(8,128)} fusion(f32[2,64,512]{2,1,0:T(8,128)S(1)} %convert_reduce_fusion, f32[256,256]{1,0:T(8,128)S(1)} %get-tuple-element.35, f32[256,256]{1,0:T(8,128)S(1)} %get-tuple-element.34, f32[256,256]{1,0:T(8,128)S(1)} %fusion.26, f32[2]{0:T(128)S(1)} %broadcast_add_fusion.2), kind=kOutput, calls=%fused_computation.10 | convolution fusion | flops 403505152 | bytes 1310728 | tf_op jit(solution)/shard_map/dot_general | solution.py:243
  (67 shorter events, 4.1 us)
Async XLA Ops:
  0.6 14.0 %copy-start.2 = (f32[64]{0:T(128)S(1)}, f32[64]{0:T(128)}, u32[]{:S(2)}) copy-start(f32[64]{0:T(128)} %param.11) | copy-start | bytes 772
  2.0 32.2 %all-to-all-start = ((s32[32,128,3]{1,2,0:T(4,128)}), s32[32,128,3]{1,2,0:T(4,128)S(1)}, u32[]{:S(2)}, u32[]{:S(2)}) async-start(s32[32,128,3]{1,2,0:T(4,128)} %broadcast_in_dim.183), calls=%async_computation | async-start | bytes 131072 | tf_op jit(solution)/shard_map/all_to_all | solution.py:131
  26.8 7.4 %copy-start.1 = (s32[128]{0:T(128)S(1)}, s32[128]{0:T(128)}, u32[]{:S(2)}) copy-start(s32[128]{0:T(128)} %param.8) | copy-start | bytes 1540
  39.4 9.8 %copy-start = (f32[36,512]{1,0:T(8,128)S(1)}, f32[36,512]{1,0:T(8,128)}, u32[]{:S(2)}) copy-start(f32[36,512]{1,0:T(8,128)} %param.10) | copy-start | bytes 221188
  82.8 9.4 %collective-permute-start = (bf16[16,2,64,512]{3,2,1,0:T(8,128)(2,1)}, bf16[16,2,64,512]{3,2,1,0:T(8,128)(2,1)S(1)}, u32[]{:S(2)}, u32[]{:S(2)}) collective-permute-start(bf16[16,2,64,512]{3,2,1,0:T(8,128)(2,1)} %dynamic-slice_bitcast_fusion), channel_id=1, source_target_pairs={{0,4},{4,0},{8,12},{12,8},{16,20},{20,16},{24,28},{28,24},{32,36},... | collective-permute-start | bytes 6291464 | tf_op jit(solution)/shard_map/ppermute | solution.py:236
  84.7 14.8 %all-to-all-start.2 = ((f32[32,1,10]{2,1,0:T(1,128)}), f32[32,1,10]{2,1,0:T(1,128)S(1)}, u32[]{:S(2)}, u32[]{:S(2)}) async-start(f32[32,1,10]{2,1,0:T(1,128)} %copy.43), calls=%async_computation.2 | async-start | bytes 32768 | tf_op jit(solution)/shard_map/all_to_all | solution.py:258
  99.5 34.8 %all-to-all-start.1 = ((bf16[16,2,64,512]{3,2,1,0:T(8,128)(2,1)}), bf16[16,2,64,512]{3,2,1,0:T(8,128)(2,1)S(1)}, u32[]{:S(2)}, u32[]{:S(2)}) async-start(bf16[16,2,64,512]{3,2,1,0:T(8,128)(2,1)} %fusion), calls=%async_computation.1 | async-start | bytes 4194304 | tf_op jit(solution)/shard_map/all_to_all | solution.py:239

commit v7 on v4

--- a/solution.py
+++ b/solution.py
@@ -27,6 +27,7 @@
 
 
 CHUNK = 512
+EXTRA = 16
 
 
 def cross_kernel(
@@ -110,6 +111,12 @@
         return carry
 
     lax.fori_loop(0, acc_ref.shape[0] // CHUNK, finish, 0)
+
+
+def split_pair(x):
+    high = x.astype(jnp.bfloat16)
+    low = (x - high.astype(F32)).astype(jnp.bfloat16)
+    return high, low
 
 
 def smem():
@@ -227,13 +234,7 @@
         compiler_params=params,
     )(count_arr, ent_p, ent_k, image_hat, coef_c[:, :row_width], ref_hat, volume_full)
 
-    outgoing = numer.reshape(dp_count, per_owner, NSHELL, row_width)
-    arrived = lax.all_to_all(outgoing, "dp", split_axis=0, concat_axis=0, tiled=True)
-    summed = jnp.sum(arrived.astype(F32), axis=0)
-    summed = jnp.dot(
-        summed.reshape(-1, row_width), inverse, precision=HIGHEST
-    ).reshape(summed.shape)
-
+    core = dp_index % 2
     dest = pose_slot // blocksize
     dest_hit = dest[None, :] == jnp.arange(dp_count, dtype=jnp.int32)[:, None]
     dest_i = dest_hit.astype(jnp.int32)
@@ -244,11 +245,41 @@
     send_ev = jnp.sum(jnp.where(sel, evidence[None, None, :], 0.0), axis=2)
     send_pos = jnp.sum(jnp.where(sel, (pose_slot % blocksize).astype(F32)[None, None, :], 0.0), axis=2)
     send_den = denom_part.reshape(dp_count, per_owner)
-    small = jnp.concatenate([send_ev, send_pos, send_den], axis=1)
-    got = lax.all_to_all(small, "dp", 0, 0, tiled=True)
-    got_ev = got[:, :per_pair].reshape(-1)
-    got_pos = got[:, per_pair : 2 * per_pair].reshape(-1)
-    own_denom = jnp.sum(got[:, 2 * per_pair :], axis=0)
+    ev_hi, ev_lo = split_pair(send_ev)
+    den_hi, den_lo = split_pair(send_den)
+    small = jnp.concatenate(
+        [ev_hi, ev_lo, send_pos.astype(jnp.bfloat16), den_hi, den_lo], axis=1
+    )
+    slot_w = small.shape[1]
+    small_row = lax.dynamic_update_slice(
+        jnp.zeros((dp_count, row_width), jnp.bfloat16), small, (0, core * slot_w)
+    )
+    extra = jnp.zeros((dp_count, EXTRA, row_width), jnp.bfloat16).at[:, 0, :].set(small_row)
+    chunk_rows = per_owner * NSHELL
+    chunks = jnp.concatenate(
+        [numer.reshape(dp_count, chunk_rows, row_width), extra], axis=1
+    )
+
+    by_core = chunks.reshape(dp_count // 2, 2, chunk_rows + EXTRA, row_width)
+    keep = lax.dynamic_index_in_dim(by_core, core, axis=1, keepdims=False)
+    give = lax.dynamic_index_in_dim(by_core, 1 - core, axis=1, keepdims=False)
+    taken = lax.ppermute(give, "dp", perm=[(i, i ^ 1) for i in range(dp_count)])
+    pair_sum = (keep.astype(F32) + taken.astype(F32)).astype(jnp.bfloat16)
+    groups = [list(range(q, dp_count, 2)) for q in range(2)]
+    arrived = lax.all_to_all(
+        pair_sum, "dp", split_axis=0, concat_axis=0, tiled=True, axis_index_groups=groups
+    )
+    summed = jnp.sum(arrived[:, :chunk_rows].astype(F32), axis=0)
+    summed = jnp.dot(summed, inverse, precision=HIGHEST).reshape(per_owner, NSHELL, row_width)
+
+    got = arrived[:, chunk_rows, : 2 * slot_w].astype(F32).reshape(dp_count, slot_w)
+    got_ev = (got[:, :per_pair] + got[:, per_pair : 2 * per_pair]).reshape(-1)
+    got_pos = got[:, 2 * per_pair : 3 * per_pair].reshape(-1)
+    den_at = 3 * per_pair
+    own_denom = jnp.sum(
+        got[:, den_at : den_at + per_owner] + got[:, den_at + per_owner : den_at + 2 * per_owner],
+        axis=0,
+    )
     gradient = summed / (1.0 + own_denom)[:, None, None]
     rows = jnp.arange(blocksize, dtype=F32)
     placed = jnp.sum(jnp.where(got_pos[None, :] == rows[:, None], got_ev[None, :], 0.0), axis=1)

time: 154 us -> 133 us (0.86)
  waiting for transfers between devices: 52.3 us -> 5.46 us
  blocking collectives: 10.2 us -> 46.9 us
  starting transfers between devices: 22.6 us -> 11.1 us
  other arithmetic: 19 us -> 20.6 us
    all_to_all x2 -> x0, waiting for transfers between devices: 51.8 us -> none  [the longest x1 51.8 us: local(): lax.all_to_all(outgoing, 'dp', split_axis=0, concat_axis=0, tiled=True)]
    all_to_all x0 -> x1, blocking collectives: none -> 37.6 us  [local(): lax.all_to_all(pair_sum, 'dp', split_axis=0, concat_axis=0, tiled=True, a...]
    all_to_all x2 -> x0, starting transfers between devices: 14.3 us -> none  [the longest x1 7.62 us: local(): lax.all_to_all(outgoing, 'dp', split_axis=0, concat_axis=0, tiled=True)]
    ppermute x0 -> x1, waiting for transfers between devices: none -> 4.29 us  [local(): taken = lax.ppermute(give, 'dp', perm=[(i, i ^ 1) for i in range(dp_count)])]
    ppermute x0 -> x1, starting transfers between devices: none -> 2.9 us  [local(): taken = lax.ppermute(give, 'dp', perm=[(i, i ^ 1) for i in range(dp_count)])]
    reduce_sum x3, other arithmetic: 3.16 us -> 0.5 us  [the longest x1 0.29 us: local(): summed = jnp.sum(arrived[:, :chunk_rows].astype(F32), axis=0)]
    convert_element_type x1 -> x4, other arithmetic: 0.67 us -> 3.08 us  [the longest x1 3.04 us: local(): pair_sum = (keep.astype(F32) + taken.astype(F32)).astype(jnp.bfloat16)]
    squeeze x0 -> x1, other arithmetic: none -> 1.8 us  [local(): give = lax.dynamic_index_in_dim(by_core, 1 - core, axis=1, keepdims=False)]
  transfers between devices with their start and end apart: 3 -> 2, of which waited for: 2 -> 2; matrix products, arithmetic and copies ran while one was open for 8% -> 5% of each run, Pallas kernels for 7% -> 0%
where the time goes in v7:
time: 133 us
  blocking collectives  46.9 us (35%)
  Pallas kernels  34.7 us (26%)
  other arithmetic  20.6 us (15%)
  starting transfers between devices  11.1 us (8%)
  local copies, waits for them, and re-layouts  7.95 us (6%)
  waiting for transfers between devices  5.46 us (4%)
  matrix products  4.78 us (4%)
    all_to_all x1, blocking collectives, local(): lax.all_to_all(pair_sum, 'dp', split_axis=0, concat_axis=0, tiled=True, a...  37.6 us
    pallas_call x1, Pallas kernels, local(): pl.pallas_call(cross_kernel, out_shape=(jax.ShapeDtypeStruct((entries, ro...  24 us
    pallas_call x1, Pallas kernels, local(): pl.pallas_call(grad_kernel, out_shape=jax.ShapeDtypeStruct((ref_rows, row...  10.7 us
    all_gather x1, blocking collectives, local(): gathered = lax.all_gather(jnp.stack([top_local, total_local]), 'cls')  9.33 us
    all_to_all x1, starting transfers between devices, local(): lax.all_to_all(jnp.broadcast_to(packed[None], (dp_count,) + packed.shape)...  8.25 us
    ppermute x1, waiting for transfers between devices, local(): taken = lax.ppermute(give, 'dp', perm=[(i, i ^ 1) for i in range(dp_count)])  4.29 us
    convert_element_type x1, other arithmetic, local(): pair_sum = (keep.astype(F32) + taken.astype(F32)).astype(jnp.bfloat16)  3.04 us
    ppermute x1, starting transfers between devices, local(): taken = lax.ppermute(give, 'dp', perm=[(i, i ^ 1) for i in range(dp_count)])  2.9 us
  transfers between devices with their start and end apart: 2, of which 2 were waited for; matrix products, arithmetic and copies ran while one was open for 5% of the time, Pallas kernels for 0%

profile of v7, /device:TPU:0, one launch (start us, length us, event | category | flops | bytes accessed | tf_op | source)
XLA Modules:
  0.0 132.6 jit_solution(7463102071805936192)
XLA Ops:
  0.7 0.7 pad_add_fusion
  1.4 0.6 broadcast_in_dim.187
  2.0 8.2 %all-to-all-start = ((s32[32,128,3]{1,2,0:T(4,128)}), s32[32,128,3]{1,2,0:T(4,128)S(1)}, u32[]{:S(2)}, u32[]{:S(2)}) async-start(s32[32,128,3]{1,2,0:T(4,128)} %broadcast_in_dim.187), calls=%async_computation | async-start | bytes 131072 | tf_op jit(solution)/shard_map/all_to_all | solution.py:147
  10.3 1.1 sine_multiply_fusion
  11.3 1.0 fusion.30
  12.3 0.7 and_select_fusion.3
  13.0 0.8 fusion.66
  13.8 0.7 convert_log-plus-one_fusion
  14.5 0.3 reduce_window_sum.82
  14.8 0.9 fusion.7.forward_ref
  15.7 0.9 broadcast_in_dim_tile.4.wrow_ref
  16.6 1.2 all-to-all-done
  17.8 0.6 select_reduce_fusion.1
  18.8 0.3 reduce-window.16
  19.1 0.6 convert_reduce_fusion.1
  20.1 0.3 reduce-window.24
  21.0 0.7 compare_and_fusion.2
  21.7 0.7 select_reduce_fusion.2
  22.4 0.6 and_select_fusion.4.ent_p_ref
  23.0 24.0 %shard_map.86 = (f32[256,512]{1,0:T(8,128)}, bf16[8192,512]{1,0:T(8,128)(2,1)}, bf16[4096,512]{1,0:T(8,128)(2,1)}) custom-call(s32[1]{0:T(128)} %bitcast.6.count_ref, s32[256]{0:T(256)} %and_select_fusion.4.ent_p_ref, s32[256]{0:T(256)} %get-tuple-element.22.ent_k_ref, bf16[8192,512]{1,0:T(8,128)(2,1)} %bitcast.86, bf16[4096,512]{1,0:T(8,128)(2,1)} %bitcast.89, ...), custom_call_target="tpu_custom_call" | custom-call | tf_op jit(solution)/shard_map/pallas_call | solution.py:175
  47.1 1.6 %fusion.69 = f32[256,36]{1,0:T(8,128)S(1)} fusion(f32[256,512]{1,0:T(8,128)} %get-tuple-element.18, f32[36,512]{1,0:T(8,128)S(1)} %copy-done.2), kind=kOutput, calls=%fused_computation.157 | convolution fusion | flops 56623104 | bytes 634880 | tf_op jit(solution)/shard_map/dot_general | solution.py:196
  48.8 0.7 compare_select_fusion
  50.2 0.2 reshape.483
  50.4 0.7 gather_fusion
  51.1 0.7 compare_and_fusion.1
  51.8 0.2 fusion.31
  52.4 0.2 sub.202
  52.5 0.3 select_reduce_fusion.4
  53.1 9.3 %all-gather.1 = f32[4,2,128]{2,1,0:T(2,128)S(1)} all-gather(f32[1,2,128]{2,1,0:T(2,128)S(1)} %maximum_bitcast_fusion), channel_id=2, replica_groups=mesh['dp'=32,'cls'=4] {'cls'}, dimensions={0}, use_global_device_ids=true | all-gather | bytes 5120 | tf_op jit(solution)/shard_map/all_gather | solution.py:204
  62.5 0.2 div.62
  62.8 0.2 sub.206
  63.3 0.3 fusion.24
  63.6 1.0 fusion.16
  64.5 0.2 fusion.11
  64.8 1.1 gather_fusion.1
  65.9 0.7 pad_maximum_fusion.volume_ref
  67.2 0.6 dynamic_update_slice.6
  67.9 0.9 slice_select_fusion.coef_ref
  68.8 10.7 %shard_map.87 = bf16[4096,512]{1,0:T(8,128)(2,1)} custom-call(s32[1]{0:T(128)} %bitcast.6.count_ref, s32[256]{0:T(256)} %and_select_fusion.4.ent_p_ref, s32[256]{0:T(256)} %get-tuple-element.22.ent_k_ref, bf16[8192,512]{1,0:T(8,128)(2,1)} %get-tuple-element.17.image_hat_ref, f32[256,512]{1,0:T(8,128)} %slice_select_fusion.coef_ref, ...), custom_call_target="tpu_custom_call" | custom-call | tf_op jit(solution)/shard_map/pallas_call | solution.py:228
  79.5 1.8 %fusion.2 = bf16[16,144,512]{2,1,0:T(8,128)(2,1)S(1)} fusion(s32[]{:T(128)S(6)} %select_n.198, bf16[16,2,128,512]{3,2,1,0:T(8,128)(2,1)} %bitcast.84, bf16[16,2,16,512]{3,2,1,0:T(8,128)(2,1)S(1)} %bitcast.87), kind=kLoop, calls=%fused_computation.10 | loop fusion | flops 4718592 | bytes 7077892 | tf_op jit(solution)/shard_map/jit(dynamic_index_in_dim)/squeeze | solution.py:265
  81.3 2.9 %collective-permute-start = (bf16[16,144,512]{2,1,0:T(8,128)(2,1)S(1)}, bf16[16,144,512]{2,1,0:T(8,128)(2,1)}, u32[]{:S(2)}, u32[]{:S(2)}) collective-permute-start(bf16[16,144,512]{2,1,0:T(8,128)(2,1)S(1)} %fusion.2), channel_id=1, source_target_pairs={{0,4},{4,0},{8,12},{12,8},{16,20},{20,16},{24,28},{28,24},{32,36},... | collective-permute-start | bytes 7077896 | tf_op jit(solution)/shard_map/ppermute | solution.py:266
  84.2 4.3 %collective-permute-done = bf16[16,144,512]{2,1,0:T(8,128)(2,1)} collective-permute-done((bf16[16,144,512]{2,1,0:T(8,128)(2,1)S(1)}, bf16[16,144,512]{2,1,0:T(8,128)(2,1)}, u32[]{:S(2)}, u32[]{:S(2)}) %collective-permute-start) | collective-permute-done | bytes 2359328 | tf_op jit(solution)/shard_map/ppermute | solution.py:266
  88.5 3.0 %fusion = bf16[16,144,512]{2,1,0:T(8,128)(2,1)S(1)} fusion(bf16[16,144,512]{2,1,0:T(8,128)(2,1)} %collective-permute-done, s32[]{:T(128)S(6)} %select_n.197, bf16[16,2,128,512]{3,2,1,0:T(8,128)(2,1)} %bitcast.85, bf16[16,2,16,512]{3,2,1,0:T(8,128)(2,1)S(1)} %bitcast.88), kind=kLoop, calls=%fused_computation.5 | loop fusion | flops 9437184 | bytes 9437188 | tf_op jit(solution)/shard_map/convert_element_type | solution.py:267
  91.5 37.6 %all_to_all.10 = bf16[16,144,512]{2,1,0:T(8,128)(2,1)S(1)} all-to-all(bf16[16,144,512]{2,1,0:T(8,128)(2,1)S(1)} %fusion), channel_id=1, replica_groups={{0,8,16,24,32,40,48,56,64,72,80,88,96,104,112,120},{4,12,20,28,36,44,52..., dimensions={0} | all-to-all | bytes 4718592 | tf_op jit(solution)/shard_map/all_to_all | solution.py:269
  129.6 0.3 convert_reduce_fusion
  129.9 0.2 copy-done.1
  130.0 1.9 %fusion.5 = f32[1,2,64,512]{3,2,1,0:T(8,128)} fusion(f32[2,64,512]{2,1,0:T(8,128)S(1)} %bitcast.90, f32[256,256]{1,0:T(8,128)S(1)} %get-tuple-element.55, f32[256,256]{1,0:T(8,128)S(1)} %get-tuple-element.54, f32[256,256]{1,0:T(8,128)S(1)} %copy-done.1, f32[2]{0:T(128)S(1)} %broadcast_add_fusion.2), kind=kOutput, calls=%fused_computation.17 | convolution fusion | flops 403505152 | bytes 1310728 | tf_op jit(solution)/shard_map/dot_general | solution.py:273
  131.9 0.6 select_reduce_fusion.5
  (72 shorter events, 4.5 us)
Async XLA Ops:
  0.6 17.2 %copy-start.3 = (s32[128]{0:T(128)S(1)}, s32[128]{0:T(128)}, u32[]{:S(2)}) copy-start(s32[128]{0:T(128)} %param.10) | copy-start | bytes 1540
  0.6 15.1 %copy-start.4 = (f32[64]{0:T(128)S(1)}, f32[64]{0:T(128)}, u32[]{:S(2)}) copy-start(f32[64]{0:T(128)} %param.13) | copy-start | bytes 772
  2.0 15.8 %all-to-all-start = ((s32[32,128,3]{1,2,0:T(4,128)}), s32[32,128,3]{1,2,0:T(4,128)S(1)}, u32[]{:S(2)}, u32[]{:S(2)}) async-start(s32[32,128,3]{1,2,0:T(4,128)} %broadcast_in_dim.187), calls=%async_computation | async-start | bytes 131072 | tf_op jit(solution)/shard_map/all_to_all | solution.py:147
  12.3 34.8 %copy-start = (f32[256,256]{1,0:T(8,128)}, f32[256,256]{1,0:T(8,128)S(1)}, u32[]{:S(2)}) copy-start(f32[256,256]{1,0:T(8,128)S(1)} %fusion.30) | copy-start | bytes 786436
  23.0 24.1 %copy-start.2 = (f32[36,512]{1,0:T(8,128)S(1)}, f32[36,512]{1,0:T(8,128)}, u32[]{:S(2)}) copy-start(f32[36,512]{1,0:T(8,128)} %param.12) | copy-start | bytes 221188
  81.3 7.2 %collective-permute-start = (bf16[16,144,512]{2,1,0:T(8,128)(2,1)S(1)}, bf16[16,144,512]{2,1,0:T(8,128)(2,1)}, u32[]{:S(2)}, u32[]{:S(2)}) collective-permute-start(bf16[16,144,512]{2,1,0:T(8,128)(2,1)S(1)} %fusion.2), channel_id=1, source_target_pairs={{0,4},{4,0},{8,12},{12,8},{16,20},{20,16},{24,28},{28,24},{32,36},... | collective-permute-start | bytes 7077896 | tf_op jit(solution)/shard_map/ppermute | solution.py:266
  129.1 1.0 copy-start.1

commit v8 on v7

--- a/solution.py
+++ b/solution.py
@@ -225,16 +225,41 @@
     volume = jnp.dot(class_pick, coef[:, row_width:], precision=HIGHEST)
     denom_part = jnp.dot(class_pick, post_sum, precision=HIGHEST)
     volume_full = jnp.concatenate([volume, volume], axis=1)
-    numer = pl.pallas_call(
-        grad_kernel,
-        out_shape=jax.ShapeDtypeStruct((ref_rows, row_width), jnp.bfloat16),
-        in_specs=[smem(), smem(), smem(), vmem(), vmem(), vmem(), vmem()],
-        out_specs=vmem(),
-        scratch_shapes=[pltpu.VMEM((ref_rows, row_width), F32)],
-        compiler_params=params,
-    )(count_arr, ent_p, ent_k, image_hat, coef_c[:, :row_width], ref_hat, volume_full)
-
     core = dp_index % 2
+    half_rows = ref_rows // 2
+    half_classes = col_classes // 2
+    ref_by = ref_hat.reshape(dp_count // 2, 2, per_owner * NSHELL, row_width)
+    vol_by = volume_full.reshape(dp_count // 2, 2, per_owner, row_width)
+    owner_core = (local_class // per_owner) % 2
+    within_half = jnp.clip(
+        (local_class // (2 * per_owner)) * per_owner + local_class % per_owner, 0, half_classes - 1
+    )
+
+    def half_numer(hcore):
+        in_half = inside & (owner_core == hcore)
+        half_i = in_half.astype(jnp.int32)
+        half_count = jnp.sum(half_i)
+        half_rank = jnp.where(
+            in_half, jnp.cumsum(half_i) - half_i, half_count + jnp.cumsum(1 - half_i) - (1 - half_i)
+        )
+        hit = half_rank[None, :] == slots[:, None]
+        half_order = jnp.sum(jnp.where(hit, slots[None, :], 0), axis=1)
+        half_p = half_order // LIST
+        half_k = jnp.sum(jnp.where(hit, within_half[None, :], 0), axis=1)
+        half_coef = jnp.take(coef[:, :row_width], half_order, axis=0)
+        half_refs = lax.dynamic_index_in_dim(ref_by, hcore, 1, False).reshape(half_rows, row_width)
+        half_vol = lax.dynamic_index_in_dim(vol_by, hcore, 1, False).reshape(half_classes, row_width)
+        return pl.pallas_call(
+            grad_kernel,
+            out_shape=jax.ShapeDtypeStruct((half_rows, row_width), jnp.bfloat16),
+            in_specs=[smem(), smem(), smem(), vmem(), vmem(), vmem(), vmem()],
+            out_specs=vmem(),
+            scratch_shapes=[pltpu.VMEM((half_rows, row_width), F32)],
+            compiler_params=params,
+        )(half_count.reshape(1), half_p, half_k, image_hat, half_coef, half_refs, half_vol)
+
+    give_numer = half_numer(1 - core)
+
     dest = pose_slot // blocksize
     dest_hit = dest[None, :] == jnp.arange(dp_count, dtype=jnp.int32)[:, None]
     dest_i = dest_hit.astype(jnp.int32)
@@ -256,14 +281,23 @@
     )
     extra = jnp.zeros((dp_count, EXTRA, row_width), jnp.bfloat16).at[:, 0, :].set(small_row)
     chunk_rows = per_owner * NSHELL
-    chunks = jnp.concatenate(
-        [numer.reshape(dp_count, chunk_rows, row_width), extra], axis=1
-    )
-
-    by_core = chunks.reshape(dp_count // 2, 2, chunk_rows + EXTRA, row_width)
-    keep = lax.dynamic_index_in_dim(by_core, core, axis=1, keepdims=False)
-    give = lax.dynamic_index_in_dim(by_core, 1 - core, axis=1, keepdims=False)
+    extra_by = extra.reshape(dp_count // 2, 2, EXTRA, row_width)
+    give = jnp.concatenate(
+        [
+            give_numer.reshape(dp_count // 2, chunk_rows, row_width),
+            lax.dynamic_index_in_dim(extra_by, 1 - core, 1, False),
+        ],
+        axis=1,
+    )
     taken = lax.ppermute(give, "dp", perm=[(i, i ^ 1) for i in range(dp_count)])
+    keep_numer = half_numer(core)
+    keep = jnp.concatenate(
+        [
+            keep_numer.reshape(dp_count // 2, chunk_rows, row_width),
+            lax.dynamic_index_in_dim(extra_by, core, 1, False),
+        ],
+        axis=1,
+    )
     pair_sum = (keep.astype(F32) + taken.astype(F32)).astype(jnp.bfloat16)
     groups = [list(range(q, dp_count, 2)) for q in range(2)]
     arrived = lax.all_to_all(

time: 133 us -> 147 us (1.11)
  local copies, waits for them, and re-layouts: 7.95 us -> 16.4 us
  other arithmetic: 20.6 us -> 25.6 us
  Pallas kernels: 34.7 us -> 39.2 us
  waiting for transfers between devices: 5.46 us -> 1.13 us
    pallas_call x1 -> x2, Pallas kernels: 10.7 us -> 15.5 us  [half_numer(): pl.pallas_call(grad_kernel, out_shape=jax.ShapeDtypeStruct((half_rows, ro...]
    dynamic_slice x0 -> x1, local copies, waits for them, and re-layouts: none -> 4.63 us  [half_numer(): lax.dynamic_index_in_dim(ref_by, hcore, 1, False)]
    ppermute x1, waiting for transfers between devices: 4.29 us -> 0.01 us  [local(): taken = lax.ppermute(give, 'dp', perm=[(i, i ^ 1) for i in range(dp_count)])]
    concatenate x0 -> x1, other arithmetic: none -> 3.28 us  [local(): jnp.concatenate([give_numer.reshape(dp_count // 2, chunk_rows, row_width)...]
    select_n x3 -> x7, other arithmetic: 2.14 us -> 4.97 us  [the longest x4 3.04 us: half_numer(): half_coef = jnp.take(coef[:, :row_width], half_order, axis=0)]
    squeeze x1 -> x0, other arithmetic: 1.8 us -> none  [local(): give = lax.dynamic_index_in_dim(by_core, 1 - core, axis=1, keepdims=False)]
  transfers between devices with their start and end apart: 2 -> 2, of which waited for: 2 -> 1; matrix products, arithmetic and copies ran while one was open for 5% -> 6% of each run, Pallas kernels for 0% -> 5%
where the time goes in v8:
time: 147 us; the launch traced here: 146 us
  blocking collectives  47 us (32%)
  Pallas kernels  39.2 us (27%)
  other arithmetic  25.6 us (17%)
  local copies, waits for them, and re-layouts  16.4 us (11%)
  starting transfers between devices  11 us (7%)
  matrix products  4.78 us (3%)
    all_to_all x1, blocking collectives, local(): lax.all_to_all(pair_sum, 'dp', split_axis=0, concat_axis=0, tiled=True, a...  36.8 us
    pallas_call x1, Pallas kernels, local(): pl.pallas_call(cross_kernel, out_shape=(jax.ShapeDtypeStruct((entries, ro...  23.7 us
    pallas_call x2, Pallas kernels, half_numer(): pl.pallas_call(grad_kernel, out_shape=jax.ShapeDtypeStruct((half_rows, ro...  15.5 us
    all_gather x1, blocking collectives, local(): gathered = lax.all_gather(jnp.stack([top_local, total_local]), 'cls')  10.3 us
    all_to_all x1, starting transfers between devices, local(): lax.all_to_all(jnp.broadcast_to(packed[None], (dp_count,) + packed.shape)...  8.25 us
    dynamic_slice x1, local copies, waits for them, and re-layouts, half_numer(): lax.dynamic_index_in_dim(ref_by, hcore, 1, False)  4.63 us
    concatenate x1, other arithmetic, local(): jnp.concatenate([give_numer.reshape(dp_count // 2, chunk_rows, row_width)...  3.28 us
    select_n x4, other arithmetic, half_numer(): half_coef = jnp.take(coef[:, :row_width], half_order, axis=0)  3.04 us
  transfers between devices with their start and end apart: 2, of which 1 were waited for; matrix products, arithmetic and copies ran while one was open for 6% of the time, Pallas kernels for 5%

profile of v8, /device:TPU:0, one launch (start us, length us, event | category | flops | bytes accessed | tf_op | source)
XLA Modules:
  0.0 146.2 jit_solution(9066850098019449316)
XLA Ops:
  0.7 0.7 pad_add_fusion
  1.4 0.6 broadcast_in_dim.216
  2.0 8.2 %all-to-all-start = ((s32[32,128,3]{1,2,0:T(4,128)}), s32[32,128,3]{1,2,0:T(4,128)S(1)}, u32[]{:S(2)}, u32[]{:S(2)}) async-start(s32[32,128,3]{1,2,0:T(4,128)} %broadcast_in_dim.216), calls=%async_computation | async-start | bytes 131072 | tf_op jit(solution)/shard_map/all_to_all | solution.py:147
  10.3 0.7 and_select_fusion.4
  10.9 1.0 fusion.25
  11.9 1.1 sine_multiply_fusion
  13.0 0.7 convert_log-plus-one_fusion
  14.0 0.8 fusion.72
  14.9 0.9 fusion.2.forward_ref
  15.7 0.9 broadcast_in_dim_tile.4.wrow_ref
  16.7 1.1 all-to-all-done
  17.8 0.7 select_reduce_fusion.1
  18.9 0.7 fusion.57
  20.2 0.3 reduce-window.76
  20.5 0.3 reduce-window.74
  21.3 0.3 reduce-window.56
  22.1 0.3 reduce-window.54
  23.9 0.6 compare_and_fusion.5
  24.6 1.3 fusion.49
  26.0 0.7 select_reduce_fusion.4
  26.7 0.6 compare_select_fusion
  27.7 0.8 select_reduce_fusion.6
  28.5 0.6 add_select_fusion.2
  29.1 23.7 %shard_map.86 = (f32[256,512]{1,0:T(8,128)}, bf16[8192,512]{1,0:T(8,128)(2,1)}, bf16[4096,512]{1,0:T(8,128)(2,1)}) custom-call(s32[1]{0:T(128)} %bitcast.9.count_ref, s32[256]{0:T(256)} %get-tuple-element.81.ent_p_ref, s32[256]{0:T(256)} %get-tuple-element.29.ent_k_ref, bf16[8192,512]{1,0:T(8,128)(2,1)} %bitcast.101, bf16[4096,512]{1,0:T(8,128)(2,1)} %bitcast.106, ...), custom_call_target="tpu_custom_call" | custom-call | tf_op jit(solution)/shard_map/pallas_call | solution.py:175
  52.8 1.6 %fusion.76 = f32[256,36]{1,0:T(8,128)S(1)} fusion(f32[256,512]{1,0:T(8,128)} %get-tuple-element.19, f32[36,512]{1,0:T(8,128)S(1)} %copy-done.7), kind=kOutput, calls=%fused_computation.228 | convolution fusion | flops 56623104 | bytes 634880 | tf_op jit(solution)/shard_map/dot_general | solution.py:196
  54.4 0.6 compare_and_fusion.4
  55.0 0.7 gather_fusion
  57.0 10.3 %all-gather.1 = f32[4,2,128]{2,1,0:T(2,128)S(1)} all-gather(f32[1,2,128]{2,1,0:T(2,128)S(1)} %maximum_bitcast_fusion), channel_id=2, replica_groups=mesh['dp'=32,'cls'=4] {'cls'}, dimensions={0}, use_global_device_ids=true | all-gather | bytes 5120 | tf_op jit(solution)/shard_map/all_gather | solution.py:204
  67.9 0.3 fusion.19
  68.2 1.0 fusion.11
  70.1 0.6 dynamic_update_slice.6
  70.8 4.6 %constant_dynamic-slice_fusion.1 = (bf16[16,1,128,512]{3,2,1,0:T(8,128)(2,1)}, bf16[16,1,128,512]{3,2,1,0:T(8,128)(2,1)}) fusion(bf16[16,2,128,512]{3,2,1,0:T(8,128)(2,1)} %bitcast.107, s32[]{:T(128)S(6)} %select_n.283, s32[]{:T(128)S(6)} %select_n.294), kind=kLoop, calls=%fused_computation.166 | loop fusion | bytes 8388616 | tf_op jit(solution)/shard_map/jit(dynamic_index_in_dim)/dynamic_slice | solution.py:250
  75.4 0.7 dynamic-slice_bitcast_fusion.1
  76.3 0.7 reshape.739.volume_ref
  76.9 1.0 gather_fusion.2
  77.9 1.0 broadcast_select_fusion.coef_ref
  78.9 7.6 %shard_map.88 = bf16[2048,512]{1,0:T(8,128)(2,1)} custom-call(s32[1]{0:T(128)} %bitcast.36.count_ref, s32[256]{0:T(256)} %get-tuple-element.71.ent_p_ref, s32[256]{0:T(256)} %get-tuple-element.27.ent_k_ref, bf16[8192,512]{1,0:T(8,128)(2,1)} %get-tuple-element.18.image_hat_ref, f32[256,512]{1,0:T(8,128)} %broadcast_select_fusion.coef_ref, ...), custom_call_target="tpu_custom_call" | custom-call | tf_op jit(solution)/shard_map/pallas_call | solution.py:252
  86.5 3.3 %pad_maximum_fusion = bf16[16,144,512]{2,1,0:T(8,128)(2,1)} fusion(bf16[16,16,512]{2,1,0:T(8,128)(2,1)S(1)} %get-tuple-element.53, bf16[16,128,512]{2,1,0:T(8,128)(2,1)} %bitcast.105), kind=kLoop, calls=%fused_computation.5 | loop fusion | flops 4718592 | bytes 4718592 | tf_op jit(solution)/shard_map/concatenate | solution.py:285
  89.8 2.7 %collective-permute-start = (bf16[16,144,512]{2,1,0:T(8,128)(2,1)}, bf16[16,144,512]{2,1,0:T(8,128)(2,1)S(1)}, u32[]{:S(2)}, u32[]{:S(2)}) collective-permute-start(bf16[16,144,512]{2,1,0:T(8,128)(2,1)} %pad_maximum_fusion), channel_id=1, source_target_pairs={{0,4},{4,0},{8,12},{12,8},{16,20},{20,16},{24,28},{28,24},{32,36},... | collective-permute-start | bytes 7077896 | tf_op jit(solution)/shard_map/ppermute | solution.py:292
  92.5 0.7 reshape.731.volume_ref
  93.1 0.6 add_select_fusion.3
  93.7 1.0 gather_fusion.1
  94.7 0.9 broadcast_select_fusion.1.coef_ref
  95.6 7.9 %shard_map.87 = bf16[2048,512]{1,0:T(8,128)(2,1)} custom-call(s32[1]{0:T(128)} %bitcast.6.count_ref, s32[256]{0:T(256)} %get-tuple-element.69.ent_p_ref, s32[256]{0:T(256)} %get-tuple-element.25.ent_k_ref, bf16[8192,512]{1,0:T(8,128)(2,1)} %get-tuple-element.18.image_hat_ref, f32[256,512]{1,0:T(8,128)} %broadcast_select_fusion.1.coef_ref, ...), custom_call_target="tpu_custom_call" | custom-call | tf_op jit(solution)/shard_map/pallas_call | solution.py:252
  103.5 2.3 %add_convert_fusion = bf16[16,144,512]{2,1,0:T(8,128)(2,1)S(1)} fusion(bf16[16,144,512]{2,1,0:T(8,128)(2,1)S(1)} %collective-permute-done, bf16[16,16,512]{2,1,0:T(8,128)(2,1)S(1)} %copy-done, bf16[16,128,512]{2,1,0:T(8,128)(2,1)} %bitcast.104), kind=kLoop, calls=%fused_computation.3 | loop fusion | flops 8257536 | bytes 7077888 | tf_op jit(solution)/shard_map/convert_element_type | solution.py:301
  105.8 36.8 %all_to_all.10 = bf16[16,144,512]{2,1,0:T(8,128)(2,1)S(1)} all-to-all(bf16[16,144,512]{2,1,0:T(8,128)(2,1)S(1)} %add_convert_fusion), channel_id=1, replica_groups={{0,8,16,24,32,40,48,56,64,72,80,88,96,104,112,120},{4,12,20,28,36,44,52..., dimensions={0} | all-to-all | bytes 4718592 | tf_op jit(solution)/shard_map/all_to_all | solution.py:303
  143.7 1.9 %fusion = f32[1,2,64,512]{3,2,1,0:T(8,128)} fusion(f32[2,64,512]{2,1,0:T(8,128)S(1)} %bitcast.109, f32[256,256]{1,0:T(8,128)S(1)} %copy-done.6, f32[256,256]{1,0:T(8,128)S(1)} %copy-done.4, f32[256,256]{1,0:T(8,128)S(1)} %copy-done.2, f32[2]{0:T(128)S(1)} %broadcast_add_fusion.2), kind=kOutput, calls=%fused_computation.10 | convolution fusion | flops 403505152 | bytes 1310728 | tf_op jit(solution)/shard_map/dot_general | solution.py:307
  145.6 0.6 select_reduce_fusion.9
  (113 shorter events, 8.4 us)
Async XLA Ops:
  0.6 17.2 %copy-start.8 = (s32[128]{0:T(128)S(1)}, s32[128]{0:T(128)}, u32[]{:S(2)}) copy-start(s32[128]{0:T(128)} %param.12) | copy-start | bytes 1540
  0.6 15.1 %copy-start.9 = (f32[64]{0:T(128)S(1)}, f32[64]{0:T(128)}, u32[]{:S(2)}) copy-start(f32[64]{0:T(128)} %param.15) | copy-start | bytes 772
  2.0 15.8 %all-to-all-start = ((s32[32,128,3]{1,2,0:T(4,128)}), s32[32,128,3]{1,2,0:T(4,128)S(1)}, u32[]{:S(2)}, u32[]{:S(2)}) async-start(s32[32,128,3]{1,2,0:T(4,128)} %broadcast_in_dim.216), calls=%async_computation | async-start | bytes 131072 | tf_op jit(solution)/shard_map/all_to_all | solution.py:147
  11.9 40.9 %copy-start.1 = (f32[256,256]{1,0:T(8,128)}, f32[256,256]{1,0:T(8,128)S(1)}, u32[]{:S(2)}) copy-start(f32[256,256]{1,0:T(8,128)S(1)} %fusion.25) | copy-start | bytes 786436
  13.0 39.8 %copy-start.3 = (f32[256,256]{1,0:T(8,128)}, f32[256,256]{1,0:T(8,128)S(1)}, u32[]{:S(2)}) copy-start(f32[256,256]{1,0:T(8,128)S(1)} %get-tuple-element.82) | copy-start | bytes 786436
  13.0 39.8 %copy-start.5 = (f32[256,256]{1,0:T(8,128)}, f32[256,256]{1,0:T(8,128)S(1)}, u32[]{:S(2)}) copy-start(f32[256,256]{1,0:T(8,128)S(1)} %get-tuple-element.83) | copy-start | bytes 786436
  29.1 23.7 %copy-start.7 = (f32[36,512]{1,0:T(8,128)S(1)}, f32[36,512]{1,0:T(8,128)}, u32[]{:S(2)}) copy-start(f32[36,512]{1,0:T(8,128)} %param.14) | copy-start | bytes 221188
  89.8 13.7 %collective-permute-start = (bf16[16,144,512]{2,1,0:T(8,128)(2,1)}, bf16[16,144,512]{2,1,0:T(8,128)(2,1)S(1)}, u32[]{:S(2)}, u32[]{:S(2)}) collective-permute-start(bf16[16,144,512]{2,1,0:T(8,128)(2,1)} %pad_maximum_fusion), channel_id=1, source_target_pairs={{0,4},{4,0},{8,12},{12,8},{16,20},{20,16},{24,28},{28,24},{32,36},... | collective-permute-start | bytes 7077896 | tf_op jit(solution)/shard_map/ppermute | solution.py:292
  95.6 7.9 %copy-start = (bf16[16,16,512]{2,1,0:T(8,128)(2,1)S(1)}, bf16[16,16,512]{2,1,0:T(8,128)(2,1)}, u32[]{:S(2)}) copy-start(bf16[16,16,512]{2,1,0:T(8,128)(2,1)} %get-tuple-element.52) | copy-start | bytes 786436
  142.6 1.0 copy-start.2
  142.6 1.0 copy-start.4
  142.6 1.1 copy-start.6

commit v9 on v7

--- a/solution.py
+++ b/solution.py
@@ -31,36 +31,54 @@
 
 
 def cross_kernel(
-    count_ref, ent_p_ref, ent_k_ref, image_ref, refs_ref, forward_ref, wrow_ref,
-    cross_ref, image_hat_ref, ref_hat_ref, weighted_ref,
+    count_ref, ent_p_ref, ent_k_ref, image_hbm, refs_hbm, forward_ref, wrow_ref,
+    cross_ref, image_hat_hbm, ref_hat_hbm,
+    image_buf, refs_buf, hat_buf, ref_hat_buf, weighted_ref, in_sem, out_sem,
 ):
+    n_image = image_buf.shape[0] // CHUNK
+    n_ref = refs_buf.shape[0] // CHUNK
+
+    def rows(c):
+        return pl.ds(c * CHUNK, CHUNK)
+
+    loads = []
+    for c in range(n_ref):
+        copy = pltpu.make_async_copy(refs_hbm.at[rows(c)], refs_buf.at[rows(c)], in_sem.at[c])
+        copy.start()
+        loads.append(copy)
+    for c in range(n_image):
+        copy = pltpu.make_async_copy(
+            image_hbm.at[rows(c)], image_buf.at[rows(c)], in_sem.at[n_ref + c]
+        )
+        copy.start()
+        loads.append(copy)
     forward = forward_ref[...]
     wrow = wrow_ref[...]
-
-    def image_dft(c, carry):
-        r = pl.multiple_of(c * CHUNK, CHUNK)
-        image_hat_ref[pl.ds(r, CHUNK), :] = jnp.dot(
-            image_ref[pl.ds(r, CHUNK), :], forward, preferred_element_type=F32
+    stores = []
+    for c in range(n_ref):
+        loads[c].wait()
+        hat = jnp.dot(refs_buf[rows(c)], forward, preferred_element_type=F32).astype(jnp.bfloat16)
+        ref_hat_buf[rows(c)] = hat
+        weighted_ref[rows(c)] = (hat.astype(F32) * wrow).astype(jnp.bfloat16)
+        copy = pltpu.make_async_copy(ref_hat_buf.at[rows(c)], ref_hat_hbm.at[rows(c)], out_sem.at[c])
+        copy.start()
+        stores.append(copy)
+    for c in range(n_image):
+        loads[n_ref + c].wait()
+        hat_buf[rows(c)] = jnp.dot(
+            image_buf[rows(c)], forward, preferred_element_type=F32
         ).astype(jnp.bfloat16)
-        return carry
-
-    def ref_dft(c, carry):
-        r = pl.multiple_of(c * CHUNK, CHUNK)
-        hat = jnp.dot(
-            refs_ref[pl.ds(r, CHUNK), :], forward, preferred_element_type=F32
-        ).astype(jnp.bfloat16)
-        ref_hat_ref[pl.ds(r, CHUNK), :] = hat
-        weighted_ref[pl.ds(r, CHUNK), :] = (hat.astype(F32) * wrow).astype(jnp.bfloat16)
-        return carry
-
-    lax.fori_loop(0, image_ref.shape[0] // CHUNK, image_dft, 0)
-    lax.fori_loop(0, refs_ref.shape[0] // CHUNK, ref_dft, 0)
+        copy = pltpu.make_async_copy(
+            hat_buf.at[rows(c)], image_hat_hbm.at[rows(c)], out_sem.at[n_ref + c]
+        )
+        copy.start()
+        stores.append(copy)
     cross_ref[...] = jnp.zeros_like(cross_ref)
 
     def body(e, carry):
         rp = pl.multiple_of(ent_p_ref[e] * NSHELL, NSHELL)
         rk = pl.multiple_of(ent_k_ref[e] * NSHELL, NSHELL)
-        x = image_hat_ref[pl.ds(rp, NSHELL), :].astype(F32)
+        x = hat_buf[pl.ds(rp, NSHELL), :].astype(F32)
         w = weighted_ref[pl.ds(rk, NSHELL), :].astype(F32)
         x_re = x[:, :NANG]
         x_im = x[:, NANG:]
@@ -72,6 +90,8 @@
         return carry
 
     lax.fori_loop(0, count_ref[0], body, 0)
+    for copy in stores:
+        copy.wait()
 
 
 def grad_kernel(
@@ -172,6 +192,7 @@
     ref_rows = col_classes * NSHELL
     wrow = jnp.tile(shell_weight, CHUNK // NSHELL)[:, None]
     params = pltpu.CompilerParams(vmem_limit_bytes=60 * 1024 * 1024)
+    anywhere = pl.BlockSpec(memory_space=pl.MemorySpace.ANY)
     cross_c, image_hat, ref_hat = pl.pallas_call(
         cross_kernel,
         out_shape=(
@@ -179,9 +200,17 @@
             jax.ShapeDtypeStruct((image_rows, row_width), jnp.bfloat16),
             jax.ShapeDtypeStruct((ref_rows, row_width), jnp.bfloat16),
         ),
-        in_specs=[smem(), smem(), smem(), vmem(), vmem(), vmem(), vmem()],
-        out_specs=(vmem(), vmem(), vmem()),
-        scratch_shapes=[pltpu.VMEM((ref_rows, row_width), jnp.bfloat16)],
+        in_specs=[smem(), smem(), smem(), anywhere, anywhere, vmem(), vmem()],
+        out_specs=(vmem(), anywhere, anywhere),
+        scratch_shapes=[
+            pltpu.VMEM((image_rows, row_width), jnp.bfloat16),
+            pltpu.VMEM((ref_rows, row_width), jnp.bfloat16),
+            pltpu.VMEM((image_rows, row_width), jnp.bfloat16),
+            pltpu.VMEM((ref_rows, row_width), jnp.bfloat16),
+            pltpu.VMEM((ref_rows, row_width), jnp.bfloat16),
+            pltpu.SemaphoreType.DMA(((image_rows + ref_rows) // CHUNK,)),
+            pltpu.SemaphoreType.DMA(((image_rows + ref_rows) // CHUNK,)),
+        ],
         compiler_params=params,
     )(
         count_arr, ent_p, ent_k, images.reshape(image_rows, row_width),

time: 133 us -> 127 us (0.955)
  Pallas kernels: 34.7 us -> 29 us
    pallas_call x1, Pallas kernels: 24 us -> 18.1 us  [local(): pl.pallas_call(cross_kernel, out_shape=(jax.ShapeDtypeStruct((entries, ro...]
where the time goes in v9:
time: 127 us; the launch traced here: 126 us
  blocking collectives  46.6 us (37%)
  Pallas kernels  29 us (23%)
  other arithmetic  20.6 us (16%)
  starting transfers between devices  11 us (9%)
  local copies, waits for them, and re-layouts  7.96 us (6%)
  waiting for transfers between devices  5.46 us (4%)
  matrix products  4.78 us (4%)
    all_to_all x1, blocking collectives, local(): lax.all_to_all(pair_sum, 'dp', split_axis=0, concat_axis=0, tiled=True, a...  37.2 us
    pallas_call x1, Pallas kernels, local(): pl.pallas_call(cross_kernel, out_shape=(jax.ShapeDtypeStruct((entries, ro...  18.1 us
    pallas_call x1, Pallas kernels, local(): pl.pallas_call(grad_kernel, out_shape=jax.ShapeDtypeStruct((ref_rows, row...  10.8 us
    all_gather x1, blocking collectives, local(): gathered = lax.all_gather(jnp.stack([top_local, total_local]), 'cls')  9.43 us
    all_to_all x1, starting transfers between devices, local(): lax.all_to_all(jnp.broadcast_to(packed[None], (dp_count,) + packed.shape)...  8.25 us
    ppermute x1, waiting for transfers between devices, local(): taken = lax.ppermute(give, 'dp', perm=[(i, i ^ 1) for i in range(dp_count)])  4.29 us
    convert_element_type x1, other arithmetic, local(): pair_sum = (keep.astype(F32) + taken.astype(F32)).astype(jnp.bfloat16)  3.04 us
    ppermute x1, starting transfers between devices, local(): taken = lax.ppermute(give, 'dp', perm=[(i, i ^ 1) for i in range(dp_count)])  2.74 us
  transfers between devices with their start and end apart: 2, of which 2 were waited for; matrix products, arithmetic and copies ran while one was open for 5% of the time, Pallas kernels for 0%

profile of v9, /device:TPU:0, one launch (start us, length us, event | category | flops | bytes accessed | tf_op | source)
XLA Modules:
  0.0 126.3 jit_solution(9032261096755776240)
XLA Ops:
  0.7 0.7 pad_add_fusion
  1.4 0.6 broadcast_in_dim.187
  2.0 8.2 %all-to-all-start = ((s32[32,128,3]{1,2,0:T(4,128)}), s32[32,128,3]{1,2,0:T(4,128)S(1)}, u32[]{:S(2)}, u32[]{:S(2)}) async-start(s32[32,128,3]{1,2,0:T(4,128)} %broadcast_in_dim.187), calls=%async_computation | async-start | bytes 131072 | tf_op jit(solution)/shard_map/all_to_all | solution.py:167
  10.3 1.1 sine_multiply_fusion
  11.3 1.0 fusion.30
  12.3 0.7 and_select_fusion.3
  13.0 0.8 fusion.66
  13.8 0.7 convert_log-plus-one_fusion
  14.5 0.3 reduce_window_sum.82
  14.8 0.9 fusion.7.forward_ref
  15.7 0.9 broadcast_in_dim_tile.4.wrow_ref
  16.6 1.2 all-to-all-done
  17.8 0.6 select_reduce_fusion.1
  18.8 0.3 reduce-window.16
  19.1 0.6 convert_reduce_fusion.1
  20.1 0.3 reduce-window.24
  21.0 0.7 compare_and_fusion.2
  21.7 0.7 select_reduce_fusion.2
  22.4 0.6 and_select_fusion.4.ent_p_ref
  23.0 18.1 %shard_map.86 = (f32[256,512]{1,0:T(8,128)}, bf16[8192,512]{1,0:T(8,128)(2,1)}, bf16[4096,512]{1,0:T(8,128)(2,1)}) custom-call(s32[1]{0:T(128)} %bitcast.6.count_ref, s32[256]{0:T(256)} %and_select_fusion.4.ent_p_ref, s32[256]{0:T(256)} %get-tuple-element.22.ent_k_ref, bf16[8192,512]{1,0:T(8,128)(2,1)} %bitcast.86, bf16[4096,512]{1,0:T(8,128)(2,1)} %bitcast.89, ...), custom_call_target="tpu_custom_call" | custom-call | tf_op jit(solution)/shard_map/pallas_call | solution.py:196
  41.2 1.6 %fusion.69 = f32[256,36]{1,0:T(8,128)S(1)} fusion(f32[256,512]{1,0:T(8,128)} %get-tuple-element.18, f32[36,512]{1,0:T(8,128)S(1)} %copy-done.2), kind=kOutput, calls=%fused_computation.157 | convolution fusion | flops 56623104 | bytes 634880 | tf_op jit(solution)/shard_map/dot_general | solution.py:225
  43.0 0.7 compare_select_fusion
  44.3 0.2 reshape.483
  44.5 0.7 gather_fusion
  45.2 0.7 compare_and_fusion.1
  45.9 0.2 fusion.31
  46.5 0.2 sub.202
  46.6 0.3 select_reduce_fusion.4
  47.2 9.4 %all-gather.1 = f32[4,2,128]{2,1,0:T(2,128)S(1)} all-gather(f32[1,2,128]{2,1,0:T(2,128)S(1)} %maximum_bitcast_fusion), channel_id=2, replica_groups=mesh['dp'=32,'cls'=4] {'cls'}, dimensions={0}, use_global_device_ids=true | all-gather | bytes 5120 | tf_op jit(solution)/shard_map/all_gather | solution.py:233
  56.8 0.2 div.62
  57.0 0.2 sub.206
  57.5 0.3 fusion.24
  57.8 1.0 fusion.16
  58.8 0.2 fusion.11
  59.0 1.1 gather_fusion.1
  60.1 0.7 pad_maximum_fusion.volume_ref
  61.4 0.6 dynamic_update_slice.6
  62.1 0.9 slice_select_fusion.coef_ref
  63.0 10.8 %shard_map.87 = bf16[4096,512]{1,0:T(8,128)(2,1)} custom-call(s32[1]{0:T(128)} %bitcast.6.count_ref, s32[256]{0:T(256)} %and_select_fusion.4.ent_p_ref, s32[256]{0:T(256)} %get-tuple-element.22.ent_k_ref, bf16[8192,512]{1,0:T(8,128)(2,1)} %get-tuple-element.17.image_hat_ref, f32[256,512]{1,0:T(8,128)} %slice_select_fusion.coef_ref, ...), custom_call_target="tpu_custom_call" | custom-call | tf_op jit(solution)/shard_map/pallas_call | solution.py:257
  73.8 1.8 %fusion.2 = bf16[16,144,512]{2,1,0:T(8,128)(2,1)S(1)} fusion(s32[]{:T(128)S(6)} %select_n.198, bf16[16,2,128,512]{3,2,1,0:T(8,128)(2,1)} %bitcast.84, bf16[16,2,16,512]{3,2,1,0:T(8,128)(2,1)S(1)} %bitcast.87), kind=kLoop, calls=%fused_computation.10 | loop fusion | flops 4718592 | bytes 7077892 | tf_op jit(solution)/shard_map/jit(dynamic_index_in_dim)/squeeze | solution.py:294
  75.6 2.7 %collective-permute-start = (bf16[16,144,512]{2,1,0:T(8,128)(2,1)S(1)}, bf16[16,144,512]{2,1,0:T(8,128)(2,1)}, u32[]{:S(2)}, u32[]{:S(2)}) collective-permute-start(bf16[16,144,512]{2,1,0:T(8,128)(2,1)S(1)} %fusion.2), channel_id=1, source_target_pairs={{0,4},{4,0},{8,12},{12,8},{16,20},{20,16},{24,28},{28,24},{32,36},... | collective-permute-start | bytes 7077896 | tf_op jit(solution)/shard_map/ppermute | solution.py:295
  78.4 4.3 %collective-permute-done = bf16[16,144,512]{2,1,0:T(8,128)(2,1)} collective-permute-done((bf16[16,144,512]{2,1,0:T(8,128)(2,1)S(1)}, bf16[16,144,512]{2,1,0:T(8,128)(2,1)}, u32[]{:S(2)}, u32[]{:S(2)}) %collective-permute-start) | collective-permute-done | bytes 2359328 | tf_op jit(solution)/shard_map/ppermute | solution.py:295
  82.7 3.0 %fusion = bf16[16,144,512]{2,1,0:T(8,128)(2,1)S(1)} fusion(bf16[16,144,512]{2,1,0:T(8,128)(2,1)} %collective-permute-done, s32[]{:T(128)S(6)} %select_n.197, bf16[16,2,128,512]{3,2,1,0:T(8,128)(2,1)} %bitcast.85, bf16[16,2,16,512]{3,2,1,0:T(8,128)(2,1)S(1)} %bitcast.88), kind=kLoop, calls=%fused_computation.5 | loop fusion | flops 9437184 | bytes 9437188 | tf_op jit(solution)/shard_map/convert_element_type | solution.py:296
  85.7 37.2 %all_to_all.10 = bf16[16,144,512]{2,1,0:T(8,128)(2,1)S(1)} all-to-all(bf16[16,144,512]{2,1,0:T(8,128)(2,1)S(1)} %fusion), channel_id=1, replica_groups={{0,8,16,24,32,40,48,56,64,72,80,88,96,104,112,120},{4,12,20,28,36,44,52..., dimensions={0} | all-to-all | bytes 4718592 | tf_op jit(solution)/shard_map/all_to_all | solution.py:298
  123.4 0.3 convert_reduce_fusion
  123.7 0.2 copy-done.1
  123.8 1.9 %fusion.5 = f32[1,2,64,512]{3,2,1,0:T(8,128)} fusion(f32[2,64,512]{2,1,0:T(8,128)S(1)} %bitcast.90, f32[256,256]{1,0:T(8,128)S(1)} %get-tuple-element.55, f32[256,256]{1,0:T(8,128)S(1)} %get-tuple-element.54, f32[256,256]{1,0:T(8,128)S(1)} %copy-done.1, f32[2]{0:T(128)S(1)} %broadcast_add_fusion.2), kind=kOutput, calls=%fused_computation.17 | convolution fusion | flops 403505152 | bytes 1310728 | tf_op jit(solution)/shard_map/dot_general | solution.py:302
  125.7 0.6 select_reduce_fusion.5
  (72 shorter events, 4.5 us)
Async XLA Ops:
  0.6 17.2 %copy-start.3 = (s32[128]{0:T(128)S(1)}, s32[128]{0:T(128)}, u32[]{:S(2)}) copy-start(s32[128]{0:T(128)} %param.10) | copy-start | bytes 1540
  0.6 15.1 %copy-start.4 = (f32[64]{0:T(128)S(1)}, f32[64]{0:T(128)}, u32[]{:S(2)}) copy-start(f32[64]{0:T(128)} %param.13) | copy-start | bytes 772
  2.0 15.8 %all-to-all-start = ((s32[32,128,3]{1,2,0:T(4,128)}), s32[32,128,3]{1,2,0:T(4,128)S(1)}, u32[]{:S(2)}, u32[]{:S(2)}) async-start(s32[32,128,3]{1,2,0:T(4,128)} %broadcast_in_dim.187), calls=%async_computation | async-start | bytes 131072 | tf_op jit(solution)/shard_map/all_to_all | solution.py:167
  12.3 28.9 %copy-start = (f32[256,256]{1,0:T(8,128)}, f32[256,256]{1,0:T(8,128)S(1)}, u32[]{:S(2)}) copy-start(f32[256,256]{1,0:T(8,128)S(1)} %fusion.30) | copy-start | bytes 786436
  23.0 18.2 %copy-start.2 = (f32[36,512]{1,0:T(8,128)S(1)}, f32[36,512]{1,0:T(8,128)}, u32[]{:S(2)}) copy-start(f32[36,512]{1,0:T(8,128)} %param.12) | copy-start | bytes 221188
  75.6 7.0 %collective-permute-start = (bf16[16,144,512]{2,1,0:T(8,128)(2,1)S(1)}, bf16[16,144,512]{2,1,0:T(8,128)(2,1)}, u32[]{:S(2)}, u32[]{:S(2)}) collective-permute-start(bf16[16,144,512]{2,1,0:T(8,128)(2,1)S(1)} %fusion.2), channel_id=1, source_target_pairs={{0,4},{4,0},{8,12},{12,8},{16,20},{20,16},{24,28},{28,24},{32,36},... | collective-permute-start | bytes 7077896 | tf_op jit(solution)/shard_map/ppermute | solution.py:295
  122.9 1.0 copy-start.1

commit v10 on v9

--- a/solution.py
+++ b/solution.py
@@ -95,22 +95,47 @@
 
 
 def grad_kernel(
-    count_ref, ent_p_ref, ent_k_ref, image_hat_ref, coef_ref, ref_hat_ref, volume_ref,
-    out_ref, acc_ref,
+    count_ref, ent_p_ref, ent_k_ref, image_hat_hbm, coef_ref, ref_hat_hbm, volume_ref,
+    out_hbm, image_buf, ref_buf, acc_ref, out_buf, in_sem, out_sem,
 ):
-    def init(k, carry):
-        r = pl.multiple_of(k * NSHELL, NSHELL)
-        acc_ref[pl.ds(r, NSHELL), :] = -volume_ref[pl.ds(k, 1), :] * ref_hat_ref[
-            pl.ds(r, NSHELL), :
-        ].astype(F32)
-        return carry
-
-    lax.fori_loop(0, volume_ref.shape[0], init, 0)
+    n_image = image_buf.shape[0] // CHUNK
+    n_ref = ref_buf.shape[0] // CHUNK
+    chunk_classes = CHUNK // NSHELL
+
+    def rows(c):
+        return pl.ds(c * CHUNK, CHUNK)
+
+    loads = []
+    for c in range(n_ref):
+        copy = pltpu.make_async_copy(ref_hat_hbm.at[rows(c)], ref_buf.at[rows(c)], in_sem.at[c])
+        copy.start()
+        loads.append(copy)
+    for c in range(n_image):
+        copy = pltpu.make_async_copy(
+            image_hat_hbm.at[rows(c)], image_buf.at[rows(c)], in_sem.at[n_ref + c]
+        )
+        copy.start()
+        loads.append(copy)
+
+    for c in range(n_ref):
+        loads[c].wait()
+
+        def init(i, carry, c=c):
+            k = c * chunk_classes + i
+            r = pl.multiple_of(k * NSHELL, NSHELL)
+            acc_ref[pl.ds(r, NSHELL), :] = -volume_ref[pl.ds(k, 1), :] * ref_buf[
+                pl.ds(r, NSHELL), :
+            ].astype(F32)
+            return carry
+
+        lax.fori_loop(0, chunk_classes, init, 0)
+    for c in range(n_image):
+        loads[n_ref + c].wait()
 
     def body(e, carry):
         rp = pl.multiple_of(ent_p_ref[e] * NSHELL, NSHELL)
         rk = pl.multiple_of(ent_k_ref[e] * NSHELL, NSHELL)
-        x = image_hat_ref[pl.ds(rp, NSHELL), :].astype(F32)
+        x = image_buf[pl.ds(rp, NSHELL), :].astype(F32)
         c = coef_ref[pl.ds(e, 1), :]
         c_re = c[:, :NANG]
         c_im = c[:, NANG:]
@@ -125,12 +150,14 @@
 
     lax.fori_loop(0, count_ref[0], body, 0)
 
-    def finish(c, carry):
-        r = pl.multiple_of(c * CHUNK, CHUNK)
-        out_ref[pl.ds(r, CHUNK), :] = acc_ref[pl.ds(r, CHUNK), :].astype(jnp.bfloat16)
-        return carry
-
-    lax.fori_loop(0, acc_ref.shape[0] // CHUNK, finish, 0)
+    stores = []
+    for c in range(n_ref):
+        out_buf[rows(c)] = acc_ref[rows(c)].astype(jnp.bfloat16)
+        copy = pltpu.make_async_copy(out_buf.at[rows(c)], out_hbm.at[rows(c)], out_sem.at[c])
+        copy.start()
+        stores.append(copy)
+    for copy in stores:
+        copy.wait()
 
 
 def split_pair(x):
@@ -257,9 +284,16 @@
     numer = pl.pallas_call(
         grad_kernel,
         out_shape=jax.ShapeDtypeStruct((ref_rows, row_width), jnp.bfloat16),
-        in_specs=[smem(), smem(), smem(), vmem(), vmem(), vmem(), vmem()],
-        out_specs=vmem(),
-        scratch_shapes=[pltpu.VMEM((ref_rows, row_width), F32)],
+        in_specs=[smem(), smem(), smem(), anywhere, vmem(), anywhere, vmem()],
+        out_specs=anywhere,
+        scratch_shapes=[
+            pltpu.VMEM((image_rows, row_width), jnp.bfloat16),
+            pltpu.VMEM((ref_rows, row_width), jnp.bfloat16),
+            pltpu.VMEM((ref_rows, row_width), F32),
+            pltpu.VMEM((ref_rows, row_width), jnp.bfloat16),
+            pltpu.SemaphoreType.DMA(((image_rows + ref_rows) // CHUNK,)),
+            pltpu.SemaphoreType.DMA((ref_rows // CHUNK,)),
+        ],
         compiler_params=params,
     )(count_arr, ent_p, ent_k, image_hat, coef_c[:, :row_width], ref_hat, volume_full)
 

time: 127 us -> 127 us (level)
  blocking collectives: 46.6 us -> 48 us
where the time goes in v10:
time: 127 us
  blocking collectives  48 us (38%)
  Pallas kernels  27.8 us (22%)
  other arithmetic  20.6 us (16%)
  starting transfers between devices  10.9 us (9%)
  local copies, waits for them, and re-layouts  7.96 us (6%)
  waiting for transfers between devices  5.46 us (4%)
  matrix products  4.78 us (4%)
    all_to_all x1, blocking collectives, local(): lax.all_to_all(pair_sum, 'dp', split_axis=0, concat_axis=0, tiled=True, a...  38 us
    pallas_call x1, Pallas kernels, local(): pl.pallas_call(cross_kernel, out_shape=(jax.ShapeDtypeStruct((entries, ro...  17.5 us
    pallas_call x1, Pallas kernels, local(): pl.pallas_call(grad_kernel, out_shape=jax.ShapeDtypeStruct((ref_rows, row...  10.3 us
    all_gather x1, blocking collectives, local(): gathered = lax.all_gather(jnp.stack([top_local, total_local]), 'cls')  10 us
    all_to_all x1, starting transfers between devices, local(): lax.all_to_all(jnp.broadcast_to(packed[None], (dp_count,) + packed.shape)...  8.25 us
    ppermute x1, waiting for transfers between devices, local(): taken = lax.ppermute(give, 'dp', perm=[(i, i ^ 1) for i in range(dp_count)])  4.29 us
    convert_element_type x1, other arithmetic, local(): pair_sum = (keep.astype(F32) + taken.astype(F32)).astype(jnp.bfloat16)  3.04 us
    ppermute x1, starting transfers between devices, local(): taken = lax.ppermute(give, 'dp', perm=[(i, i ^ 1) for i in range(dp_count)])  2.67 us
  transfers between devices with their start and end apart: 2, of which 2 were waited for; matrix products, arithmetic and copies ran while one was open for 5% of the time, Pallas kernels for 0%

profile of v10, /device:TPU:0, one launch (start us, length us, event | category | flops | bytes accessed | tf_op | source)
XLA Modules:
  0.0 126.5 jit_solution(15373873036209128009)
XLA Ops:
  0.7 0.7 pad_add_fusion
  1.4 0.6 broadcast_in_dim.187
  2.0 8.2 %all-to-all-start = ((s32[32,128,3]{1,2,0:T(4,128)}), s32[32,128,3]{1,2,0:T(4,128)S(1)}, u32[]{:S(2)}, u32[]{:S(2)}) async-start(s32[32,128,3]{1,2,0:T(4,128)} %broadcast_in_dim.187), calls=%async_computation | async-start | bytes 131072 | tf_op jit(solution)/shard_map/all_to_all | solution.py:194
  10.3 1.1 sine_multiply_fusion
  11.3 1.0 fusion.30
  12.3 0.7 and_select_fusion.3
  13.0 0.8 fusion.66
  13.8 0.7 convert_log-plus-one_fusion
  14.5 0.3 reduce_window_sum.82
  14.8 0.9 fusion.7.forward_ref
  15.7 0.9 broadcast_in_dim_tile.4.wrow_ref
  16.6 1.2 all-to-all-done
  17.8 0.6 select_reduce_fusion.1
  18.8 0.3 reduce-window.16
  19.1 0.6 convert_reduce_fusion.1
  20.1 0.3 reduce-window.24
  21.0 0.7 compare_and_fusion.2
  21.7 0.7 select_reduce_fusion.2
  22.4 0.6 and_select_fusion.4.ent_p_ref
  23.0 17.5 %shard_map.86 = (f32[256,512]{1,0:T(8,128)}, bf16[8192,512]{1,0:T(8,128)(2,1)}, bf16[4096,512]{1,0:T(8,128)(2,1)}) custom-call(s32[1]{0:T(128)} %bitcast.6.count_ref, s32[256]{0:T(256)} %and_select_fusion.4.ent_p_ref, s32[256]{0:T(256)} %get-tuple-element.22.ent_k_ref, bf16[8192,512]{1,0:T(8,128)(2,1)} %bitcast.86, bf16[4096,512]{1,0:T(8,128)(2,1)} %bitcast.89, ...), custom_call_target="tpu_custom_call" | custom-call | tf_op jit(solution)/shard_map/pallas_call | solution.py:223
  40.6 1.6 %fusion.69 = f32[256,36]{1,0:T(8,128)S(1)} fusion(f32[256,512]{1,0:T(8,128)} %get-tuple-element.18, f32[36,512]{1,0:T(8,128)S(1)} %copy-done.2), kind=kOutput, calls=%fused_computation.157 | convolution fusion | flops 56623104 | bytes 634880 | tf_op jit(solution)/shard_map/dot_general | solution.py:252
  42.3 0.7 compare_select_fusion
  43.7 0.2 reshape.483
  43.9 0.7 gather_fusion
  44.6 0.7 compare_and_fusion.1
  45.3 0.2 fusion.31
  45.8 0.2 sub.202
  46.0 0.3 select_reduce_fusion.4
  46.6 10.0 %all-gather.1 = f32[4,2,128]{2,1,0:T(2,128)S(1)} all-gather(f32[1,2,128]{2,1,0:T(2,128)S(1)} %maximum_bitcast_fusion), channel_id=2, replica_groups=mesh['dp'=32,'cls'=4] {'cls'}, dimensions={0}, use_global_device_ids=true | all-gather | bytes 5120 | tf_op jit(solution)/shard_map/all_gather | solution.py:260
  56.7 0.2 div.62
  57.0 0.2 sub.206
  57.4 0.3 fusion.24
  57.8 1.0 fusion.16
  58.7 0.2 fusion.11
  59.0 1.1 gather_fusion.1
  60.1 0.7 pad_maximum_fusion.volume_ref
  61.4 0.6 dynamic_update_slice.6
  62.0 0.9 slice_select_fusion.coef_ref
  62.9 10.3 %shard_map.87 = bf16[4096,512]{1,0:T(8,128)(2,1)} custom-call(s32[1]{0:T(128)} %bitcast.6.count_ref, s32[256]{0:T(256)} %and_select_fusion.4.ent_p_ref, s32[256]{0:T(256)} %get-tuple-element.22.ent_k_ref, bf16[8192,512]{1,0:T(8,128)(2,1)} %get-tuple-element.17.image_hat_hbm, f32[256,512]{1,0:T(8,128)} %slice_select_fusion.coef_ref, ...), custom_call_target="tpu_custom_call" | custom-call | tf_op jit(solution)/shard_map/pallas_call | solution.py:284
  73.2 1.8 %fusion.2 = bf16[16,144,512]{2,1,0:T(8,128)(2,1)S(1)} fusion(s32[]{:T(128)S(6)} %select_n.198, bf16[16,2,128,512]{3,2,1,0:T(8,128)(2,1)} %bitcast.84, bf16[16,2,16,512]{3,2,1,0:T(8,128)(2,1)S(1)} %bitcast.87), kind=kLoop, calls=%fused_computation.10 | loop fusion | flops 4718592 | bytes 7077892 | tf_op jit(solution)/shard_map/jit(dynamic_index_in_dim)/squeeze | solution.py:328
  75.1 2.7 %collective-permute-start = (bf16[16,144,512]{2,1,0:T(8,128)(2,1)S(1)}, bf16[16,144,512]{2,1,0:T(8,128)(2,1)}, u32[]{:S(2)}, u32[]{:S(2)}) collective-permute-start(bf16[16,144,512]{2,1,0:T(8,128)(2,1)S(1)} %fusion.2), channel_id=1, source_target_pairs={{0,4},{4,0},{8,12},{12,8},{16,20},{20,16},{24,28},{28,24},{32,36},... | collective-permute-start | bytes 7077896 | tf_op jit(solution)/shard_map/ppermute | solution.py:329
  77.7 4.3 %collective-permute-done = bf16[16,144,512]{2,1,0:T(8,128)(2,1)} collective-permute-done((bf16[16,144,512]{2,1,0:T(8,128)(2,1)S(1)}, bf16[16,144,512]{2,1,0:T(8,128)(2,1)}, u32[]{:S(2)}, u32[]{:S(2)}) %collective-permute-start) | collective-permute-done | bytes 2359328 | tf_op jit(solution)/shard_map/ppermute | solution.py:329
  82.0 3.0 %fusion = bf16[16,144,512]{2,1,0:T(8,128)(2,1)S(1)} fusion(bf16[16,144,512]{2,1,0:T(8,128)(2,1)} %collective-permute-done, s32[]{:T(128)S(6)} %select_n.197, bf16[16,2,128,512]{3,2,1,0:T(8,128)(2,1)} %bitcast.85, bf16[16,2,16,512]{3,2,1,0:T(8,128)(2,1)S(1)} %bitcast.88), kind=kLoop, calls=%fused_computation.5 | loop fusion | flops 9437184 | bytes 9437188 | tf_op jit(solution)/shard_map/convert_element_type | solution.py:330
  85.1 38.0 %all_to_all.10 = bf16[16,144,512]{2,1,0:T(8,128)(2,1)S(1)} all-to-all(bf16[16,144,512]{2,1,0:T(8,128)(2,1)S(1)} %fusion), channel_id=1, replica_groups={{0,8,16,24,32,40,48,56,64,72,80,88,96,104,112,120},{4,12,20,28,36,44,52..., dimensions={0} | all-to-all | bytes 4718592 | tf_op jit(solution)/shard_map/all_to_all | solution.py:332
  123.6 0.3 convert_reduce_fusion
  123.9 0.2 copy-done.1
  124.0 1.9 %fusion.5 = f32[1,2,64,512]{3,2,1,0:T(8,128)} fusion(f32[2,64,512]{2,1,0:T(8,128)S(1)} %bitcast.90, f32[256,256]{1,0:T(8,128)S(1)} %get-tuple-element.55, f32[256,256]{1,0:T(8,128)S(1)} %get-tuple-element.54, f32[256,256]{1,0:T(8,128)S(1)} %copy-done.1, f32[2]{0:T(128)S(1)} %broadcast_add_fusion.2), kind=kOutput, calls=%fused_computation.17 | convolution fusion | flops 403505152 | bytes 1310728 | tf_op jit(solution)/shard_map/dot_general | solution.py:336
  125.9 0.6 select_reduce_fusion.5
  (72 shorter events, 4.5 us)
Async XLA Ops:
  0.6 17.2 %copy-start.3 = (s32[128]{0:T(128)S(1)}, s32[128]{0:T(128)}, u32[]{:S(2)}) copy-start(s32[128]{0:T(128)} %param.10) | copy-start | bytes 1540
  0.6 15.1 %copy-start.4 = (f32[64]{0:T(128)S(1)}, f32[64]{0:T(128)}, u32[]{:S(2)}) copy-start(f32[64]{0:T(128)} %param.13) | copy-start | bytes 772
  2.0 15.8 %all-to-all-start = ((s32[32,128,3]{1,2,0:T(4,128)}), s32[32,128,3]{1,2,0:T(4,128)S(1)}, u32[]{:S(2)}, u32[]{:S(2)}) async-start(s32[32,128,3]{1,2,0:T(4,128)} %broadcast_in_dim.187), calls=%async_computation | async-start | bytes 131072 | tf_op jit(solution)/shard_map/all_to_all | solution.py:194
  12.3 28.2 %copy-start = (f32[256,256]{1,0:T(8,128)}, f32[256,256]{1,0:T(8,128)S(1)}, u32[]{:S(2)}) copy-start(f32[256,256]{1,0:T(8,128)S(1)} %fusion.30) | copy-start | bytes 786436
  23.0 17.5 %copy-start.2 = (f32[36,512]{1,0:T(8,128)S(1)}, f32[36,512]{1,0:T(8,128)}, u32[]{:S(2)}) copy-start(f32[36,512]{1,0:T(8,128)} %param.12) | copy-start | bytes 221188
  75.1 7.0 %collective-permute-start = (bf16[16,144,512]{2,1,0:T(8,128)(2,1)S(1)}, bf16[16,144,512]{2,1,0:T(8,128)(2,1)}, u32[]{:S(2)}, u32[]{:S(2)}) collective-permute-start(bf16[16,144,512]{2,1,0:T(8,128)(2,1)S(1)} %fusion.2), channel_id=1, source_target_pairs={{0,4},{4,0},{8,12},{12,8},{16,20},{20,16},{24,28},{28,24},{32,36},... | collective-permute-start | bytes 7077896 | tf_op jit(solution)/shard_map/ppermute | solution.py:329
  123.1 1.0 copy-start.1

commit v11 on v10

--- a/solution.py
+++ b/solution.py
@@ -1,6 +1,7 @@
 import math
 
 import jax
+import numpy as np
 import jax.numpy as jnp
 from jax import lax
 from jax.experimental import pallas as pl
@@ -13,6 +14,18 @@
 
 HIGHEST = lax.Precision.HIGHEST
 F32 = jnp.float32
+
+
+def table_constant(points):
+    positions = np.arange(points, dtype=np.int32)
+    product = positions[:, None] * positions[None, :] % points
+    angles = product.astype(np.float32) * np.float32(2.0 * math.pi / points)
+    scale = np.float32(math.sqrt(points))
+    cosine = np.cos(angles) / scale
+    sine_part = np.sin(angles) / scale
+    upper_half = np.concatenate([cosine, -sine_part], axis=1)
+    lower_half = np.concatenate([sine_part, cosine], axis=1)
+    return np.concatenate([upper_half, lower_half], axis=0).astype(np.float32)
 
 
 def angular_tables(points):
@@ -53,13 +66,15 @@
         copy.start()
         loads.append(copy)
     forward = forward_ref[...]
-    wrow = wrow_ref[...]
+    wrow = wrow_ref[...][None]
     stores = []
     for c in range(n_ref):
         loads[c].wait()
         hat = jnp.dot(refs_buf[rows(c)], forward, preferred_element_type=F32).astype(jnp.bfloat16)
         ref_hat_buf[rows(c)] = hat
-        weighted_ref[rows(c)] = (hat.astype(F32) * wrow).astype(jnp.bfloat16)
+        weighted_ref[rows(c)] = (
+            hat.astype(F32).reshape(-1, NSHELL, hat.shape[1]) * wrow
+        ).reshape(hat.shape).astype(jnp.bfloat16)
         copy = pltpu.make_async_copy(ref_hat_buf.at[rows(c)], ref_hat_hbm.at[rows(c)], out_sem.at[c])
         copy.start()
         stores.append(copy)
@@ -186,9 +201,9 @@
     per_pair = blocksize // dp_count
     row_width = 2 * NANG
     entries = blocksize * LIST
-    full_table = angular_tables(NANG)
-    forward = full_table.astype(jnp.bfloat16)
-    inverse = full_table.T
+    full_table = table_constant(NANG)
+    forward = jnp.asarray(full_table).astype(jnp.bfloat16)
+    inverse = jnp.asarray(np.ascontiguousarray(full_table.T))
 
     packed = jnp.concatenate([class_lists, pose_slot[:, None]], axis=1)
     all_packed = lax.all_to_all(
@@ -217,7 +232,7 @@
 
     image_rows = images.shape[0] * NSHELL
     ref_rows = col_classes * NSHELL
-    wrow = jnp.tile(shell_weight, CHUNK // NSHELL)[:, None]
+    wrow = shell_weight[:, None]
     params = pltpu.CompilerParams(vmem_limit_bytes=60 * 1024 * 1024)
     anywhere = pl.BlockSpec(memory_space=pl.MemorySpace.ANY)
     cross_c, image_hat, ref_hat = pl.pallas_call(

time: 127 us -> 124 us (0.976)
  waiting for transfers between devices: 5.46 us -> 7.96 us
  other arithmetic: 20.6 us -> 18.3 us
  blocking collectives: 48 us -> 45.9 us
    all_to_all x1, blocking collectives: 38 us -> 35.2 us  [local(): lax.all_to_all(pair_sum, 'dp', split_axis=0, concat_axis=0, tiled=True, a...]
    all_to_all x1, waiting for transfers between devices: 1.17 us -> 3.67 us  [local(): lax.all_to_all(jnp.broadcast_to(packed[None], (dp_count,) + packed.shape)...]
    broadcast_in_dim x0 -> x1, local copies, waits for them, and re-layouts: none -> 1.35 us  [local(): wrow = shell_weight[:, None]]
  transfers between devices with their start and end apart: 2 -> 2, of which waited for: 2 -> 2; matrix products, arithmetic and copies ran while one was open for 5% -> 3% of each run, Pallas kernels for 0% -> 0%
where the time goes in v11:
time: 124 us
  blocking collectives  45.9 us (37%)
  Pallas kernels  27 us (22%)
  other arithmetic  18.3 us (15%)
  starting transfers between devices  11.2 us (9%)
  local copies, waits for them, and re-layouts  8.23 us (7%)
  waiting for transfers between devices  7.96 us (6%)
  matrix products  4.31 us (3%)
    all_to_all x1, blocking collectives, local(): lax.all_to_all(pair_sum, 'dp', split_axis=0, concat_axis=0, tiled=True, a...  35.2 us
    pallas_call x1, Pallas kernels, local(): pl.pallas_call(cross_kernel, out_shape=(jax.ShapeDtypeStruct((entries, ro...  16.9 us
    all_gather x1, blocking collectives, local(): gathered = lax.all_gather(jnp.stack([top_local, total_local]), 'cls')  10.7 us
    pallas_call x1, Pallas kernels, local(): pl.pallas_call(grad_kernel, out_shape=jax.ShapeDtypeStruct((ref_rows, row...  10.1 us
    all_to_all x1, starting transfers between devices, local(): lax.all_to_all(jnp.broadcast_to(packed[None], (dp_count,) + packed.shape)...  8.25 us
    ppermute x1, waiting for transfers between devices, local(): taken = lax.ppermute(give, 'dp', perm=[(i, i ^ 1) for i in range(dp_count)])  4.29 us
    all_to_all x1, waiting for transfers between devices, local(): lax.all_to_all(jnp.broadcast_to(packed[None], (dp_count,) + packed.shape)...  3.67 us
    convert_element_type x1, other arithmetic, local(): pair_sum = (keep.astype(F32) + taken.astype(F32)).astype(jnp.bfloat16)  3.04 us
  transfers between devices with their start and end apart: 2, of which 2 were waited for; matrix products, arithmetic and copies ran while one was open for 3% of the time, Pallas kernels for 0%

profile of v11, /device:TPU:0, one launch (start us, length us, event | category | flops | bytes accessed | tf_op | source)
XLA Modules:
  0.0 123.8 jit_solution(16825413109568699662)
XLA Ops:
  0.6 0.7 pad_add_fusion
  1.3 0.6 broadcast_in_dim.180
  2.0 8.2 %all-to-all-start = ((s32[32,128,3]{1,2,0:T(4,128)}), s32[32,128,3]{1,2,0:T(4,128)S(1)}, u32[]{:S(2)}, u32[]{:S(2)}) async-start(s32[32,128,3]{1,2,0:T(4,128)} %broadcast_in_dim.180), calls=%async_computation | async-start | bytes 131072 | tf_op jit(solution)/shard_map/all_to_all | solution.py:209
  10.2 0.7 and_select_fusion.3
  10.9 0.8 fusion.56
  11.7 0.7 convert_log-plus-one_fusion
  12.4 0.3 reduce_window_sum.82
  12.7 1.3 %copy.55.wrow_ref = f32[64,1]{1,0:T(8,128)} copy(f32[64,1]{0,1:T(1,128)} %bitcast.111) | data formatting | bytes 512 | tf_op jit(solution)/shard_map/broadcast_in_dim | solution.py:235
  14.1 3.7 %all-to-all-done = s32[32,128,3]{1,2,0:T(4,128)S(1)} async-done(((s32[32,128,3]{1,2,0:T(4,128)}), s32[32,128,3]{1,2,0:T(4,128)S(1)}, u32[]{:S(2)}, u32[]{:S(2)}) %all-to-all-start) | async-done | bytes 49184 | tf_op jit(solution)/shard_map/all_to_all | solution.py:209
  17.8 1.3 %select_reduce_fusion.1 = (s32[128]{0:T(128)S(1)}, s32[128]{0:T(128)S(1)}) fusion(s32[4096]{0:T(1024)S(1)} %bitcast.93, s32[128]{0:T(128)} %param.12, s32[4096]{0:T(1024)S(1)} %bitcast.92), kind=kLoop, calls=%fused_computation.14 | loop fusion | flops 2621184 | bytes 34304 | tf_op jit(solution)/shard_map/reduce_sum | solution.py:215
  19.4 0.3 reduce-window.16
  19.7 0.6 convert_reduce_fusion.1
  20.7 0.3 reduce-window.24
  21.6 0.7 compare_and_fusion.2
  22.4 0.7 select_reduce_fusion.2
  23.0 0.6 and_select_fusion.4.ent_p_ref
  23.6 16.9 %shard_map.104 = (f32[256,512]{1,0:T(8,128)}, bf16[8192,512]{1,0:T(8,128)(2,1)}, bf16[4096,512]{1,0:T(8,128)(2,1)}) custom-call(s32[1]{0:T(128)} %bitcast.6.count_ref, s32[256]{0:T(256)} %and_select_fusion.4.ent_p_ref, s32[256]{0:T(256)} %get-tuple-element.22.ent_k_ref, bf16[8192,512]{1,0:T(8,128)(2,1)} %bitcast.86, bf16[4096,512]{1,0:T(8,128)(2,1)} %bitcast.89, ...), custom_call_target="tpu_custom_call" | custom-call | tf_op jit(solution)/shard_map/pallas_call | solution.py:238
  40.6 1.6 %fusion.59 = f32[256,36]{1,0:T(8,128)S(1)} fusion(f32[256,512]{1,0:T(8,128)} %get-tuple-element.18, f32[36,512]{1,0:T(8,128)S(1)} %copy-done.1), kind=kOutput, calls=%fused_computation.141 | convolution fusion | flops 56623104 | bytes 634880 | tf_op jit(solution)/shard_map/dot_general | solution.py:267
  42.2 0.1 and.125
  42.3 0.7 compare_select_fusion
  43.3 0.2 reshape.484
  43.7 0.2 reshape.482
  43.9 0.7 gather_fusion
  44.6 0.7 compare_and_fusion.1
  45.3 0.2 fusion.22
  45.9 0.2 sub.202
  46.0 0.3 select_reduce_fusion.4
  46.3 0.1 reduce_sum.151
  46.6 10.7 %all-gather.1 = f32[4,2,128]{2,1,0:T(2,128)S(1)} all-gather(f32[1,2,128]{2,1,0:T(2,128)S(1)} %maximum_bitcast_fusion), channel_id=2, replica_groups=mesh['dp'=32,'cls'=4] {'cls'}, dimensions={0}, use_global_device_ids=true | all-gather | bytes 5120 | tf_op jit(solution)/shard_map/all_gather | solution.py:275
  57.4 0.2 div.50
  57.6 0.2 sub.206
  57.9 0.1 and.123
  58.1 0.3 fusion.16
  58.4 0.9 fusion.8
  59.4 0.2 fusion.6
  59.6 1.1 gather_fusion.1
  60.7 0.7 pad_maximum_fusion.volume_ref
  62.0 0.6 dynamic_update_slice.6
  62.7 0.9 slice_select_fusion.coef_ref
  63.6 10.1 %shard_map.105 = bf16[4096,512]{1,0:T(8,128)(2,1)} custom-call(s32[1]{0:T(128)} %bitcast.6.count_ref, s32[256]{0:T(256)} %and_select_fusion.4.ent_p_ref, s32[256]{0:T(256)} %get-tuple-element.22.ent_k_ref, bf16[8192,512]{1,0:T(8,128)(2,1)} %get-tuple-element.17.image_hat_hbm, f32[256,512]{1,0:T(8,128)} %slice_select_fusion.coef_ref, ...), custom_call_target="tpu_custom_call" | custom-call | tf_op jit(solution)/shard_map/pallas_call | solution.py:299
  73.7 1.8 %fusion.2 = bf16[16,144,512]{2,1,0:T(8,128)(2,1)S(1)} fusion(s32[]{:T(128)S(6)} %select_n.185, bf16[16,2,128,512]{3,2,1,0:T(8,128)(2,1)} %bitcast.84, bf16[16,2,16,512]{3,2,1,0:T(8,128)(2,1)S(1)} %bitcast.87), kind=kLoop, calls=%fused_computation.10 | loop fusion | flops 4718592 | bytes 7077892 | tf_op jit(solution)/shard_map/jit(dynamic_index_in_dim)/squeeze | solution.py:343
  75.5 2.9 %collective-permute-start = (bf16[16,144,512]{2,1,0:T(8,128)(2,1)S(1)}, bf16[16,144,512]{2,1,0:T(8,128)(2,1)}, u32[]{:S(2)}, u32[]{:S(2)}) collective-permute-start(bf16[16,144,512]{2,1,0:T(8,128)(2,1)S(1)} %fusion.2), channel_id=1, source_target_pairs={{0,4},{4,0},{8,12},{12,8},{16,20},{20,16},{24,28},{28,24},{32,36},... | collective-permute-start | bytes 7077896 | tf_op jit(solution)/shard_map/ppermute | solution.py:344
  78.4 4.3 %collective-permute-done = bf16[16,144,512]{2,1,0:T(8,128)(2,1)} collective-permute-done((bf16[16,144,512]{2,1,0:T(8,128)(2,1)S(1)}, bf16[16,144,512]{2,1,0:T(8,128)(2,1)}, u32[]{:S(2)}, u32[]{:S(2)}) %collective-permute-start) | collective-permute-done | bytes 2359328 | tf_op jit(solution)/shard_map/ppermute | solution.py:344
  82.7 3.0 %fusion = bf16[16,144,512]{2,1,0:T(8,128)(2,1)S(1)} fusion(bf16[16,144,512]{2,1,0:T(8,128)(2,1)} %collective-permute-done, s32[]{:T(128)S(6)} %select_n.184, bf16[16,2,128,512]{3,2,1,0:T(8,128)(2,1)} %bitcast.85, bf16[16,2,16,512]{3,2,1,0:T(8,128)(2,1)S(1)} %bitcast.88), kind=kLoop, calls=%fused_computation.5 | loop fusion | flops 9437184 | bytes 9437188 | tf_op jit(solution)/shard_map/convert_element_type | solution.py:345
  85.7 35.2 %all_to_all.10 = bf16[16,144,512]{2,1,0:T(8,128)(2,1)S(1)} all-to-all(bf16[16,144,512]{2,1,0:T(8,128)(2,1)S(1)} %fusion), channel_id=1, replica_groups={{0,8,16,24,32,40,48,56,64,72,80,88,96,104,112,120},{4,12,20,28,36,44,52..., dimensions={0} | all-to-all | bytes 4718592 | tf_op jit(solution)/shard_map/all_to_all | solution.py:347
  121.5 0.6 select_reduce_fusion.5
  122.1 0.3 convert_reduce_fusion
  122.4 1.4 %fusion.5 = f32[1,2,64,512]{3,2,1,0:T(8,128)} fusion(f32[2,64,512]{2,1,0:T(8,128)S(1)} %bitcast.90, f32[512,512,1]{1,0,2:T(8,128)S(1)} %copy-done, f32[2]{0:T(128)S(1)} %broadcast_add_fusion.2), kind=kOutput, calls=%fused_computation.17 | convolution fusion | flops 402718720 | bytes 1572872 | tf_op jit(solution)/shard_map/dot_general | solution.py:351
  (62 shorter events, 3.9 us)
Async XLA Ops:
  2.0 15.8 %all-to-all-start = ((s32[32,128,3]{1,2,0:T(4,128)}), s32[32,128,3]{1,2,0:T(4,128)S(1)}, u32[]{:S(2)}, u32[]{:S(2)}) async-start(s32[32,128,3]{1,2,0:T(4,128)} %broadcast_in_dim.180), calls=%async_computation | async-start | bytes 131072 | tf_op jit(solution)/shard_map/all_to_all | solution.py:209
  23.6 16.9 %copy-start.1 = (f32[36,512]{1,0:T(8,128)S(1)}, f32[36,512]{1,0:T(8,128)}, u32[]{:S(2)}) copy-start(f32[36,512]{1,0:T(8,128)} %param.14) | copy-start | bytes 221188
  75.5 7.2 %collective-permute-start = (bf16[16,144,512]{2,1,0:T(8,128)(2,1)S(1)}, bf16[16,144,512]{2,1,0:T(8,128)(2,1)}, u32[]{:S(2)}, u32[]{:S(2)}) collective-permute-start(bf16[16,144,512]{2,1,0:T(8,128)(2,1)S(1)} %fusion.2), channel_id=1, source_target_pairs={{0,4},{4,0},{8,12},{12,8},{16,20},{20,16},{24,28},{28,24},{32,36},... | collective-permute-start | bytes 7077896 | tf_op jit(solution)/shard_map/ppermute | solution.py:344
  121.0 1.4 %copy-start = (f32[512,512,1]{1,0,2:T(8,128)S(1)}, f32[512,512,1]{1,0,2:T(8,128)}, u32[]{:S(2)}) copy-start(f32[512,512,1]{1,0,2:T(8,128)} %constant.163) | copy-start | bytes 3145732

commit v12 on v11

--- a/solution.py
+++ b/solution.py
@@ -44,12 +44,14 @@
 
 
 def cross_kernel(
-    count_ref, ent_p_ref, ent_k_ref, image_hbm, refs_hbm, forward_ref, wrow_ref,
-    cross_ref, image_hat_hbm, ref_hat_hbm,
+    packed_ref, pose_ref, column_ref, image_hbm, refs_hbm, forward_ref, wrow_ref,
+    cross_ref, image_hat_hbm, ref_hat_hbm, count_ref, ent_p_ref, ent_k_ref, ent_e_ref, class_ref,
     image_buf, refs_buf, hat_buf, ref_hat_buf, weighted_ref, in_sem, out_sem,
 ):
     n_image = image_buf.shape[0] // CHUNK
     n_ref = refs_buf.shape[0] // CHUNK
+    n_particle = pose_ref.shape[0]
+    n_class = refs_buf.shape[0] // NSHELL
 
     def rows(c):
         return pl.ds(c * CHUNK, CHUNK)
@@ -65,6 +67,34 @@
         )
         copy.start()
         loads.append(copy)
+    first = column_ref[0] * n_class
+
+    def clear(e, carry):
+        ent_p_ref[e] = 0
+        ent_k_ref[e] = 0
+        ent_e_ref[e] = 0
+        return carry
+
+    lax.fori_loop(0, n_particle * LIST, clear, 0)
+
+    def prep(p, cnt):
+        slot = pose_ref[p]
+        for a in range(LIST):
+            k = packed_ref[slot * (LIST + 1) + a] - first
+            e = p * LIST + a
+            class_ref[e] = k
+            ins = jnp.logical_and(k >= 0, k < n_class)
+
+            @pl.when(ins)
+            def _():
+                ent_p_ref[cnt] = p
+                ent_k_ref[cnt] = k
+                ent_e_ref[cnt] = e
+
+            cnt = cnt + ins.astype(jnp.int32)
+        return cnt
+
+    count_ref[0] = lax.fori_loop(0, n_particle, prep, 0)
     forward = forward_ref[...]
     wrow = wrow_ref[...][None]
     stores = []
@@ -101,7 +131,7 @@
         w_im = w[:, NANG:]
         c_re = jnp.sum(x_re * w_re + x_im * w_im, axis=0, keepdims=True)
         c_im = jnp.sum(x_im * w_re - x_re * w_im, axis=0, keepdims=True)
-        cross_ref[pl.ds(e, 1), :] = jnp.concatenate([c_re, c_im], axis=1)
+        cross_ref[pl.ds(ent_e_ref[e], 1), :] = jnp.concatenate([c_re, c_im], axis=1)
         return carry
 
     lax.fori_loop(0, count_ref[0], body, 0)
@@ -110,7 +140,7 @@
 
 
 def grad_kernel(
-    count_ref, ent_p_ref, ent_k_ref, image_hat_hbm, coef_ref, ref_hat_hbm, volume_ref,
+    count_ref, ent_p_ref, ent_k_ref, ent_e_ref, image_hat_hbm, coef_ref, ref_hat_hbm, volume_ref,
     out_hbm, image_buf, ref_buf, acc_ref, out_buf, in_sem, out_sem,
 ):
     n_image = image_buf.shape[0] // CHUNK
@@ -151,7 +181,7 @@
         rp = pl.multiple_of(ent_p_ref[e] * NSHELL, NSHELL)
         rk = pl.multiple_of(ent_k_ref[e] * NSHELL, NSHELL)
         x = image_buf[pl.ds(rp, NSHELL), :].astype(F32)
-        c = coef_ref[pl.ds(e, 1), :]
+        c = coef_ref[pl.ds(ent_e_ref[e], 1), :]
         c_re = c[:, :NANG]
         c_im = c[:, NANG:]
         x_re = x[:, :NANG]
@@ -209,41 +239,25 @@
     all_packed = lax.all_to_all(
         jnp.broadcast_to(packed[None], (dp_count,) + packed.shape), "dp", 0, 0, tiled=True
     ).reshape(dp_count * blocksize, LIST + 1)
-    all_lists = all_packed[:, :LIST]
-    slot_hit = jnp.arange(all_lists.shape[0], dtype=jnp.int32)[None, :] == pose_slot[:, None]
-    my_lists = jnp.stack(
-        [jnp.sum(jnp.where(slot_hit, all_lists[None, :, a], 0), axis=1) for a in range(LIST)],
-        axis=1,
-    )
-    local_class = (my_lists - column * col_classes).reshape(entries)
-    inside = (local_class >= 0) & (local_class < col_classes)
-    inside_i = inside.astype(jnp.int32)
-    count = jnp.sum(inside_i)
-    before_in = jnp.cumsum(inside_i) - inside_i
-    before_out = jnp.cumsum(1 - inside_i) - (1 - inside_i)
-    rank = jnp.where(inside, before_in, count + before_out)
-    slots = jnp.arange(entries, dtype=jnp.int32)
-    at_rank = rank[None, :] == slots[:, None]
-    order = jnp.sum(jnp.where(at_rank, slots[None, :], 0), axis=1)
-    safe_class = jnp.clip(local_class, 0, col_classes - 1)
-    ent_p = order // LIST
-    ent_k = jnp.sum(jnp.where(at_rank, safe_class[None, :], 0), axis=1)
-    count_arr = count.reshape(1)
-
     image_rows = images.shape[0] * NSHELL
     ref_rows = col_classes * NSHELL
     wrow = shell_weight[:, None]
     params = pltpu.CompilerParams(vmem_limit_bytes=60 * 1024 * 1024)
     anywhere = pl.BlockSpec(memory_space=pl.MemorySpace.ANY)
-    cross_c, image_hat, ref_hat = pl.pallas_call(
+    cross_c, image_hat, ref_hat, count_arr, ent_p, ent_k, ent_e, local_class = pl.pallas_call(
         cross_kernel,
         out_shape=(
             jax.ShapeDtypeStruct((entries, row_width), F32),
             jax.ShapeDtypeStruct((image_rows, row_width), jnp.bfloat16),
             jax.ShapeDtypeStruct((ref_rows, row_width), jnp.bfloat16),
+            jax.ShapeDtypeStruct((1,), jnp.int32),
+            jax.ShapeDtypeStruct((entries,), jnp.int32),
+            jax.ShapeDtypeStruct((entries,), jnp.int32),
+            jax.ShapeDtypeStruct((entries,), jnp.int32),
+            jax.ShapeDtypeStruct((entries,), jnp.int32),
         ),
         in_specs=[smem(), smem(), smem(), anywhere, anywhere, vmem(), vmem()],
-        out_specs=(vmem(), anywhere, anywhere),
+        out_specs=(vmem(), anywhere, anywhere, smem(), smem(), smem(), smem(), smem()),
         scratch_shapes=[
             pltpu.VMEM((image_rows, row_width), jnp.bfloat16),
             pltpu.VMEM((ref_rows, row_width), jnp.bfloat16),
@@ -255,9 +269,12 @@
         ],
         compiler_params=params,
     )(
-        count_arr, ent_p, ent_k, images.reshape(image_rows, row_width),
-        references.reshape(ref_rows, row_width), forward, wrow,
-    )
+        all_packed.reshape(-1), pose_slot, column.astype(jnp.int32).reshape(1),
+        images.reshape(image_rows, row_width), references.reshape(ref_rows, row_width),
+        forward, wrow,
+    )
+    inside = (local_class >= 0) & (local_class < col_classes)
+    safe_class = jnp.clip(local_class, 0, col_classes - 1)
 
     log_prior = jnp.log1p(class_counts.astype(F32))
     prior = jnp.sum(
@@ -265,7 +282,7 @@
         axis=1,
     )
     scores_c = jnp.dot(cross_c, rotation_response.T, precision=HIGHEST)
-    scores = jnp.take(scores_c, rank, axis=0) + prior[:, None]
+    scores = scores_c + prior[:, None]
     scores = jnp.where(inside[:, None], scores, -1e30).reshape(blocksize, LIST, -1)
     inside_pa = inside.reshape(blocksize, LIST)
     top_local = jnp.max(scores, axis=(1, 2))
@@ -288,7 +305,6 @@
     rot_im = rotation_response[:, NANG:]
     coef_table = jnp.concatenate([rot_re, -rot_im, rot_re * rot_re + rot_im * rot_im], axis=1)
     coef = jnp.dot(posterior.reshape(entries, -1), coef_table, precision=HIGHEST)
-    coef_c = jnp.take(coef, order, axis=0)
 
     class_pick = (
         (local_class[None, :] == jnp.arange(col_classes, dtype=jnp.int32)[:, None]) & inside[None, :]
@@ -299,7 +315,7 @@
     numer = pl.pallas_call(
         grad_kernel,
         out_shape=jax.ShapeDtypeStruct((ref_rows, row_width), jnp.bfloat16),
-        in_specs=[smem(), smem(), smem(), anywhere, vmem(), anywhere, vmem()],
+        in_specs=[smem(), smem(), smem(), smem(), anywhere, vmem(), anywhere, vmem()],
         out_specs=anywhere,
         scratch_shapes=[
             pltpu.VMEM((image_rows, row_width), jnp.bfloat16),
@@ -310,7 +326,7 @@
             pltpu.SemaphoreType.DMA((ref_rows // CHUNK,)),
         ],
         compiler_params=params,
-    )(count_arr, ent_p, ent_k, image_hat, coef_c[:, :row_width], ref_hat, volume_full)
+    )(count_arr, ent_p, ent_k, ent_e, image_hat, coef[:, :row_width], ref_hat, volume_full)
 
     core = dp_index % 2
     dest = pose_slot // blocksize

time: 124 us -> 122 us (0.984)
  other arithmetic: 18.3 us -> 12.4 us
  Pallas kernels: 27 us -> 31.8 us
    pallas_call x1, Pallas kernels: 16.9 us -> 21.1 us  [local(): pl.pallas_call(cross_kernel, out_shape=(jax.ShapeDtypeStruct((entries, ro...]
    reduce_sum x3 -> x0, other arithmetic: 2.6 us -> none  [the longest x1 1.31 us: local(): jnp.sum(jnp.where(slot_hit, all_lists[None, :, a], 0), axis=1)]
    select_n x3 -> x0, other arithmetic: 2.16 us -> none  [the longest x2 1.56 us: local(): coef_c = jnp.take(coef, order, axis=0)]
    gather x2 -> x0, local copies, waits for them, and re-layouts: 1.83 us -> none  [the longest x1 1.09 us: local(): coef_c = jnp.take(coef, order, axis=0)]
    and x2 -> x0, other arithmetic: 1.39 us -> none  [local(): scores = jnp.take(scores_c, rank, axis=0) + prior[:, None]]
    all_gather x1, blocking collectives: 10.7 us -> 9.3 us  [local(): gathered = lax.all_gather(jnp.stack([top_local, total_local]), 'cls')]
where the time goes in v12:
time: 122 us; the launch traced here: 121 us
  blocking collectives  44.9 us (37%)
  Pallas kernels  31.8 us (26%)
  other arithmetic  12.4 us (10%)
  starting transfers between devices  11 us (9%)
  waiting for transfers between devices  7.96 us (7%)
  local copies, waits for them, and re-layouts  7.62 us (6%)
  matrix products  4.87 us (4%)
    all_to_all x1, blocking collectives, local(): lax.all_to_all(pair_sum, 'dp', split_axis=0, concat_axis=0, tiled=True, a...  35.6 us
    pallas_call x1, Pallas kernels, local(): pl.pallas_call(cross_kernel, out_shape=(jax.ShapeDtypeStruct((entries, ro...  21.1 us
    pallas_call x1, Pallas kernels, local(): pl.pallas_call(grad_kernel, out_shape=jax.ShapeDtypeStruct((ref_rows, row...  10.7 us
    all_gather x1, blocking collectives, local(): gathered = lax.all_gather(jnp.stack([top_local, total_local]), 'cls')  9.3 us
    all_to_all x1, starting transfers between devices, local(): lax.all_to_all(jnp.broadcast_to(packed[None], (dp_count,) + packed.shape)...  8.25 us
    ppermute x1, waiting for transfers between devices, local(): taken = lax.ppermute(give, 'dp', perm=[(i, i ^ 1) for i in range(dp_count)])  4.29 us
    all_to_all x1, waiting for transfers between devices, local(): lax.all_to_all(jnp.broadcast_to(packed[None], (dp_count,) + packed.shape)...  3.67 us
    convert_element_type x1, other arithmetic, local(): pair_sum = (keep.astype(F32) + taken.astype(F32)).astype(jnp.bfloat16)  3.04 us
  transfers between devices with their start and end apart: 2, of which 2 were waited for; matrix products, arithmetic and copies ran while one was open for 3% of the time, Pallas kernels for 0%

profile of v12, /device:TPU:0, one launch (start us, length us, event | category | flops | bytes accessed | tf_op | source)
XLA Modules:
  0.0 121.4 jit_solution(4193327640538034078)
XLA Ops:
  0.6 0.7 pad_add_fusion
  1.3 0.6 broadcast_in_dim.111
  2.0 8.2 %all-to-all-start = ((s32[32,128,3]{1,2,0:T(4,128)}), s32[32,128,3]{1,2,0:T(4,128)S(1)}, u32[]{:S(2)}, u32[]{:S(2)}) async-start(s32[32,128,3]{1,2,0:T(4,128)} %broadcast_in_dim.111), calls=%async_computation | async-start | bytes 131072 | tf_op jit(solution)/shard_map/all_to_all | solution.py:239
  10.2 0.7 and_select_fusion.3
  10.9 0.8 fusion.30
  11.7 0.7 convert_log-plus-one_fusion
  12.4 0.3 reduce_window_sum.11
  12.7 1.3 %copy.31.wrow_ref = f32[64,1]{1,0:T(8,128)} copy(f32[64,1]{0,1:T(1,128)} %bitcast.55) | data formatting | bytes 512 | tf_op jit(solution)/shard_map/broadcast_in_dim | solution.py:244
  14.1 3.7 %all-to-all-done = s32[32,128,3]{1,2,0:T(4,128)S(1)} async-done(((s32[32,128,3]{1,2,0:T(4,128)}), s32[32,128,3]{1,2,0:T(4,128)S(1)}, u32[]{:S(2)}, u32[]{:S(2)}) %all-to-all-start) | async-done | bytes 49184 | tf_op jit(solution)/shard_map/all_to_all | solution.py:239
  17.8 0.6 copy.30
  18.4 2.0 %reshape_reshape.3.packed_ref = s32[12288]{0:T(1024)} reshape(s32[32,128,3]{2,1,0:T(8,128)S(1)} %copy.30) | data formatting | bytes 98304 | tf_op jit(solution)/shard_map/reshape;reshape | solution.py:272
  20.4 21.1 %shard_map.104 = (f32[256,512]{1,0:T(8,128)}, bf16[8192,512]{1,0:T(8,128)(2,1)}, bf16[4096,512]{1,0:T(8,128)(2,1)}, s32[1]{0:T(128)}, s32[256]{0:T(256)}, /*index=5*/s32[256]{0:T(256)}, s32[256]{0:T(256)}, s32[256]{0:T(256)}) custom-call(s32[12288]{0:T(1024)} %reshape_reshape.3.packed_ref, s32[128]{0:T(128)} %pose_ref.1, s32[1]{0:T(128)} %bitcast.1.column_ref, ...), custom_call_target="tpu_custom_call" | custom-call | tf_op jit(solution)/shard_map/pallas_call | solution.py:247
  41.5 0.6 broadcast_clamp_fusion
  42.1 0.6 compare_and_fusion.1
  42.8 0.1 select_reduce_fusion.1
  42.9 1.6 %fusion.32 = (f32[256]{0:T(256)S(1)}, f32[256,36]{0,1:T(8,128)S(1)}) fusion(f32[256]{0:T(256)S(1)} %select_reduce_fusion.1, f32[256,512]{1,0:T(8,128)} %get-tuple-element.28, f32[36,512]{1,0:T(8,128)S(1)} %copy-done.1, pred[256]{0:T(512)(128)(4,1)S(1)} %compare_and_fusion.1), kind=kOutput, calls=%fused_computation.75 | convolution fusion | flops 56650496 | bytes 637184 | tf_op jit(solution)/shard_map/dot_general | solution.py:284
  44.5 0.1 reduce_max.26
  44.6 0.1 reduce_max.27
  44.8 0.2 sub.54
  45.0 0.1 reduce_sum.99
  45.2 0.1 reduce_sum.100
  45.3 9.3 %all-gather.1 = f32[4,2,128]{2,1,0:T(2,128)S(1)} all-gather(f32[1,2,128]{2,1,0:T(2,128)S(1)} %maximum_bitcast_fusion), channel_id=2, replica_groups=mesh['dp'=32,'cls'=4] {'cls'}, dimensions={0}, use_global_device_ids=true | all-gather | bytes 5120 | tf_op jit(solution)/shard_map/all_gather | solution.py:292
  54.6 0.1 div.34
  54.7 0.2 div.35
  54.9 0.2 sub.58
  55.1 0.8 fusion.9
  56.0 0.9 slice.73.coef_ref
  56.8 0.9 fusion.7
  57.7 0.7 pad_maximum_fusion.volume_ref
  58.4 0.1 fusion.16
  58.5 0.7 compare_and_fusion
  59.3 0.1 fusion.19
  59.4 0.1 concatenate.26
  59.5 0.1 copy.33
  59.7 0.6 dynamic_update_slice.6
  60.3 10.7 %shard_map.105 = bf16[4096,512]{1,0:T(8,128)(2,1)} custom-call(s32[1]{0:T(128)} %get-tuple-element.22.count_ref, s32[256]{0:T(256)} %get-tuple-element.23.ent_p_ref, s32[256]{0:T(256)} %get-tuple-element.24.ent_k_ref, s32[256]{0:T(256)} %get-tuple-element.25.ent_e_ref, bf16[8192,512]{1,0:T(8,128)(2,1)} %get-tuple-element.26.image_hat_hbm, ...), custom_call_target="tpu_custom_call" | custom-call | tf_op jit(solution)/shard_map/pallas_call | solution.py:315
  71.1 1.8 %fusion.2 = bf16[16,144,512]{2,1,0:T(8,128)(2,1)S(1)} fusion(s32[]{:T(128)S(6)} %select_n.68, bf16[16,2,128,512]{3,2,1,0:T(8,128)(2,1)} %bitcast.40, bf16[16,2,16,512]{3,2,1,0:T(8,128)(2,1)S(1)} %bitcast.43), kind=kLoop, calls=%fused_computation.8 | loop fusion | flops 4718592 | bytes 7077892 | tf_op jit(solution)/shard_map/jit(dynamic_index_in_dim)/squeeze | solution.py:359
  72.9 2.7 %collective-permute-start = (bf16[16,144,512]{2,1,0:T(8,128)(2,1)S(1)}, bf16[16,144,512]{2,1,0:T(8,128)(2,1)}, u32[]{:S(2)}, u32[]{:S(2)}) collective-permute-start(bf16[16,144,512]{2,1,0:T(8,128)(2,1)S(1)} %fusion.2), channel_id=1, source_target_pairs={{0,4},{4,0},{8,12},{12,8},{16,20},{20,16},{24,28},{28,24},{32,36},... | collective-permute-start | bytes 7077896 | tf_op jit(solution)/shard_map/ppermute | solution.py:360
  75.6 4.3 %collective-permute-done = bf16[16,144,512]{2,1,0:T(8,128)(2,1)} collective-permute-done((bf16[16,144,512]{2,1,0:T(8,128)(2,1)S(1)}, bf16[16,144,512]{2,1,0:T(8,128)(2,1)}, u32[]{:S(2)}, u32[]{:S(2)}) %collective-permute-start) | collective-permute-done | bytes 2359328 | tf_op jit(solution)/shard_map/ppermute | solution.py:360
  79.9 3.0 %fusion = bf16[16,144,512]{2,1,0:T(8,128)(2,1)S(1)} fusion(bf16[16,144,512]{2,1,0:T(8,128)(2,1)} %collective-permute-done, s32[]{:T(128)S(6)} %select_n.67, bf16[16,2,128,512]{3,2,1,0:T(8,128)(2,1)} %bitcast.41, bf16[16,2,16,512]{3,2,1,0:T(8,128)(2,1)S(1)} %bitcast.44), kind=kLoop, calls=%fused_computation.3 | loop fusion | flops 9437184 | bytes 9437188 | tf_op jit(solution)/shard_map/convert_element_type | solution.py:361
  83.0 35.6 %all_to_all.10 = bf16[16,144,512]{2,1,0:T(8,128)(2,1)S(1)} all-to-all(bf16[16,144,512]{2,1,0:T(8,128)(2,1)S(1)} %fusion), channel_id=1, replica_groups={{0,8,16,24,32,40,48,56,64,72,80,88,96,104,112,120},{4,12,20,28,36,44,52..., dimensions={0} | all-to-all | bytes 4718592 | tf_op jit(solution)/shard_map/all_to_all | solution.py:363
  118.7 0.1 fusion.23
  118.8 0.1 fusion.31
  118.8 0.1 broadcast_in_dim.123
  119.0 0.1 eq.115
  119.1 0.6 select_reduce_fusion
  119.7 0.3 convert_reduce_fusion
  120.0 1.4 %fusion.5 = f32[1,2,64,512]{3,2,1,0:T(8,128)} fusion(f32[2,64,512]{2,1,0:T(8,128)S(1)} %bitcast.46, f32[512,512,1]{1,0,2:T(8,128)S(1)} %copy-done, f32[2]{0:T(128)S(1)} %broadcast_add_fusion), kind=kOutput, calls=%fused_computation.12 | convolution fusion | flops 402718720 | bytes 1572872 | tf_op jit(solution)/shard_map/dot_general | solution.py:367
  (23 shorter events, 0.6 us)
Async XLA Ops:
  2.0 15.8 %all-to-all-start = ((s32[32,128,3]{1,2,0:T(4,128)}), s32[32,128,3]{1,2,0:T(4,128)S(1)}, u32[]{:S(2)}, u32[]{:S(2)}) async-start(s32[32,128,3]{1,2,0:T(4,128)} %broadcast_in_dim.111), calls=%async_computation | async-start | bytes 131072 | tf_op jit(solution)/shard_map/all_to_all | solution.py:239
  20.4 22.5 %copy-start.1 = (f32[36,512]{1,0:T(8,128)S(1)}, f32[36,512]{1,0:T(8,128)}, u32[]{:S(2)}) copy-start(f32[36,512]{1,0:T(8,128)} %param.14) | copy-start | bytes 221188
  72.9 7.0 %collective-permute-start = (bf16[16,144,512]{2,1,0:T(8,128)(2,1)S(1)}, bf16[16,144,512]{2,1,0:T(8,128)(2,1)}, u32[]{:S(2)}, u32[]{:S(2)}) collective-permute-start(bf16[16,144,512]{2,1,0:T(8,128)(2,1)S(1)} %fusion.2), channel_id=1, source_target_pairs={{0,4},{4,0},{8,12},{12,8},{16,20},{20,16},{24,28},{28,24},{32,36},... | collective-permute-start | bytes 7077896 | tf_op jit(solution)/shard_map/ppermute | solution.py:360
  83.0 37.1 %copy-start = (f32[512,512,1]{1,0,2:T(8,128)S(1)}, f32[512,512,1]{1,0,2:T(8,128)}, u32[]{:S(2)}) copy-start(f32[512,512,1]{1,0,2:T(8,128)} %constant.120) | copy-start | bytes 3145732

commit v13 on v12

--- a/solution.py
+++ b/solution.py
@@ -80,7 +80,8 @@
     def prep(p, cnt):
         slot = pose_ref[p]
         for a in range(LIST):
-            k = packed_ref[slot * (LIST + 1) + a] - first
+            block = slot // n_particle
+            k = packed_ref[(block * LIST + a) * n_particle + slot - block * n_particle] - first
             e = p * LIST + a
             class_ref[e] = k
             ins = jnp.logical_and(k >= 0, k < n_class)
@@ -235,10 +236,10 @@
     forward = jnp.asarray(full_table).astype(jnp.bfloat16)
     inverse = jnp.asarray(np.ascontiguousarray(full_table.T))
 
-    packed = jnp.concatenate([class_lists, pose_slot[:, None]], axis=1)
+    packed = class_lists.T
     all_packed = lax.all_to_all(
         jnp.broadcast_to(packed[None], (dp_count,) + packed.shape), "dp", 0, 0, tiled=True
-    ).reshape(dp_count * blocksize, LIST + 1)
+    )
     image_rows = images.shape[0] * NSHELL
     ref_rows = col_classes * NSHELL
     wrow = shell_weight[:, None]

time: 122 us -> 120 us (0.984)
  local copies, waits for them, and re-layouts: 7.62 us -> 6.29 us
    another operation x2 -> x1, local copies, waits for them, and re-layouts: 2.07 us -> 0.1 us  [the longest x1 1.97 us: local(): all_packed.reshape(-1)]
where the time goes in v13:
time: 120 us
  blocking collectives  44.7 us (37%)
  Pallas kernels  32.6 us (27%)
  other arithmetic  11.7 us (10%)
  starting transfers between devices  10.9 us (9%)
  waiting for transfers between devices  7.87 us (7%)
  local copies, waits for them, and re-layouts  6.29 us (5%)
  matrix products  4.88 us (4%)
    all_to_all x1, blocking collectives, local(): lax.all_to_all(pair_sum, 'dp', split_axis=0, concat_axis=0, tiled=True, a...  35.1 us
    pallas_call x1, Pallas kernels, local(): pl.pallas_call(cross_kernel, out_shape=(jax.ShapeDtypeStruct((entries, ro...  21.9 us
    pallas_call x1, Pallas kernels, local(): pl.pallas_call(grad_kernel, out_shape=jax.ShapeDtypeStruct((ref_rows, row...  10.7 us
    all_gather x1, blocking collectives, local(): gathered = lax.all_gather(jnp.stack([top_local, total_local]), 'cls')  9.62 us
    all_to_all x1, starting transfers between devices, local(): lax.all_to_all(jnp.broadcast_to(packed[None], (dp_count,) + packed.shape)...  8.24 us
    ppermute x1, waiting for transfers between devices, local(): taken = lax.ppermute(give, 'dp', perm=[(i, i ^ 1) for i in range(dp_count)])  4.29 us
    all_to_all x1, waiting for transfers between devices, local(): lax.all_to_all(jnp.broadcast_to(packed[None], (dp_count,) + packed.shape)...  3.58 us
    convert_element_type x1, other arithmetic, local(): pair_sum = (keep.astype(F32) + taken.astype(F32)).astype(jnp.bfloat16)  3.04 us
  transfers between devices with their start and end apart: 2, of which 2 were waited for; matrix products, arithmetic and copies ran while one was open for 3% of the time, Pallas kernels for 0%

profile of v13, /device:TPU:0, one launch (start us, length us, event | category | flops | bytes accessed | tf_op | source)
XLA Modules:
  0.0 119.8 jit_solution(10534486074571201991)
XLA Ops:
  0.6 1.3 %broadcast_in_dim.107 = s32[32,2,128]{2,1,0:T(2,128)} broadcast(s32[2,128]{1,0:T(2,128)} %bitcast.54), dimensions={1,2} | broadcast | bytes 33792 | tf_op jit(solution)/shard_map/broadcast_in_dim | solution.py:241
  1.9 8.2 %all-to-all-start = ((s32[32,2,128]{2,1,0:T(2,128)}), s32[32,2,128]{2,1,0:T(2,128)S(1)}, u32[]{:S(2)}, u32[]{:S(2)}) async-start(s32[32,2,128]{2,1,0:T(2,128)} %broadcast_in_dim.107), calls=%async_computation | async-start | bytes 65536 | tf_op jit(solution)/shard_map/all_to_all | solution.py:240
  10.2 0.8 fusion.30
  11.0 0.7 convert_log-plus-one_fusion
  11.7 0.7 and_select_fusion.3
  12.3 0.3 reduce_window_sum.11
  12.7 1.3 %copy.26.wrow_ref = f32[64,1]{1,0:T(8,128)} copy(f32[64,1]{0,1:T(1,128)} %bitcast.57) | data formatting | bytes 512 | tf_op jit(solution)/shard_map/broadcast_in_dim | solution.py:245
  14.0 3.6 %all-to-all-done = s32[32,2,128]{2,1,0:T(2,128)S(1)} async-done(((s32[32,2,128]{2,1,0:T(2,128)}), s32[32,2,128]{2,1,0:T(2,128)S(1)}, u32[]{:S(2)}, u32[]{:S(2)}) %all-to-all-start) | async-done | bytes 32800 | tf_op jit(solution)/shard_map/all_to_all | solution.py:240
  17.6 0.6 copy-done.2
  18.2 21.9 %shard_map.104 = (f32[256,512]{1,0:T(8,128)}, bf16[8192,512]{1,0:T(8,128)(2,1)}, bf16[4096,512]{1,0:T(8,128)(2,1)}, s32[1]{0:T(128)}, s32[256]{0:T(256)}, /*index=5*/s32[256]{0:T(256)}, s32[256]{0:T(256)}, s32[256]{0:T(256)}) custom-call(s32[8192]{0:T(1024)} %bitcast.48, s32[128]{0:T(128)} %pose_ref.1, s32[1]{0:T(128)} %bitcast.2.column_ref, ...), custom_call_target="tpu_custom_call" | custom-call | tf_op jit(solution)/shard_map/pallas_call | solution.py:248
  40.2 0.6 broadcast_clamp_fusion
  40.8 0.6 compare_and_fusion.1
  41.4 0.1 select_reduce_fusion.1
  41.5 1.6 %fusion.32 = (f32[256]{0:T(256)S(1)}, f32[256,36]{0,1:T(8,128)S(1)}) fusion(f32[256]{0:T(256)S(1)} %select_reduce_fusion.1, f32[256,512]{1,0:T(8,128)} %get-tuple-element.28, f32[36,512]{1,0:T(8,128)S(1)} %copy-done.1, pred[256]{0:T(512)(128)(4,1)S(1)} %compare_and_fusion.1), kind=kOutput, calls=%fused_computation.74 | convolution fusion | flops 56650496 | bytes 637184 | tf_op jit(solution)/shard_map/dot_general | solution.py:285
  43.2 0.1 reduce_max.26
  43.3 0.1 reduce_max.27
  43.4 0.1 sub.53
  43.5 0.2 sub.54
  43.7 0.1 reduce_sum.99
  43.8 0.1 reduce_sum.100
  44.0 9.6 %all-gather.1 = f32[4,2,128]{2,1,0:T(2,128)S(1)} all-gather(f32[1,2,128]{2,1,0:T(2,128)S(1)} %maximum_bitcast_fusion), channel_id=2, replica_groups=mesh['dp'=32,'cls'=4] {'cls'}, dimensions={0}, use_global_device_ids=true | all-gather | bytes 5120 | tf_op jit(solution)/shard_map/all_gather | solution.py:293
  53.6 0.1 div.34
  53.7 0.2 div.35
  53.9 0.1 sub.57
  53.9 0.2 sub.58
  54.1 0.8 fusion.9
  54.9 0.9 slice.73.coef_ref
  55.8 0.9 fusion.7
  56.7 0.7 pad_maximum_fusion.volume_ref
  57.4 0.1 fusion.16
  57.5 0.7 compare_and_fusion
  58.2 0.1 fusion.19
  58.4 0.1 concatenate.22
  58.5 0.1 copy.28
  58.7 0.6 dynamic_update_slice.6
  59.3 10.7 %shard_map.105 = bf16[4096,512]{1,0:T(8,128)(2,1)} custom-call(s32[1]{0:T(128)} %get-tuple-element.22.count_ref, s32[256]{0:T(256)} %get-tuple-element.23.ent_p_ref, s32[256]{0:T(256)} %get-tuple-element.24.ent_k_ref, s32[256]{0:T(256)} %get-tuple-element.25.ent_e_ref, bf16[8192,512]{1,0:T(8,128)(2,1)} %get-tuple-element.26.image_hat_hbm, ...), custom_call_target="tpu_custom_call" | custom-call | tf_op jit(solution)/shard_map/pallas_call | solution.py:316
  70.1 1.8 %fusion.2 = bf16[16,144,512]{2,1,0:T(8,128)(2,1)S(1)} fusion(s32[]{:T(128)S(6)} %select_n.68, bf16[16,2,128,512]{3,2,1,0:T(8,128)(2,1)} %bitcast.41, bf16[16,2,16,512]{3,2,1,0:T(8,128)(2,1)S(1)} %bitcast.44), kind=kLoop, calls=%fused_computation.8 | loop fusion | flops 4718592 | bytes 7077892 | tf_op jit(solution)/shard_map/jit(dynamic_index_in_dim)/squeeze | solution.py:360
  71.9 2.7 %collective-permute-start = (bf16[16,144,512]{2,1,0:T(8,128)(2,1)S(1)}, bf16[16,144,512]{2,1,0:T(8,128)(2,1)}, u32[]{:S(2)}, u32[]{:S(2)}) collective-permute-start(bf16[16,144,512]{2,1,0:T(8,128)(2,1)S(1)} %fusion.2), channel_id=1, source_target_pairs={{0,4},{4,0},{8,12},{12,8},{16,20},{20,16},{24,28},{28,24},{32,36},... | collective-permute-start | bytes 7077896 | tf_op jit(solution)/shard_map/ppermute | solution.py:361
  74.5 4.3 %collective-permute-done = bf16[16,144,512]{2,1,0:T(8,128)(2,1)} collective-permute-done((bf16[16,144,512]{2,1,0:T(8,128)(2,1)S(1)}, bf16[16,144,512]{2,1,0:T(8,128)(2,1)}, u32[]{:S(2)}, u32[]{:S(2)}) %collective-permute-start) | collective-permute-done | bytes 2359328 | tf_op jit(solution)/shard_map/ppermute | solution.py:361
  78.8 3.0 %fusion = bf16[16,144,512]{2,1,0:T(8,128)(2,1)S(1)} fusion(bf16[16,144,512]{2,1,0:T(8,128)(2,1)} %collective-permute-done, s32[]{:T(128)S(6)} %select_n.67, bf16[16,2,128,512]{3,2,1,0:T(8,128)(2,1)} %bitcast.42, bf16[16,2,16,512]{3,2,1,0:T(8,128)(2,1)S(1)} %bitcast.45), kind=kLoop, calls=%fused_computation.3 | loop fusion | flops 9437184 | bytes 9437188 | tf_op jit(solution)/shard_map/convert_element_type | solution.py:362
  81.9 35.1 %all_to_all.10 = bf16[16,144,512]{2,1,0:T(8,128)(2,1)S(1)} all-to-all(bf16[16,144,512]{2,1,0:T(8,128)(2,1)S(1)} %fusion), channel_id=1, replica_groups={{0,8,16,24,32,40,48,56,64,72,80,88,96,104,112,120},{4,12,20,28,36,44,52..., dimensions={0} | all-to-all | bytes 4718592 | tf_op jit(solution)/shard_map/all_to_all | solution.py:364
  117.1 0.1 fusion.23
  117.1 0.1 fusion.31
  117.2 0.1 broadcast_in_dim.119
  117.3 0.1 eq.115
  117.4 0.6 select_reduce_fusion
  118.1 0.3 convert_reduce_fusion
  118.4 1.4 %fusion.5 = f32[1,2,64,512]{3,2,1,0:T(8,128)} fusion(f32[2,64,512]{2,1,0:T(8,128)S(1)} %bitcast.47, f32[512,512,1]{1,0,2:T(8,128)S(1)} %copy-done, f32[2]{0:T(128)S(1)} %broadcast_add_fusion), kind=kOutput, calls=%fused_computation.12 | convolution fusion | flops 402718720 | bytes 1572872 | tf_op jit(solution)/shard_map/dot_general | solution.py:368
  (22 shorter events, 0.4 us)
Async XLA Ops:
  1.9 15.7 %all-to-all-start = ((s32[32,2,128]{2,1,0:T(2,128)}), s32[32,2,128]{2,1,0:T(2,128)S(1)}, u32[]{:S(2)}, u32[]{:S(2)}) async-start(s32[32,2,128]{2,1,0:T(2,128)} %broadcast_in_dim.107), calls=%async_computation | async-start | bytes 65536 | tf_op jit(solution)/shard_map/all_to_all | solution.py:240
  17.6 0.6 copy-start.2
  18.2 23.3 %copy-start.1 = (f32[36,512]{1,0:T(8,128)S(1)}, f32[36,512]{1,0:T(8,128)}, u32[]{:S(2)}) copy-start(f32[36,512]{1,0:T(8,128)} %param.14) | copy-start | bytes 221188
  71.9 7.0 %collective-permute-start = (bf16[16,144,512]{2,1,0:T(8,128)(2,1)S(1)}, bf16[16,144,512]{2,1,0:T(8,128)(2,1)}, u32[]{:S(2)}, u32[]{:S(2)}) collective-permute-start(bf16[16,144,512]{2,1,0:T(8,128)(2,1)S(1)} %fusion.2), channel_id=1, source_target_pairs={{0,4},{4,0},{8,12},{12,8},{16,20},{20,16},{24,28},{28,24},{32,36},... | collective-permute-start | bytes 7077896 | tf_op jit(solution)/shard_map/ppermute | solution.py:361
  81.9 36.5 %copy-start = (f32[512,512,1]{1,0,2:T(8,128)S(1)}, f32[512,512,1]{1,0,2:T(8,128)}, u32[]{:S(2)}) copy-start(f32[512,512,1]{1,0,2:T(8,128)} %constant.120) | copy-start | bytes 3145732

commit v14 on v13

--- a/solution.py
+++ b/solution.py
@@ -290,7 +290,11 @@
     total_local = jnp.sum(
         jnp.where(inside_pa[..., None], jnp.exp(scores - top_local[:, None, None]), 0.0), axis=(1, 2)
     )
-    gathered = lax.all_gather(jnp.stack([top_local, total_local]), "cls")
+    mine = jnp.stack([top_local, total_local])
+    slots_cls = jnp.arange(lax.axis_size("cls"), dtype=jnp.int32)
+    gathered = lax.psum(
+        jnp.where((slots_cls == column)[:, None, None], mine[None], 0.0), "cls"
+    )
     tops = gathered[:, 0]
     totals = gathered[:, 1]
     top_score = jnp.max(tops, axis=0)

time: 120 us -> 121 us (level)
  blocking collectives: 44.7 us -> 46.9 us
  Pallas kernels: 32.6 us -> 31 us
    psum x0 -> x1, blocking collectives: none -> 11.2 us  [local(): lax.psum(jnp.where((slots_cls == column)[:, None, None], mine[None], 0.0)...]
    all_gather x1 -> x0, blocking collectives: 9.62 us -> none  [local(): gathered = lax.all_gather(jnp.stack([top_local, total_local]), 'cls')]
where the time goes in v14:
time: 121 us
  blocking collectives  46.9 us (39%)
  Pallas kernels  31 us (26%)
  other arithmetic  11.8 us (10%)
  starting transfers between devices  11.2 us (9%)
  waiting for transfers between devices  7.85 us (6%)
  local copies, waits for them, and re-layouts  6.29 us (5%)
  matrix products  4.87 us (4%)
    all_to_all x1, blocking collectives, local(): lax.all_to_all(pair_sum, 'dp', split_axis=0, concat_axis=0, tiled=True, a...  35.6 us
    pallas_call x1, Pallas kernels, local(): pl.pallas_call(cross_kernel, out_shape=(jax.ShapeDtypeStruct((entries, ro...  20.9 us
    psum x1, blocking collectives, local(): lax.psum(jnp.where((slots_cls == column)[:, None, None], mine[None], 0.0)...  11.2 us
    pallas_call x1, Pallas kernels, local(): pl.pallas_call(grad_kernel, out_shape=jax.ShapeDtypeStruct((ref_rows, row...  10.1 us
    all_to_all x1, starting transfers between devices, local(): lax.all_to_all(jnp.broadcast_to(packed[None], (dp_count,) + packed.shape)...  8.24 us
    ppermute x1, waiting for transfers between devices, local(): taken = lax.ppermute(give, 'dp', perm=[(i, i ^ 1) for i in range(dp_count)])  4.29 us
    all_to_all x1, waiting for transfers between devices, local(): lax.all_to_all(jnp.broadcast_to(packed[None], (dp_count,) + packed.shape)...  3.56 us
    convert_element_type x1, other arithmetic, local(): pair_sum = (keep.astype(F32) + taken.astype(F32)).astype(jnp.bfloat16)  3.04 us
  transfers between devices with their start and end apart: 2, of which 2 were waited for; matrix products, arithmetic and copies ran while one was open for 3% of the time, Pallas kernels for 0%

profile of v14, /device:TPU:0, one launch (start us, length us, event | category | flops | bytes accessed | tf_op | source)
XLA Modules:
  0.0 120.7 jit_solution(10503436205276574270)
XLA Ops:
  0.6 1.3 %broadcast_in_dim.129 = s32[32,2,128]{2,1,0:T(2,128)} broadcast(s32[2,128]{1,0:T(2,128)} %bitcast.58), dimensions={1,2} | broadcast | bytes 33792 | tf_op jit(solution)/shard_map/broadcast_in_dim | solution.py:241
  1.9 8.2 %all-to-all-start = ((s32[32,2,128]{2,1,0:T(2,128)}), s32[32,2,128]{2,1,0:T(2,128)S(1)}, u32[]{:S(2)}, u32[]{:S(2)}) async-start(s32[32,2,128]{2,1,0:T(2,128)} %broadcast_in_dim.129), calls=%async_computation | async-start | bytes 65536 | tf_op jit(solution)/shard_map/all_to_all | solution.py:240
  10.2 0.8 fusion.33
  11.0 0.7 convert_log-plus-one_fusion
  11.7 0.7 and_select_fusion.3
  12.4 0.3 reduce_window_sum.11
  12.7 1.3 %copy.26.wrow_ref = f32[64,1]{1,0:T(8,128)} copy(f32[64,1]{0,1:T(1,128)} %bitcast.61) | data formatting | bytes 512 | tf_op jit(solution)/shard_map/broadcast_in_dim | solution.py:245
  14.1 3.6 %all-to-all-done = s32[32,2,128]{2,1,0:T(2,128)S(1)} async-done(((s32[32,2,128]{2,1,0:T(2,128)}), s32[32,2,128]{2,1,0:T(2,128)S(1)}, u32[]{:S(2)}, u32[]{:S(2)}) %all-to-all-start) | async-done | bytes 32800 | tf_op jit(solution)/shard_map/all_to_all | solution.py:240
  17.6 0.6 copy-done.2
  18.2 20.9 %shard_map.104 = (f32[256,512]{1,0:T(8,128)}, bf16[8192,512]{1,0:T(8,128)(2,1)}, bf16[4096,512]{1,0:T(8,128)(2,1)}, s32[1]{0:T(128)}, s32[256]{0:T(256)}, /*index=5*/s32[256]{0:T(256)}, s32[256]{0:T(256)}, s32[256]{0:T(256)}) custom-call(s32[8192]{0:T(1024)} %bitcast.54, s32[128]{0:T(128)} %pose_ref.1, s32[1]{0:T(128)} %bitcast.2.column_ref, ...), custom_call_target="tpu_custom_call" | custom-call | tf_op jit(solution)/shard_map/pallas_call | solution.py:248
  39.2 0.6 broadcast_clamp_fusion
  39.8 0.6 compare_and_fusion.1
  40.4 0.1 select_reduce_fusion.1
  40.5 1.6 %fusion.35 = (f32[256]{0:T(256)S(1)}, f32[256,36]{0,1:T(8,128)S(1)}) fusion(f32[256]{0:T(256)S(1)} %select_reduce_fusion.1, f32[256,512]{1,0:T(8,128)} %get-tuple-element.28, f32[36,512]{1,0:T(8,128)S(1)} %copy-done.1, pred[256]{0:T(512)(128)(4,1)S(1)} %compare_and_fusion.1), kind=kOutput, calls=%fused_computation.80 | convolution fusion | flops 56650496 | bytes 637184 | tf_op jit(solution)/shard_map/dot_general | solution.py:285
  42.2 0.1 reduce_max.26
  42.3 0.1 reduce_max.27
  42.4 0.1 sub.53
  42.5 0.2 sub.54
  42.7 0.1 reduce_sum.99
  42.8 0.1 reduce_sum.100
  43.0 11.2 %psum.7 = f32[4,2,128]{2,0,1:T(4,128)S(1)} all-reduce(f32[4,2,128]{2,0,1:T(4,128)S(1)} %broadcast_select_fusion), channel_id=1, replica_groups=mesh['dp'=32,'cls'=4] {'cls'}, use_global_device_ids=true, to_apply=%region_5.6 | all-reduce | flops 1024 | bytes 8192 | tf_op jit(solution)/shard_map/psum | solution.py:295
  54.3 0.1 div.34
  54.4 0.2 div.35
  54.5 0.1 sub.57
  54.6 0.2 sub.58
  54.8 0.8 fusion.9
  55.6 0.9 slice.73.coef_ref
  56.5 0.9 fusion.7
  57.4 0.7 pad_maximum_fusion.volume_ref
  58.0 0.1 fusion.16
  58.2 0.7 compare_and_fusion
  58.9 0.1 fusion.19
  59.1 0.1 concatenate.22
  59.2 0.1 copy.27
  59.3 0.6 dynamic_update_slice.6
  60.0 10.1 %shard_map.105 = bf16[4096,512]{1,0:T(8,128)(2,1)} custom-call(s32[1]{0:T(128)} %get-tuple-element.22.count_ref, s32[256]{0:T(256)} %get-tuple-element.23.ent_p_ref, s32[256]{0:T(256)} %get-tuple-element.24.ent_k_ref, s32[256]{0:T(256)} %get-tuple-element.25.ent_e_ref, bf16[8192,512]{1,0:T(8,128)(2,1)} %get-tuple-element.26.image_hat_hbm, ...), custom_call_target="tpu_custom_call" | custom-call | tf_op jit(solution)/shard_map/pallas_call | solution.py:320
  70.1 1.8 %fusion.2 = bf16[16,144,512]{2,1,0:T(8,128)(2,1)S(1)} fusion(s32[]{:T(128)S(6)} %select_n.73, bf16[16,2,128,512]{3,2,1,0:T(8,128)(2,1)} %bitcast.47, bf16[16,2,16,512]{3,2,1,0:T(8,128)(2,1)S(1)} %bitcast.50), kind=kLoop, calls=%fused_computation.8 | loop fusion | flops 4718592 | bytes 7077892 | tf_op jit(solution)/shard_map/jit(dynamic_index_in_dim)/squeeze | solution.py:364
  71.9 3.0 %collective-permute-start = (bf16[16,144,512]{2,1,0:T(8,128)(2,1)S(1)}, bf16[16,144,512]{2,1,0:T(8,128)(2,1)}, u32[]{:S(2)}, u32[]{:S(2)}) collective-permute-start(bf16[16,144,512]{2,1,0:T(8,128)(2,1)S(1)} %fusion.2), channel_id=1, source_target_pairs={{0,4},{4,0},{8,12},{12,8},{16,20},{20,16},{24,28},{28,24},{32,36},... | collective-permute-start | bytes 7077896 | tf_op jit(solution)/shard_map/ppermute | solution.py:365
  74.9 4.3 %collective-permute-done = bf16[16,144,512]{2,1,0:T(8,128)(2,1)} collective-permute-done((bf16[16,144,512]{2,1,0:T(8,128)(2,1)S(1)}, bf16[16,144,512]{2,1,0:T(8,128)(2,1)}, u32[]{:S(2)}, u32[]{:S(2)}) %collective-permute-start) | collective-permute-done | bytes 2359328 | tf_op jit(solution)/shard_map/ppermute | solution.py:365
  79.2 3.0 %fusion = bf16[16,144,512]{2,1,0:T(8,128)(2,1)S(1)} fusion(bf16[16,144,512]{2,1,0:T(8,128)(2,1)} %collective-permute-done, s32[]{:T(128)S(6)} %select_n.72, bf16[16,2,128,512]{3,2,1,0:T(8,128)(2,1)} %bitcast.48, bf16[16,2,16,512]{3,2,1,0:T(8,128)(2,1)S(1)} %bitcast.51), kind=kLoop, calls=%fused_computation.3 | loop fusion | flops 9437184 | bytes 9437188 | tf_op jit(solution)/shard_map/convert_element_type | solution.py:366
  82.2 35.6 %all_to_all.10 = bf16[16,144,512]{2,1,0:T(8,128)(2,1)S(1)} all-to-all(bf16[16,144,512]{2,1,0:T(8,128)(2,1)S(1)} %fusion), channel_id=1, replica_groups={{0,8,16,24,32,40,48,56,64,72,80,88,96,104,112,120},{4,12,20,28,36,44,52..., dimensions={0} | all-to-all | bytes 4718592 | tf_op jit(solution)/shard_map/all_to_all | solution.py:368
  118.0 0.1 fusion.23
  118.1 0.1 fusion.34
  118.1 0.1 broadcast_in_dim.144
  118.3 0.1 eq.127
  118.4 0.6 select_reduce_fusion
  119.0 0.3 convert_reduce_fusion
  119.3 1.4 %fusion.5 = f32[1,2,64,512]{3,2,1,0:T(8,128)} fusion(f32[2,64,512]{2,1,0:T(8,128)S(1)} %bitcast.53, f32[512,512,1]{1,0,2:T(8,128)S(1)} %copy-done, f32[2]{0:T(128)S(1)} %broadcast_add_fusion), kind=kOutput, calls=%fused_computation.12 | convolution fusion | flops 402718720 | bytes 1572872 | tf_op jit(solution)/shard_map/dot_general | solution.py:372
  (24 shorter events, 0.5 us)
Async XLA Ops:
  1.9 15.7 %all-to-all-start = ((s32[32,2,128]{2,1,0:T(2,128)}), s32[32,2,128]{2,1,0:T(2,128)S(1)}, u32[]{:S(2)}, u32[]{:S(2)}) async-start(s32[32,2,128]{2,1,0:T(2,128)} %broadcast_in_dim.129), calls=%async_computation | async-start | bytes 65536 | tf_op jit(solution)/shard_map/all_to_all | solution.py:240
  17.6 0.6 copy-start.2
  18.2 22.3 %copy-start.1 = (f32[36,512]{1,0:T(8,128)S(1)}, f32[36,512]{1,0:T(8,128)}, u32[]{:S(2)}) copy-start(f32[36,512]{1,0:T(8,128)} %param.14) | copy-start | bytes 221188
  71.9 7.3 %collective-permute-start = (bf16[16,144,512]{2,1,0:T(8,128)(2,1)S(1)}, bf16[16,144,512]{2,1,0:T(8,128)(2,1)}, u32[]{:S(2)}, u32[]{:S(2)}) collective-permute-start(bf16[16,144,512]{2,1,0:T(8,128)(2,1)S(1)} %fusion.2), channel_id=1, source_target_pairs={{0,4},{4,0},{8,12},{12,8},{16,20},{20,16},{24,28},{28,24},{32,36},... | collective-permute-start | bytes 7077896 | tf_op jit(solution)/shard_map/ppermute | solution.py:365
  82.2 37.1 %copy-start = (f32[512,512,1]{1,0,2:T(8,128)S(1)}, f32[512,512,1]{1,0,2:T(8,128)}, u32[]{:S(2)}) copy-start(f32[512,512,1]{1,0,2:T(8,128)} %constant.120) | copy-start | bytes 3145732

commit v15 on v13

--- a/solution.py
+++ b/solution.py
@@ -69,29 +69,17 @@
         loads.append(copy)
     first = column_ref[0] * n_class
 
-    def clear(e, carry):
-        ent_p_ref[e] = 0
-        ent_k_ref[e] = 0
-        ent_e_ref[e] = 0
-        return carry
-
-    lax.fori_loop(0, n_particle * LIST, clear, 0)
-
     def prep(p, cnt):
         slot = pose_ref[p]
+        block = slot // n_particle
         for a in range(LIST):
-            block = slot // n_particle
             k = packed_ref[(block * LIST + a) * n_particle + slot - block * n_particle] - first
             e = p * LIST + a
             class_ref[e] = k
             ins = jnp.logical_and(k >= 0, k < n_class)
-
-            @pl.when(ins)
-            def _():
-                ent_p_ref[cnt] = p
-                ent_k_ref[cnt] = k
-                ent_e_ref[cnt] = e
-
+            ent_p_ref[cnt] = p
+            ent_k_ref[cnt] = k
+            ent_e_ref[cnt] = e
             cnt = cnt + ins.astype(jnp.int32)
         return cnt
 

time: 120 us -> 118 us (0.983)
  Pallas kernels: 32.6 us -> 29.8 us
    pallas_call x1, Pallas kernels: 21.9 us -> 19.3 us  [local(): pl.pallas_call(cross_kernel, out_shape=(jax.ShapeDtypeStruct((entries, ro...]
where the time goes in v15:
time: 118 us; the launch traced here: 117 us
  blocking collectives  44.2 us (37%)
  Pallas kernels  29.8 us (25%)
  other arithmetic  11.7 us (10%)
  starting transfers between devices  11.3 us (10%)
  waiting for transfers between devices  7.87 us (7%)
  local copies, waits for them, and re-layouts  6.29 us (5%)
  matrix products  4.88 us (4%)
    all_to_all x1, blocking collectives, local(): lax.all_to_all(pair_sum, 'dp', split_axis=0, concat_axis=0, tiled=True, a...  34.7 us
    pallas_call x1, Pallas kernels, local(): pl.pallas_call(cross_kernel, out_shape=(jax.ShapeDtypeStruct((entries, ro...  19.3 us
    pallas_call x1, Pallas kernels, local(): pl.pallas_call(grad_kernel, out_shape=jax.ShapeDtypeStruct((ref_rows, row...  10.5 us
    all_gather x1, blocking collectives, local(): gathered = lax.all_gather(jnp.stack([top_local, total_local]), 'cls')  9.53 us
    all_to_all x1, starting transfers between devices, local(): lax.all_to_all(jnp.broadcast_to(packed[None], (dp_count,) + packed.shape)...  8.24 us
    ppermute x1, waiting for transfers between devices, local(): taken = lax.ppermute(give, 'dp', perm=[(i, i ^ 1) for i in range(dp_count)])  4.29 us
    all_to_all x1, waiting for transfers between devices, local(): lax.all_to_all(jnp.broadcast_to(packed[None], (dp_count,) + packed.shape)...  3.58 us
    ppermute x1, starting transfers between devices, local(): taken = lax.ppermute(give, 'dp', perm=[(i, i ^ 1) for i in range(dp_count)])  3.05 us
  transfers between devices with their start and end apart: 2, of which 2 were waited for; matrix products, arithmetic and copies ran while one was open for 3% of the time, Pallas kernels for 0%

profile of v15, /device:TPU:0, one launch (start us, length us, event | category | flops | bytes accessed | tf_op | source)
XLA Modules:
  0.0 116.9 jit_solution(8665737157635736533)
XLA Ops:
  0.6 1.3 %broadcast_in_dim.107 = s32[32,2,128]{2,1,0:T(2,128)} broadcast(s32[2,128]{1,0:T(2,128)} %bitcast.54), dimensions={1,2} | broadcast | bytes 33792 | tf_op jit(solution)/shard_map/broadcast_in_dim | solution.py:229
  1.9 8.2 %all-to-all-start = ((s32[32,2,128]{2,1,0:T(2,128)}), s32[32,2,128]{2,1,0:T(2,128)S(1)}, u32[]{:S(2)}, u32[]{:S(2)}) async-start(s32[32,2,128]{2,1,0:T(2,128)} %broadcast_in_dim.107), calls=%async_computation | async-start | bytes 65536 | tf_op jit(solution)/shard_map/all_to_all | solution.py:228
  10.2 0.8 fusion.30
  11.0 0.7 convert_log-plus-one_fusion
  11.7 0.7 and_select_fusion.3
  12.3 0.3 reduce_window_sum.11
  12.7 1.3 %copy.26.wrow_ref = f32[64,1]{1,0:T(8,128)} copy(f32[64,1]{0,1:T(1,128)} %bitcast.57) | data formatting | bytes 512 | tf_op jit(solution)/shard_map/broadcast_in_dim | solution.py:233
  14.0 3.6 %all-to-all-done = s32[32,2,128]{2,1,0:T(2,128)S(1)} async-done(((s32[32,2,128]{2,1,0:T(2,128)}), s32[32,2,128]{2,1,0:T(2,128)S(1)}, u32[]{:S(2)}, u32[]{:S(2)}) %all-to-all-start) | async-done | bytes 32800 | tf_op jit(solution)/shard_map/all_to_all | solution.py:228
  17.6 0.6 copy-done.2
  18.2 19.3 %shard_map.104 = (f32[256,512]{1,0:T(8,128)}, bf16[8192,512]{1,0:T(8,128)(2,1)}, bf16[4096,512]{1,0:T(8,128)(2,1)}, s32[1]{0:T(128)}, s32[256]{0:T(256)}, /*index=5*/s32[256]{0:T(256)}, s32[256]{0:T(256)}, s32[256]{0:T(256)}) custom-call(s32[8192]{0:T(1024)} %bitcast.48, s32[128]{0:T(128)} %pose_ref.1, s32[1]{0:T(128)} %bitcast.2.column_ref, ...), custom_call_target="tpu_custom_call" | custom-call | tf_op jit(solution)/shard_map/pallas_call | solution.py:236
  37.6 0.6 broadcast_clamp_fusion
  38.2 0.6 compare_and_fusion.1
  38.8 0.1 select_reduce_fusion.1
  38.9 1.6 %fusion.32 = (f32[256]{0:T(256)S(1)}, f32[256,36]{0,1:T(8,128)S(1)}) fusion(f32[256]{0:T(256)S(1)} %select_reduce_fusion.1, f32[256,512]{1,0:T(8,128)} %get-tuple-element.28, f32[36,512]{1,0:T(8,128)S(1)} %copy-done.1, pred[256]{0:T(512)(128)(4,1)S(1)} %compare_and_fusion.1), kind=kOutput, calls=%fused_computation.74 | convolution fusion | flops 56650496 | bytes 637184 | tf_op jit(solution)/shard_map/dot_general | solution.py:273
  40.6 0.1 reduce_max.26
  40.7 0.1 reduce_max.27
  40.8 0.1 sub.53
  40.9 0.2 sub.54
  41.1 0.1 reduce_sum.99
  41.3 0.1 reduce_sum.100
  41.4 9.5 %all-gather.1 = f32[4,2,128]{2,1,0:T(2,128)S(1)} all-gather(f32[1,2,128]{2,1,0:T(2,128)S(1)} %maximum_bitcast_fusion), channel_id=2, replica_groups=mesh['dp'=32,'cls'=4] {'cls'}, dimensions={0}, use_global_device_ids=true | all-gather | bytes 5120 | tf_op jit(solution)/shard_map/all_gather | solution.py:281
  51.0 0.1 div.34
  51.0 0.2 div.35
  51.2 0.1 sub.57
  51.3 0.2 sub.58
  51.4 0.8 fusion.9
  52.3 0.9 slice.73.coef_ref
  53.1 0.9 fusion.7
  54.0 0.7 pad_maximum_fusion.volume_ref
  54.7 0.1 fusion.16
  54.8 0.7 compare_and_fusion
  55.6 0.1 fusion.19
  55.7 0.1 concatenate.22
  55.8 0.1 copy.28
  56.0 0.6 dynamic_update_slice.6
  56.7 10.5 %shard_map.105 = bf16[4096,512]{1,0:T(8,128)(2,1)} custom-call(s32[1]{0:T(128)} %get-tuple-element.22.count_ref, s32[256]{0:T(256)} %get-tuple-element.23.ent_p_ref, s32[256]{0:T(256)} %get-tuple-element.24.ent_k_ref, s32[256]{0:T(256)} %get-tuple-element.25.ent_e_ref, bf16[8192,512]{1,0:T(8,128)(2,1)} %get-tuple-element.26.image_hat_hbm, ...), custom_call_target="tpu_custom_call" | custom-call | tf_op jit(solution)/shard_map/pallas_call | solution.py:304
  67.1 1.8 %fusion.2 = bf16[16,144,512]{2,1,0:T(8,128)(2,1)S(1)} fusion(s32[]{:T(128)S(6)} %select_n.68, bf16[16,2,128,512]{3,2,1,0:T(8,128)(2,1)} %bitcast.41, bf16[16,2,16,512]{3,2,1,0:T(8,128)(2,1)S(1)} %bitcast.44), kind=kLoop, calls=%fused_computation.8 | loop fusion | flops 4718592 | bytes 7077892 | tf_op jit(solution)/shard_map/jit(dynamic_index_in_dim)/squeeze | solution.py:348
  69.0 3.0 %collective-permute-start = (bf16[16,144,512]{2,1,0:T(8,128)(2,1)S(1)}, bf16[16,144,512]{2,1,0:T(8,128)(2,1)}, u32[]{:S(2)}, u32[]{:S(2)}) collective-permute-start(bf16[16,144,512]{2,1,0:T(8,128)(2,1)S(1)} %fusion.2), channel_id=1, source_target_pairs={{0,4},{4,0},{8,12},{12,8},{16,20},{20,16},{24,28},{28,24},{32,36},... | collective-permute-start | bytes 7077896 | tf_op jit(solution)/shard_map/ppermute | solution.py:349
  72.0 4.3 %collective-permute-done = bf16[16,144,512]{2,1,0:T(8,128)(2,1)} collective-permute-done((bf16[16,144,512]{2,1,0:T(8,128)(2,1)S(1)}, bf16[16,144,512]{2,1,0:T(8,128)(2,1)}, u32[]{:S(2)}, u32[]{:S(2)}) %collective-permute-start) | collective-permute-done | bytes 2359328 | tf_op jit(solution)/shard_map/ppermute | solution.py:349
  76.3 3.0 %fusion = bf16[16,144,512]{2,1,0:T(8,128)(2,1)S(1)} fusion(bf16[16,144,512]{2,1,0:T(8,128)(2,1)} %collective-permute-done, s32[]{:T(128)S(6)} %select_n.67, bf16[16,2,128,512]{3,2,1,0:T(8,128)(2,1)} %bitcast.42, bf16[16,2,16,512]{3,2,1,0:T(8,128)(2,1)S(1)} %bitcast.45), kind=kLoop, calls=%fused_computation.3 | loop fusion | flops 9437184 | bytes 9437188 | tf_op jit(solution)/shard_map/convert_element_type | solution.py:350
  79.4 34.7 %all_to_all.10 = bf16[16,144,512]{2,1,0:T(8,128)(2,1)S(1)} all-to-all(bf16[16,144,512]{2,1,0:T(8,128)(2,1)S(1)} %fusion), channel_id=1, replica_groups={{0,8,16,24,32,40,48,56,64,72,80,88,96,104,112,120},{4,12,20,28,36,44,52..., dimensions={0} | all-to-all | bytes 4718592 | tf_op jit(solution)/shard_map/all_to_all | solution.py:352
  114.1 0.1 fusion.23
  114.2 0.1 fusion.31
  114.3 0.1 broadcast_in_dim.119
  114.4 0.1 eq.115
  114.5 0.6 select_reduce_fusion
  115.1 0.3 convert_reduce_fusion
  115.5 1.4 %fusion.5 = f32[1,2,64,512]{3,2,1,0:T(8,128)} fusion(f32[2,64,512]{2,1,0:T(8,128)S(1)} %bitcast.47, f32[512,512,1]{1,0,2:T(8,128)S(1)} %copy-done, f32[2]{0:T(128)S(1)} %broadcast_add_fusion), kind=kOutput, calls=%fused_computation.12 | convolution fusion | flops 402718720 | bytes 1572872 | tf_op jit(solution)/shard_map/dot_general | solution.py:356
  (22 shorter events, 0.4 us)
Async XLA Ops:
  1.9 15.7 %all-to-all-start = ((s32[32,2,128]{2,1,0:T(2,128)}), s32[32,2,128]{2,1,0:T(2,128)S(1)}, u32[]{:S(2)}, u32[]{:S(2)}) async-start(s32[32,2,128]{2,1,0:T(2,128)} %broadcast_in_dim.107), calls=%async_computation | async-start | bytes 65536 | tf_op jit(solution)/shard_map/all_to_all | solution.py:228
  17.6 0.6 copy-start.2
  18.2 20.7 %copy-start.1 = (f32[36,512]{1,0:T(8,128)S(1)}, f32[36,512]{1,0:T(8,128)}, u32[]{:S(2)}) copy-start(f32[36,512]{1,0:T(8,128)} %param.14) | copy-start | bytes 221188
  69.0 7.3 %collective-permute-start = (bf16[16,144,512]{2,1,0:T(8,128)(2,1)S(1)}, bf16[16,144,512]{2,1,0:T(8,128)(2,1)}, u32[]{:S(2)}, u32[]{:S(2)}) collective-permute-start(bf16[16,144,512]{2,1,0:T(8,128)(2,1)S(1)} %fusion.2), channel_id=1, source_target_pairs={{0,4},{4,0},{8,12},{12,8},{16,20},{20,16},{24,28},{28,24},{32,36},... | collective-permute-start | bytes 7077896 | tf_op jit(solution)/shard_map/ppermute | solution.py:349
  79.3 36.1 %copy-start = (f32[512,512,1]{1,0,2:T(8,128)S(1)}, f32[512,512,1]{1,0,2:T(8,128)}, u32[]{:S(2)}) copy-start(f32[512,512,1]{1,0,2:T(8,128)} %constant.120) | copy-start | bytes 3145732

commit v16 on v15

--- a/solution.py
+++ b/solution.py
@@ -151,18 +151,7 @@
         copy.start()
         loads.append(copy)
 
-    for c in range(n_ref):
-        loads[c].wait()
-
-        def init(i, carry, c=c):
-            k = c * chunk_classes + i
-            r = pl.multiple_of(k * NSHELL, NSHELL)
-            acc_ref[pl.ds(r, NSHELL), :] = -volume_ref[pl.ds(k, 1), :] * ref_buf[
-                pl.ds(r, NSHELL), :
-            ].astype(F32)
-            return carry
-
-        lax.fori_loop(0, chunk_classes, init, 0)
+    acc_ref[...] = jnp.zeros_like(acc_ref)
     for c in range(n_image):
         loads[n_ref + c].wait()
 
@@ -186,7 +175,11 @@
 
     stores = []
     for c in range(n_ref):
-        out_buf[rows(c)] = acc_ref[rows(c)].astype(jnp.bfloat16)
+        loads[c].wait()
+        vol = volume_ref[pl.ds(c * chunk_classes, chunk_classes), :][:, None, :]
+        ref_part = ref_buf[rows(c)].astype(F32).reshape(chunk_classes, NSHELL, -1)
+        acc_part = acc_ref[rows(c)].reshape(chunk_classes, NSHELL, -1)
+        out_buf[rows(c)] = (acc_part - vol * ref_part).reshape(CHUNK, -1).astype(jnp.bfloat16)
         copy = pltpu.make_async_copy(out_buf.at[rows(c)], out_hbm.at[rows(c)], out_sem.at[c])
         copy.start()
         stores.append(copy)

time: 118 us -> 118 us (level)
  no operation moved by 1% of the time
where the time goes in v16:
time: 118 us; the launch traced here: 117 us
  blocking collectives  44.3 us (38%)
  Pallas kernels  30.5 us (26%)
  other arithmetic  11.7 us (10%)
  starting transfers between devices  10.8 us (9%)
  waiting for transfers between devices  7.87 us (7%)
  local copies, waits for them, and re-layouts  6.29 us (5%)
  matrix products  4.88 us (4%)
    all_to_all x1, blocking collectives, local(): lax.all_to_all(pair_sum, 'dp', split_axis=0, concat_axis=0, tiled=True, a...  35.1 us
    pallas_call x1, Pallas kernels, local(): pl.pallas_call(cross_kernel, out_shape=(jax.ShapeDtypeStruct((entries, ro...  19.7 us
    pallas_call x1, Pallas kernels, local(): pl.pallas_call(grad_kernel, out_shape=jax.ShapeDtypeStruct((ref_rows, row...  10.8 us
    all_gather x1, blocking collectives, local(): gathered = lax.all_gather(jnp.stack([top_local, total_local]), 'cls')  9.17 us
    all_to_all x1, starting transfers between devices, local(): lax.all_to_all(jnp.broadcast_to(packed[None], (dp_count,) + packed.shape)...  8.24 us
    ppermute x1, waiting for transfers between devices, local(): taken = lax.ppermute(give, 'dp', perm=[(i, i ^ 1) for i in range(dp_count)])  4.29 us
    all_to_all x1, waiting for transfers between devices, local(): lax.all_to_all(jnp.broadcast_to(packed[None], (dp_count,) + packed.shape)...  3.58 us
    convert_element_type x1, other arithmetic, local(): pair_sum = (keep.astype(F32) + taken.astype(F32)).astype(jnp.bfloat16)  3.04 us
  transfers between devices with their start and end apart: 2, of which 2 were waited for; matrix products, arithmetic and copies ran while one was open for 3% of the time, Pallas kernels for 0%

profile of v16, /device:TPU:0, one launch (start us, length us, event | category | flops | bytes accessed | tf_op | source)
XLA Modules:
  0.0 117.2 jit_solution(14397647862876697676)
XLA Ops:
  0.6 1.3 %broadcast_in_dim.107 = s32[32,2,128]{2,1,0:T(2,128)} broadcast(s32[2,128]{1,0:T(2,128)} %bitcast.54), dimensions={1,2} | broadcast | bytes 33792 | tf_op jit(solution)/shard_map/broadcast_in_dim | solution.py:222
  1.9 8.2 %all-to-all-start = ((s32[32,2,128]{2,1,0:T(2,128)}), s32[32,2,128]{2,1,0:T(2,128)S(1)}, u32[]{:S(2)}, u32[]{:S(2)}) async-start(s32[32,2,128]{2,1,0:T(2,128)} %broadcast_in_dim.107), calls=%async_computation | async-start | bytes 65536 | tf_op jit(solution)/shard_map/all_to_all | solution.py:221
  10.2 0.8 fusion.30
  11.0 0.7 convert_log-plus-one_fusion
  11.7 0.7 and_select_fusion.3
  12.3 0.3 reduce_window_sum.11
  12.7 1.3 %copy.26.wrow_ref = f32[64,1]{1,0:T(8,128)} copy(f32[64,1]{0,1:T(1,128)} %bitcast.57) | data formatting | bytes 512 | tf_op jit(solution)/shard_map/broadcast_in_dim | solution.py:226
  14.0 3.6 %all-to-all-done = s32[32,2,128]{2,1,0:T(2,128)S(1)} async-done(((s32[32,2,128]{2,1,0:T(2,128)}), s32[32,2,128]{2,1,0:T(2,128)S(1)}, u32[]{:S(2)}, u32[]{:S(2)}) %all-to-all-start) | async-done | bytes 32800 | tf_op jit(solution)/shard_map/all_to_all | solution.py:221
  17.6 0.6 copy-done.2
  18.2 19.7 %shard_map.104 = (f32[256,512]{1,0:T(8,128)}, bf16[8192,512]{1,0:T(8,128)(2,1)}, bf16[4096,512]{1,0:T(8,128)(2,1)}, s32[1]{0:T(128)}, s32[256]{0:T(256)}, /*index=5*/s32[256]{0:T(256)}, s32[256]{0:T(256)}, s32[256]{0:T(256)}) custom-call(s32[8192]{0:T(1024)} %bitcast.48, s32[128]{0:T(128)} %pose_ref.1, s32[1]{0:T(128)} %bitcast.2.column_ref, ...), custom_call_target="tpu_custom_call" | custom-call | tf_op jit(solution)/shard_map/pallas_call | solution.py:229
  37.9 0.6 broadcast_clamp_fusion
  38.6 0.6 compare_and_fusion.1
  39.2 0.1 select_reduce_fusion.1
  39.3 1.6 %fusion.32 = (f32[256]{0:T(256)S(1)}, f32[256,36]{0,1:T(8,128)S(1)}) fusion(f32[256]{0:T(256)S(1)} %select_reduce_fusion.1, f32[256,512]{1,0:T(8,128)} %get-tuple-element.28, f32[36,512]{1,0:T(8,128)S(1)} %copy-done.1, pred[256]{0:T(512)(128)(4,1)S(1)} %compare_and_fusion.1), kind=kOutput, calls=%fused_computation.74 | convolution fusion | flops 56650496 | bytes 637184 | tf_op jit(solution)/shard_map/dot_general | solution.py:266
  40.9 0.1 reduce_max.26
  41.1 0.1 reduce_max.27
  41.2 0.1 sub.53
  41.3 0.2 sub.54
  41.5 0.1 reduce_sum.99
  41.6 0.1 reduce_sum.100
  41.7 9.2 %all-gather.1 = f32[4,2,128]{2,1,0:T(2,128)S(1)} all-gather(f32[1,2,128]{2,1,0:T(2,128)S(1)} %maximum_bitcast_fusion), channel_id=2, replica_groups=mesh['dp'=32,'cls'=4] {'cls'}, dimensions={0}, use_global_device_ids=true | all-gather | bytes 5120 | tf_op jit(solution)/shard_map/all_gather | solution.py:274
  51.0 0.1 div.34
  51.0 0.2 div.35
  51.2 0.1 sub.57
  51.3 0.2 sub.58
  51.4 0.8 fusion.9
  52.3 0.9 slice.73.coef_ref
  53.1 0.9 fusion.7
  54.0 0.7 pad_maximum_fusion.volume_ref
  54.7 0.1 fusion.16
  54.8 0.7 compare_and_fusion
  55.6 0.1 fusion.19
  55.7 0.1 concatenate.22
  55.8 0.1 copy.28
  56.0 0.6 dynamic_update_slice.6
  56.7 10.8 %shard_map.105 = bf16[4096,512]{1,0:T(8,128)(2,1)} custom-call(s32[1]{0:T(128)} %get-tuple-element.22.count_ref, s32[256]{0:T(256)} %get-tuple-element.23.ent_p_ref, s32[256]{0:T(256)} %get-tuple-element.24.ent_k_ref, s32[256]{0:T(256)} %get-tuple-element.25.ent_e_ref, bf16[8192,512]{1,0:T(8,128)(2,1)} %get-tuple-element.26.image_hat_hbm, ...), custom_call_target="tpu_custom_call" | custom-call | tf_op jit(solution)/shard_map/pallas_call | solution.py:297
  67.5 1.8 %fusion.2 = bf16[16,144,512]{2,1,0:T(8,128)(2,1)S(1)} fusion(s32[]{:T(128)S(6)} %select_n.68, bf16[16,2,128,512]{3,2,1,0:T(8,128)(2,1)} %bitcast.41, bf16[16,2,16,512]{3,2,1,0:T(8,128)(2,1)S(1)} %bitcast.44), kind=kLoop, calls=%fused_computation.8 | loop fusion | flops 4718592 | bytes 7077892 | tf_op jit(solution)/shard_map/jit(dynamic_index_in_dim)/squeeze | solution.py:341
  69.3 2.6 %collective-permute-start = (bf16[16,144,512]{2,1,0:T(8,128)(2,1)S(1)}, bf16[16,144,512]{2,1,0:T(8,128)(2,1)}, u32[]{:S(2)}, u32[]{:S(2)}) collective-permute-start(bf16[16,144,512]{2,1,0:T(8,128)(2,1)S(1)} %fusion.2), channel_id=1, source_target_pairs={{0,4},{4,0},{8,12},{12,8},{16,20},{20,16},{24,28},{28,24},{32,36},... | collective-permute-start | bytes 7077896 | tf_op jit(solution)/shard_map/ppermute | solution.py:342
  71.9 4.3 %collective-permute-done = bf16[16,144,512]{2,1,0:T(8,128)(2,1)} collective-permute-done((bf16[16,144,512]{2,1,0:T(8,128)(2,1)S(1)}, bf16[16,144,512]{2,1,0:T(8,128)(2,1)}, u32[]{:S(2)}, u32[]{:S(2)}) %collective-permute-start) | collective-permute-done | bytes 2359328 | tf_op jit(solution)/shard_map/ppermute | solution.py:342
  76.2 3.0 %fusion = bf16[16,144,512]{2,1,0:T(8,128)(2,1)S(1)} fusion(bf16[16,144,512]{2,1,0:T(8,128)(2,1)} %collective-permute-done, s32[]{:T(128)S(6)} %select_n.67, bf16[16,2,128,512]{3,2,1,0:T(8,128)(2,1)} %bitcast.42, bf16[16,2,16,512]{3,2,1,0:T(8,128)(2,1)S(1)} %bitcast.45), kind=kLoop, calls=%fused_computation.3 | loop fusion | flops 9437184 | bytes 9437188 | tf_op jit(solution)/shard_map/convert_element_type | solution.py:343
  79.2 35.1 %all_to_all.10 = bf16[16,144,512]{2,1,0:T(8,128)(2,1)S(1)} all-to-all(bf16[16,144,512]{2,1,0:T(8,128)(2,1)S(1)} %fusion), channel_id=1, replica_groups={{0,8,16,24,32,40,48,56,64,72,80,88,96,104,112,120},{4,12,20,28,36,44,52..., dimensions={0} | all-to-all | bytes 4718592 | tf_op jit(solution)/shard_map/all_to_all | solution.py:345
  114.4 0.1 fusion.23
  114.5 0.1 fusion.31
  114.6 0.1 broadcast_in_dim.119
  114.7 0.1 eq.115
  114.8 0.6 select_reduce_fusion
  115.5 0.3 convert_reduce_fusion
  115.8 1.4 %fusion.5 = f32[1,2,64,512]{3,2,1,0:T(8,128)} fusion(f32[2,64,512]{2,1,0:T(8,128)S(1)} %bitcast.47, f32[512,512,1]{1,0,2:T(8,128)S(1)} %copy-done, f32[2]{0:T(128)S(1)} %broadcast_add_fusion), kind=kOutput, calls=%fused_computation.12 | convolution fusion | flops 402718720 | bytes 1572872 | tf_op jit(solution)/shard_map/dot_general | solution.py:349
  (22 shorter events, 0.4 us)
Async XLA Ops:
  1.9 15.7 %all-to-all-start = ((s32[32,2,128]{2,1,0:T(2,128)}), s32[32,2,128]{2,1,0:T(2,128)S(1)}, u32[]{:S(2)}, u32[]{:S(2)}) async-start(s32[32,2,128]{2,1,0:T(2,128)} %broadcast_in_dim.107), calls=%async_computation | async-start | bytes 65536 | tf_op jit(solution)/shard_map/all_to_all | solution.py:221
  17.6 0.6 copy-start.2
  18.2 21.1 %copy-start.1 = (f32[36,512]{1,0:T(8,128)S(1)}, f32[36,512]{1,0:T(8,128)}, u32[]{:S(2)}) copy-start(f32[36,512]{1,0:T(8,128)} %param.14) | copy-start | bytes 221188
  69.3 6.9 %collective-permute-start = (bf16[16,144,512]{2,1,0:T(8,128)(2,1)S(1)}, bf16[16,144,512]{2,1,0:T(8,128)(2,1)}, u32[]{:S(2)}, u32[]{:S(2)}) collective-permute-start(bf16[16,144,512]{2,1,0:T(8,128)(2,1)S(1)} %fusion.2), channel_id=1, source_target_pairs={{0,4},{4,0},{8,12},{12,8},{16,20},{20,16},{24,28},{28,24},{32,36},... | collective-permute-start | bytes 7077896 | tf_op jit(solution)/shard_map/ppermute | solution.py:342
  79.2 36.6 %copy-start = (f32[512,512,1]{1,0,2:T(8,128)S(1)}, f32[512,512,1]{1,0,2:T(8,128)}, u32[]{:S(2)}) copy-start(f32[512,512,1]{1,0,2:T(8,128)} %constant.120) | copy-start | bytes 3145732

commit v17 on v16

--- a/solution.py
+++ b/solution.py
@@ -159,7 +159,7 @@
         rp = pl.multiple_of(ent_p_ref[e] * NSHELL, NSHELL)
         rk = pl.multiple_of(ent_k_ref[e] * NSHELL, NSHELL)
         x = image_buf[pl.ds(rp, NSHELL), :].astype(F32)
-        c = coef_ref[pl.ds(ent_e_ref[e], 1), :]
+        c = coef_ref[pl.ds(ent_e_ref[e], 1), pl.ds(0, 2 * NANG)]
         c_re = c[:, :NANG]
         c_im = c[:, NANG:]
         x_re = x[:, :NANG]
@@ -176,7 +176,8 @@
     stores = []
     for c in range(n_ref):
         loads[c].wait()
-        vol = volume_ref[pl.ds(c * chunk_classes, chunk_classes), :][:, None, :]
+        vol_half = volume_ref[pl.ds(c * chunk_classes, chunk_classes), :]
+        vol = jnp.concatenate([vol_half, vol_half], axis=1)[:, None, :]
         ref_part = ref_buf[rows(c)].astype(F32).reshape(chunk_classes, NSHELL, -1)
         acc_part = acc_ref[rows(c)].reshape(chunk_classes, NSHELL, -1)
         out_buf[rows(c)] = (acc_part - vol * ref_part).reshape(CHUNK, -1).astype(jnp.bfloat16)
@@ -293,7 +294,6 @@
     ).astype(F32)
     volume = jnp.dot(class_pick, coef[:, row_width:], precision=HIGHEST)
     denom_part = jnp.dot(class_pick, post_sum, precision=HIGHEST)
-    volume_full = jnp.concatenate([volume, volume], axis=1)
     numer = pl.pallas_call(
         grad_kernel,
         out_shape=jax.ShapeDtypeStruct((ref_rows, row_width), jnp.bfloat16),
@@ -308,7 +308,7 @@
             pltpu.SemaphoreType.DMA((ref_rows // CHUNK,)),
         ],
         compiler_params=params,
-    )(count_arr, ent_p, ent_k, ent_e, image_hat, coef[:, :row_width], ref_hat, volume_full)
+    )(count_arr, ent_p, ent_k, ent_e, image_hat, coef, ref_hat, volume)
 
     core = dp_index % 2
     dest = pose_slot // blocksize

time: 118 us -> 117 us (level)
  no operation moved by 1% of the time
where the time goes in v17:
time: 117 us; the launch traced here: 116 us
  blocking collectives  45 us (38%)
  Pallas kernels  29.7 us (25%)
  other arithmetic  11 us (9%)
  starting transfers between devices  10.7 us (9%)
  waiting for transfers between devices  7.87 us (7%)
  matrix products  5.51 us (5%)
  local copies, waits for them, and re-layouts  5.44 us (5%)
    all_to_all x1, blocking collectives, local(): lax.all_to_all(pair_sum, 'dp', split_axis=0, concat_axis=0, tiled=True, a...  34.7 us
    pallas_call x1, Pallas kernels, local(): pl.pallas_call(cross_kernel, out_shape=(jax.ShapeDtypeStruct((entries, ro...  19.2 us
    pallas_call x1, Pallas kernels, local(): pl.pallas_call(grad_kernel, out_shape=jax.ShapeDtypeStruct((ref_rows, row...  10.5 us
    all_gather x1, blocking collectives, local(): gathered = lax.all_gather(jnp.stack([top_local, total_local]), 'cls')  10.3 us
    all_to_all x1, starting transfers between devices, local(): lax.all_to_all(jnp.broadcast_to(packed[None], (dp_count,) + packed.shape)...  8.24 us
    ppermute x1, waiting for transfers between devices, local(): taken = lax.ppermute(give, 'dp', perm=[(i, i ^ 1) for i in range(dp_count)])  4.29 us
    all_to_all x1, waiting for transfers between devices, local(): lax.all_to_all(jnp.broadcast_to(packed[None], (dp_count,) + packed.shape)...  3.58 us
    convert_element_type x1, other arithmetic, local(): pair_sum = (keep.astype(F32) + taken.astype(F32)).astype(jnp.bfloat16)  3.04 us
  transfers between devices with their start and end apart: 2, of which 2 were waited for; matrix products, arithmetic and copies ran while one was open for 3% of the time, Pallas kernels for 0%

profile of v17, /device:TPU:0, one launch (start us, length us, event | category | flops | bytes accessed | tf_op | source)
XLA Modules:
  0.0 116.2 jit_solution(5414993912167458419)
XLA Ops:
  0.6 1.3 %broadcast_in_dim.107 = s32[32,2,128]{2,1,0:T(2,128)} broadcast(s32[2,128]{1,0:T(2,128)} %bitcast.54), dimensions={1,2} | broadcast | bytes 33792 | tf_op jit(solution)/shard_map/broadcast_in_dim | solution.py:223
  1.9 8.2 %all-to-all-start = ((s32[32,2,128]{2,1,0:T(2,128)}), s32[32,2,128]{2,1,0:T(2,128)S(1)}, u32[]{:S(2)}, u32[]{:S(2)}) async-start(s32[32,2,128]{2,1,0:T(2,128)} %broadcast_in_dim.107), calls=%async_computation | async-start | bytes 65536 | tf_op jit(solution)/shard_map/all_to_all | solution.py:222
  10.2 0.8 fusion.30
  11.0 0.7 convert_log-plus-one_fusion
  11.7 0.7 and_select_fusion.3
  12.3 0.3 reduce_window_sum.11
  12.7 1.3 %copy.26.wrow_ref = f32[64,1]{1,0:T(8,128)} copy(f32[64,1]{0,1:T(1,128)} %bitcast.57) | data formatting | bytes 512 | tf_op jit(solution)/shard_map/broadcast_in_dim | solution.py:227
  14.0 3.6 %all-to-all-done = s32[32,2,128]{2,1,0:T(2,128)S(1)} async-done(((s32[32,2,128]{2,1,0:T(2,128)}), s32[32,2,128]{2,1,0:T(2,128)S(1)}, u32[]{:S(2)}, u32[]{:S(2)}) %all-to-all-start) | async-done | bytes 32800 | tf_op jit(solution)/shard_map/all_to_all | solution.py:222
  17.6 0.6 copy-done.3
  18.2 19.2 %shard_map.104 = (f32[256,512]{1,0:T(8,128)}, bf16[8192,512]{1,0:T(8,128)(2,1)}, bf16[4096,512]{1,0:T(8,128)(2,1)}, s32[1]{0:T(128)}, s32[256]{0:T(256)}, /*index=5*/s32[256]{0:T(256)}, s32[256]{0:T(256)}, s32[256]{0:T(256)}) custom-call(s32[8192]{0:T(1024)} %bitcast.48, s32[128]{0:T(128)} %pose_ref.1, s32[1]{0:T(128)} %bitcast.2.column_ref, ...), custom_call_target="tpu_custom_call" | custom-call | tf_op jit(solution)/shard_map/pallas_call | solution.py:230
  37.4 0.6 broadcast_clamp_fusion
  38.1 0.6 compare_and_fusion.1
  38.7 0.1 select_reduce_fusion.1
  38.8 1.6 %fusion.32 = (f32[256]{0:T(256)S(1)}, f32[256,36]{0,1:T(8,128)S(1)}) fusion(f32[256]{0:T(256)S(1)} %select_reduce_fusion.1, f32[256,512]{1,0:T(8,128)} %get-tuple-element.28, f32[36,512]{1,0:T(8,128)S(1)} %copy-done.2, pred[256]{0:T(512)(128)(4,1)S(1)} %compare_and_fusion.1), kind=kOutput, calls=%fused_computation.73 | convolution fusion | flops 56650496 | bytes 637184 | tf_op jit(solution)/shard_map/dot_general | solution.py:267
  40.4 0.1 reduce_max.26
  40.6 0.1 reduce_max.27
  40.7 0.1 sub.53
  40.8 0.2 sub.54
  41.0 0.1 reduce_sum.99
  41.1 0.1 reduce_sum.100
  41.2 10.3 %all-gather.1 = f32[4,2,128]{2,1,0:T(2,128)S(1)} all-gather(f32[1,2,128]{2,1,0:T(2,128)S(1)} %maximum_bitcast_fusion), channel_id=2, replica_groups=mesh['dp'=32,'cls'=4] {'cls'}, dimensions={0}, use_global_device_ids=true | all-gather | bytes 5120 | tf_op jit(solution)/shard_map/all_gather | solution.py:275
  51.6 0.1 div.34
  51.7 0.2 div.35
  51.8 0.1 sub.57
  51.9 0.2 sub.58
  52.1 0.8 fusion.9.coef_ref
  53.0 1.5 %fusion.7.volume_ref = f32[64,256]{1,0:T(8,128)} fusion(f32[256,768]{1,0:T(8,128)S(1)} %fusion.9.coef_ref, s32[256]{0:T(256)} %get-tuple-element.27, pred[256]{0:T(512)(128)(4,1)S(1)} %compare_and_fusion.1), kind=kOutput, calls=%fused_computation.15 | convolution fusion | flops 50364416 | bytes 329216 | tf_op jit(solution)/shard_map/dot_general | solution.py:295
  54.4 0.1 fusion.16
  54.6 0.7 compare_and_fusion
  55.3 0.1 fusion.19
  55.5 0.1 concatenate.18
  55.6 0.1 copy.28
  55.7 0.6 dynamic_update_slice.6
  56.3 0.1 scatter.4
  56.4 10.5 %shard_map.105 = bf16[4096,512]{1,0:T(8,128)(2,1)} custom-call(s32[1]{0:T(128)} %get-tuple-element.22.count_ref, s32[256]{0:T(256)} %get-tuple-element.23.ent_p_ref, s32[256]{0:T(256)} %get-tuple-element.24.ent_k_ref, s32[256]{0:T(256)} %get-tuple-element.25.ent_e_ref, bf16[8192,512]{1,0:T(8,128)(2,1)} %get-tuple-element.26.image_hat_hbm, ...), custom_call_target="tpu_custom_call" | custom-call | tf_op jit(solution)/shard_map/pallas_call | solution.py:297
  67.0 1.8 %fusion.2 = bf16[16,144,512]{2,1,0:T(8,128)(2,1)S(1)} fusion(s32[]{:T(128)S(6)} %select_n.68, bf16[16,2,128,512]{3,2,1,0:T(8,128)(2,1)} %bitcast.41, bf16[16,2,16,512]{3,2,1,0:T(8,128)(2,1)S(1)} %bitcast.44), kind=kLoop, calls=%fused_computation.8 | loop fusion | flops 4718592 | bytes 7077892 | tf_op jit(solution)/shard_map/jit(dynamic_index_in_dim)/squeeze | solution.py:341
  68.8 2.5 %collective-permute-start = (bf16[16,144,512]{2,1,0:T(8,128)(2,1)S(1)}, bf16[16,144,512]{2,1,0:T(8,128)(2,1)}, u32[]{:S(2)}, u32[]{:S(2)}) collective-permute-start(bf16[16,144,512]{2,1,0:T(8,128)(2,1)S(1)} %fusion.2), channel_id=1, source_target_pairs={{0,4},{4,0},{8,12},{12,8},{16,20},{20,16},{24,28},{28,24},{32,36},... | collective-permute-start | bytes 7077896 | tf_op jit(solution)/shard_map/ppermute | solution.py:342
  71.2 4.3 %collective-permute-done = bf16[16,144,512]{2,1,0:T(8,128)(2,1)} collective-permute-done((bf16[16,144,512]{2,1,0:T(8,128)(2,1)S(1)}, bf16[16,144,512]{2,1,0:T(8,128)(2,1)}, u32[]{:S(2)}, u32[]{:S(2)}) %collective-permute-start) | collective-permute-done | bytes 2359328 | tf_op jit(solution)/shard_map/ppermute | solution.py:342
  75.5 3.0 %fusion = bf16[16,144,512]{2,1,0:T(8,128)(2,1)S(1)} fusion(bf16[16,144,512]{2,1,0:T(8,128)(2,1)} %collective-permute-done, s32[]{:T(128)S(6)} %select_n.67, bf16[16,2,128,512]{3,2,1,0:T(8,128)(2,1)} %bitcast.42, bf16[16,2,16,512]{3,2,1,0:T(8,128)(2,1)S(1)} %bitcast.45), kind=kLoop, calls=%fused_computation.3 | loop fusion | flops 9437184 | bytes 9437188 | tf_op jit(solution)/shard_map/convert_element_type | solution.py:343
  78.6 34.7 %all_to_all.10 = bf16[16,144,512]{2,1,0:T(8,128)(2,1)S(1)} all-to-all(bf16[16,144,512]{2,1,0:T(8,128)(2,1)S(1)} %fusion), channel_id=1, replica_groups={{0,8,16,24,32,40,48,56,64,72,80,88,96,104,112,120},{4,12,20,28,36,44,52..., dimensions={0} | all-to-all | bytes 4718592 | tf_op jit(solution)/shard_map/all_to_all | solution.py:345
  113.4 0.1 reshape.180
  113.4 0.1 fusion.23
  113.5 0.1 fusion.31
  113.6 0.1 broadcast_in_dim.119
  113.7 0.1 eq.115
  113.8 0.6 select_reduce_fusion
  114.5 0.3 convert_reduce_fusion
  114.8 1.4 %fusion.5 = f32[1,2,64,512]{3,2,1,0:T(8,128)} fusion(f32[2,64,512]{2,1,0:T(8,128)S(1)} %bitcast.47, f32[512,512,1]{1,0,2:T(8,128)S(1)} %copy-done.1, f32[2]{0:T(128)S(1)} %broadcast_add_fusion), kind=kOutput, calls=%fused_computation.12 | convolution fusion | flops 402718720 | bytes 1572872 | tf_op jit(solution)/shard_map/dot_general | solution.py:349
  (22 shorter events, 0.3 us)
Async XLA Ops:
  1.9 15.7 %all-to-all-start = ((s32[32,2,128]{2,1,0:T(2,128)}), s32[32,2,128]{2,1,0:T(2,128)S(1)}, u32[]{:S(2)}, u32[]{:S(2)}) async-start(s32[32,2,128]{2,1,0:T(2,128)} %broadcast_in_dim.107), calls=%async_computation | async-start | bytes 65536 | tf_op jit(solution)/shard_map/all_to_all | solution.py:222
  17.6 0.6 copy-start.3
  18.2 20.6 %copy-start.2 = (f32[36,512]{1,0:T(8,128)S(1)}, f32[36,512]{1,0:T(8,128)}, u32[]{:S(2)}) copy-start(f32[36,512]{1,0:T(8,128)} %param.14) | copy-start | bytes 221188
  52.9 3.5 %copy-start = (f32[256,768]{1,0:T(8,128)}, f32[256,768]{1,0:T(8,128)S(1)}, u32[]{:S(2)}) copy-start(f32[256,768]{1,0:T(8,128)S(1)} %fusion.9.coef_ref) | copy-start | bytes 2359300
  68.8 6.8 %collective-permute-start = (bf16[16,144,512]{2,1,0:T(8,128)(2,1)S(1)}, bf16[16,144,512]{2,1,0:T(8,128)(2,1)}, u32[]{:S(2)}, u32[]{:S(2)}) collective-permute-start(bf16[16,144,512]{2,1,0:T(8,128)(2,1)S(1)} %fusion.2), channel_id=1, source_target_pairs={{0,4},{4,0},{8,12},{12,8},{16,20},{20,16},{24,28},{28,24},{32,36},... | collective-permute-start | bytes 7077896 | tf_op jit(solution)/shard_map/ppermute | solution.py:342
  78.6 36.2 %copy-start.1 = (f32[512,512,1]{1,0,2:T(8,128)S(1)}, f32[512,512,1]{1,0,2:T(8,128)}, u32[]{:S(2)}) copy-start(f32[512,512,1]{1,0,2:T(8,128)} %constant.120) | copy-start | bytes 3145732

commit v18 on v17

--- a/solution.py
+++ b/solution.py
@@ -129,8 +129,8 @@
 
 
 def grad_kernel(
-    count_ref, ent_p_ref, ent_k_ref, ent_e_ref, image_hat_hbm, coef_ref, ref_hat_hbm, volume_ref,
-    out_hbm, image_buf, ref_buf, acc_ref, out_buf, in_sem, out_sem,
+    count_ref, ent_p_ref, ent_k_ref, ent_e_ref, core_ref, image_hat_hbm, coef_ref, ref_hat_hbm,
+    volume_ref, extra_ref, give_hbm, keep_hbm, image_buf, ref_buf, acc_ref, out_buf, in_sem, out_sem,
 ):
     n_image = image_buf.shape[0] // CHUNK
     n_ref = ref_buf.shape[0] // CHUNK
@@ -173,17 +173,35 @@
 
     lax.fori_loop(0, count_ref[0], body, 0)
 
-    stores = []
     for c in range(n_ref):
         loads[c].wait()
-        vol_half = volume_ref[pl.ds(c * chunk_classes, chunk_classes), :]
-        vol = jnp.concatenate([vol_half, vol_half], axis=1)[:, None, :]
-        ref_part = ref_buf[rows(c)].astype(F32).reshape(chunk_classes, NSHELL, -1)
-        acc_part = acc_ref[rows(c)].reshape(chunk_classes, NSHELL, -1)
-        out_buf[rows(c)] = (acc_part - vol * ref_part).reshape(CHUNK, -1).astype(jnp.bfloat16)
-        copy = pltpu.make_async_copy(out_buf.at[rows(c)], out_hbm.at[rows(c)], out_sem.at[c])
-        copy.start()
-        stores.append(copy)
+    core = core_ref[0]
+    owner_rows = 2 * NSHELL
+    n_chip = give_hbm.shape[0]
+    stores = []
+    for i in range(n_chip):
+        for h, target in enumerate((give_hbm, keep_hbm)):
+            owner = 2 * i + (1 - core if h == 0 else core)
+            r = pl.multiple_of(owner * owner_rows, owner_rows)
+            vol_half = volume_ref[owner]
+            vol = jnp.concatenate([vol_half, vol_half], axis=1)[:, None, :]
+            ref_part = ref_buf[pl.ds(r, owner_rows), :].astype(F32).reshape(2, NSHELL, -1)
+            acc_part = acc_ref[pl.ds(r, owner_rows), :].reshape(2, NSHELL, -1)
+            out_buf[pl.ds(r, owner_rows), :] = (
+                (acc_part - vol * ref_part).reshape(owner_rows, -1).astype(jnp.bfloat16)
+            )
+            slot = 2 * i + h
+            copy = pltpu.make_async_copy(
+                out_buf.at[pl.ds(r, owner_rows)], target.at[i, pl.ds(0, owner_rows)], out_sem.at[slot]
+            )
+            copy.start()
+            stores.append(copy)
+            copy = pltpu.make_async_copy(
+                extra_ref.at[owner], target.at[i, pl.ds(owner_rows, EXTRA)],
+                out_sem.at[2 * n_chip + slot],
+            )
+            copy.start()
+            stores.append(copy)
     for copy in stores:
         copy.wait()
 
@@ -294,22 +312,6 @@
     ).astype(F32)
     volume = jnp.dot(class_pick, coef[:, row_width:], precision=HIGHEST)
     denom_part = jnp.dot(class_pick, post_sum, precision=HIGHEST)
-    numer = pl.pallas_call(
-        grad_kernel,
-        out_shape=jax.ShapeDtypeStruct((ref_rows, row_width), jnp.bfloat16),
-        in_specs=[smem(), smem(), smem(), smem(), anywhere, vmem(), anywhere, vmem()],
-        out_specs=anywhere,
-        scratch_shapes=[
-            pltpu.VMEM((image_rows, row_width), jnp.bfloat16),
-            pltpu.VMEM((ref_rows, row_width), jnp.bfloat16),
-            pltpu.VMEM((ref_rows, row_width), F32),
-            pltpu.VMEM((ref_rows, row_width), jnp.bfloat16),
-            pltpu.SemaphoreType.DMA(((image_rows + ref_rows) // CHUNK,)),
-            pltpu.SemaphoreType.DMA((ref_rows // CHUNK,)),
-        ],
-        compiler_params=params,
-    )(count_arr, ent_p, ent_k, ent_e, image_hat, coef, ref_hat, volume)
-
     core = dp_index % 2
     dest = pose_slot // blocksize
     dest_hit = dest[None, :] == jnp.arange(dp_count, dtype=jnp.int32)[:, None]
@@ -332,13 +334,26 @@
     )
     extra = jnp.zeros((dp_count, EXTRA, row_width), jnp.bfloat16).at[:, 0, :].set(small_row)
     chunk_rows = per_owner * NSHELL
-    chunks = jnp.concatenate(
-        [numer.reshape(dp_count, chunk_rows, row_width), extra], axis=1
-    )
-
-    by_core = chunks.reshape(dp_count // 2, 2, chunk_rows + EXTRA, row_width)
-    keep = lax.dynamic_index_in_dim(by_core, core, axis=1, keepdims=False)
-    give = lax.dynamic_index_in_dim(by_core, 1 - core, axis=1, keepdims=False)
+    half_shape = jax.ShapeDtypeStruct((dp_count // 2, chunk_rows + EXTRA, row_width), jnp.bfloat16)
+    give, keep = pl.pallas_call(
+        grad_kernel,
+        out_shape=(half_shape, half_shape),
+        in_specs=[smem(), smem(), smem(), smem(), smem(), anywhere, vmem(), anywhere, vmem(), vmem()],
+        out_specs=(anywhere, anywhere),
+        scratch_shapes=[
+            pltpu.VMEM((image_rows, row_width), jnp.bfloat16),
+            pltpu.VMEM((ref_rows, row_width), jnp.bfloat16),
+            pltpu.VMEM((ref_rows, row_width), F32),
+            pltpu.VMEM((ref_rows, row_width), jnp.bfloat16),
+            pltpu.SemaphoreType.DMA(((image_rows + ref_rows) // CHUNK,)),
+            pltpu.SemaphoreType.DMA((2 * dp_count,)),
+        ],
+        compiler_params=params,
+    )(
+        count_arr, ent_p, ent_k, ent_e, core.astype(jnp.int32).reshape(1), image_hat, coef,
+        ref_hat, volume.reshape(dp_count, per_owner, -1), extra,
+    )
+
     taken = lax.ppermute(give, "dp", perm=[(i, i ^ 1) for i in range(dp_count)])
     pair_sum = (keep.astype(F32) + taken.astype(F32)).astype(jnp.bfloat16)
     groups = [list(range(q, dp_count, 2)) for q in range(2)]

time: 117 us -> 117 us (level)
  other arithmetic: 11 us -> 8.66 us
  Pallas kernels: 29.7 us -> 31.8 us
  local copies, waits for them, and re-layouts: 5.44 us -> 6.97 us
  matrix products: 5.51 us -> 4.24 us
    pallas_call x1, Pallas kernels: 10.5 us -> 12.6 us  [local(): pl.pallas_call(grad_kernel, out_shape=(half_shape, half_shape), in_specs=...]
    squeeze x1 -> x0, other arithmetic: 1.81 us -> none  [local(): give = lax.dynamic_index_in_dim(by_core, 1 - core, axis=1, keepdims=False)]
    dot_general x1, matrix products: 1.49 us -> 0.22 us  [local(): volume = jnp.dot(class_pick, coef[:, row_width:], precision=HIGHEST)]
where the time goes in v18:
time: 117 us; the launch traced here: 116 us
  blocking collectives  45 us (38%)
  Pallas kernels  31.8 us (27%)
  starting transfers between devices  10.9 us (9%)
  other arithmetic  8.66 us (7%)
  waiting for transfers between devices  7.95 us (7%)
  local copies, waits for them, and re-layouts  6.97 us (6%)
  matrix products  4.24 us (4%)
    all_to_all x1, blocking collectives, local(): lax.all_to_all(pair_sum, 'dp', split_axis=0, concat_axis=0, tiled=True, a...  34.8 us
    pallas_call x1, Pallas kernels, local(): pl.pallas_call(cross_kernel, out_shape=(jax.ShapeDtypeStruct((entries, ro...  19.2 us
    pallas_call x1, Pallas kernels, local(): pl.pallas_call(grad_kernel, out_shape=(half_shape, half_shape), in_specs=...  12.6 us
    all_gather x1, blocking collectives, local(): gathered = lax.all_gather(jnp.stack([top_local, total_local]), 'cls')  10.2 us
    all_to_all x1, starting transfers between devices, local(): lax.all_to_all(jnp.broadcast_to(packed[None], (dp_count,) + packed.shape)...  8.24 us
    ppermute x1, waiting for transfers between devices, local(): taken = lax.ppermute(give, 'dp', perm=[(i, i ^ 1) for i in range(dp_count)])  4.37 us
    all_to_all x1, waiting for transfers between devices, local(): lax.all_to_all(jnp.broadcast_to(packed[None], (dp_count,) + packed.shape)...  3.57 us
    ppermute x1, starting transfers between devices, local(): taken = lax.ppermute(give, 'dp', perm=[(i, i ^ 1) for i in range(dp_count)])  2.65 us
  transfers between devices with their start and end apart: 2, of which 2 were waited for; matrix products, arithmetic and copies ran while one was open for 3% of the time, Pallas kernels for 0%

profile of v18, /device:TPU:0, one launch (start us, length us, event | category | flops | bytes accessed | tf_op | source)
XLA Modules:
  0.0 116.4 jit_solution(1762072382365374892)
XLA Ops:
  0.6 1.3 %broadcast_in_dim.107 = s32[32,2,128]{2,1,0:T(2,128)} broadcast(s32[2,128]{1,0:T(2,128)} %bitcast.38), dimensions={1,2} | broadcast | bytes 33792 | tf_op jit(solution)/shard_map/broadcast_in_dim | solution.py:241
  1.9 8.2 %all-to-all-start = ((s32[32,2,128]{2,1,0:T(2,128)}), s32[32,2,128]{2,1,0:T(2,128)S(1)}, u32[]{:S(2)}, u32[]{:S(2)}) async-start(s32[32,2,128]{2,1,0:T(2,128)} %broadcast_in_dim.107), calls=%async_computation | async-start | bytes 65536 | tf_op jit(solution)/shard_map/all_to_all | solution.py:240
  10.2 0.7 convert_log-plus-one_fusion
  10.8 0.7 and_select_fusion.3
  11.5 0.3 reduce_window_sum.11
  11.8 0.8 fusion.25
  12.7 1.3 %copy.19.wrow_ref = f32[64,1]{1,0:T(8,128)} copy(f32[64,1]{0,1:T(1,128)} %bitcast.41) | data formatting | bytes 512 | tf_op jit(solution)/shard_map/broadcast_in_dim | solution.py:245
  14.0 3.6 %all-to-all-done = s32[32,2,128]{2,1,0:T(2,128)S(1)} async-done(((s32[32,2,128]{2,1,0:T(2,128)}), s32[32,2,128]{2,1,0:T(2,128)S(1)}, u32[]{:S(2)}, u32[]{:S(2)}) %all-to-all-start) | async-done | bytes 32800 | tf_op jit(solution)/shard_map/all_to_all | solution.py:240
  17.6 0.6 copy-done.3
  18.2 19.2 %shard_map.104 = (f32[256,512]{1,0:T(8,128)}, bf16[8192,512]{1,0:T(8,128)(2,1)}, bf16[4096,512]{1,0:T(8,128)(2,1)}, s32[1]{0:T(128)}, s32[256]{0:T(256)}, /*index=5*/s32[256]{0:T(256)}, s32[256]{0:T(256)}, s32[256]{0:T(256)}) custom-call(s32[8192]{0:T(1024)} %bitcast.32, s32[128]{0:T(128)} %pose_ref.1, s32[1]{0:T(128)} %bitcast.2.column_ref, ...), custom_call_target="tpu_custom_call" | custom-call | tf_op jit(solution)/shard_map/pallas_call | solution.py:248
  37.4 0.7 compare_and_fusion.1
  38.1 0.6 broadcast_clamp_fusion
  38.8 0.1 select_reduce_fusion.1
  38.9 0.7 compare_and_fusion
  39.6 1.6 %fusion.27 = (f32[256]{0:T(256)S(1)}, f32[256,36]{0,1:T(8,128)S(1)}) fusion(f32[256]{0:T(256)S(1)} %select_reduce_fusion.1, f32[256,512]{1,0:T(8,128)} %get-tuple-element.30, f32[36,512]{1,0:T(8,128)S(1)} %copy-done.2, pred[256]{0:T(512)(128)(4,1)S(1)} %compare_and_fusion.1), kind=kOutput, calls=%fused_computation.64 | convolution fusion | flops 56650496 | bytes 637184 | tf_op jit(solution)/shard_map/dot_general | solution.py:285
  41.3 0.1 reduce_max.26
  41.4 0.1 reduce_max.27
  41.5 0.1 sub.50
  41.6 0.2 sub.51
  41.8 0.1 reduce_sum.99
  42.0 0.1 reduce_sum.100
  42.1 10.2 %all-gather.1 = f32[4,2,128]{2,1,0:T(2,128)S(1)} all-gather(f32[1,2,128]{2,1,0:T(2,128)S(1)} %maximum_bitcast_fusion), channel_id=2, replica_groups=mesh['dp'=32,'cls'=4] {'cls'}, dimensions={0}, use_global_device_ids=true | all-gather | bytes 5120 | tf_op jit(solution)/shard_map/all_gather | solution.py:293
  52.3 0.1 fusion.11
  52.5 0.1 div.34
  52.6 0.1 div.35
  52.7 0.1 sub.54
  52.8 0.2 sub.55
  53.0 0.1 fusion.14
  53.1 0.1 concatenate.9
  53.2 0.1 copy.21
  53.4 0.6 dynamic_update_slice.6
  54.0 0.9 scatter.4.extra_ref
  54.9 0.8 fusion.4.coef_ref
  55.8 0.2 fusion.2
  56.0 0.7 reshape.178.volume_ref
  56.7 12.6 %shard_map.105 = (bf16[16,144,512]{2,1,0:T(8,128)(2,1)}, bf16[16,144,512]{2,1,0:T(8,128)(2,1)}) custom-call(s32[1]{0:T(128)} %get-tuple-element.24.count_ref, s32[256]{0:T(256)} %get-tuple-element.25.ent_p_ref, s32[256]{0:T(256)} %get-tuple-element.26.ent_k_ref, s32[256]{0:T(256)} %get-tuple-element.27.ent_e_ref, s32[1]{0:T(128)} %bitcast.6.core_ref, ...), custom_call_target="tpu_custom_call" | custom-call | tf_op jit(solution)/shard_map/pallas_call | solution.py:338
  69.3 2.7 %collective-permute-start = (bf16[16,144,512]{2,1,0:T(8,128)(2,1)}, bf16[16,144,512]{2,1,0:T(8,128)(2,1)S(1)}, u32[]{:S(2)}, u32[]{:S(2)}) collective-permute-start(bf16[16,144,512]{2,1,0:T(8,128)(2,1)} %get-tuple-element.33), channel_id=1, source_target_pairs={{0,4},{4,0},{8,12},{12,8},{16,20},{20,16},{24,28},{28,24},{32,36},... | collective-permute-start | bytes 7077896 | tf_op jit(solution)/shard_map/ppermute | solution.py:357
  72.0 4.4 %collective-permute-done = bf16[16,144,512]{2,1,0:T(8,128)(2,1)S(1)} collective-permute-done((bf16[16,144,512]{2,1,0:T(8,128)(2,1)}, bf16[16,144,512]{2,1,0:T(8,128)(2,1)S(1)}, u32[]{:S(2)}, u32[]{:S(2)}) %collective-permute-start) | collective-permute-done | bytes 2359328 | tf_op jit(solution)/shard_map/ppermute | solution.py:357
  76.4 2.4 %add_convert_fusion = bf16[16,144,512]{2,1,0:T(8,128)(2,1)S(1)} fusion(bf16[16,144,512]{2,1,0:T(8,128)(2,1)S(1)} %collective-permute-done, bf16[16,144,512]{2,1,0:T(8,128)(2,1)} %get-tuple-element.32), kind=kLoop, calls=%fused_computation | loop fusion | flops 4718592 | bytes 7077888 | tf_op jit(solution)/shard_map/convert_element_type | solution.py:358
  78.8 34.8 %all_to_all.10 = bf16[16,144,512]{2,1,0:T(8,128)(2,1)S(1)} all-to-all(bf16[16,144,512]{2,1,0:T(8,128)(2,1)S(1)} %add_convert_fusion), channel_id=1, replica_groups={{0,8,16,24,32,40,48,56,64,72,80,88,96,104,112,120},{4,12,20,28,36,44,52..., dimensions={0} | all-to-all | bytes 4718592 | tf_op jit(solution)/shard_map/all_to_all | solution.py:360
  113.6 0.1 reshape.180
  113.6 0.1 fusion.18
  113.7 0.1 fusion.26
  113.8 0.1 eq.115
  113.9 0.1 broadcast_in_dim.119
  114.0 0.6 select_reduce_fusion
  114.7 0.3 convert_reduce_fusion
  115.0 1.4 %fusion = f32[1,2,64,512]{3,2,1,0:T(8,128)} fusion(f32[2,64,512]{2,1,0:T(8,128)S(1)} %bitcast.31, f32[512,512,1]{1,0,2:T(8,128)S(1)} %copy-done.1, f32[2]{0:T(128)S(1)} %broadcast_add_fusion), kind=kOutput, calls=%fused_computation.3 | convolution fusion | flops 402718720 | bytes 1572872 | tf_op jit(solution)/shard_map/dot_general | solution.py:364
  (24 shorter events, 0.3 us)
Async XLA Ops:
  1.9 15.7 %all-to-all-start = ((s32[32,2,128]{2,1,0:T(2,128)}), s32[32,2,128]{2,1,0:T(2,128)S(1)}, u32[]{:S(2)}, u32[]{:S(2)}) async-start(s32[32,2,128]{2,1,0:T(2,128)} %broadcast_in_dim.107), calls=%async_computation | async-start | bytes 65536 | tf_op jit(solution)/shard_map/all_to_all | solution.py:240
  17.6 0.6 copy-start.3
  18.2 21.4 %copy-start.2 = (f32[36,512]{1,0:T(8,128)S(1)}, f32[36,512]{1,0:T(8,128)}, u32[]{:S(2)}) copy-start(f32[36,512]{1,0:T(8,128)} %param.14) | copy-start | bytes 221188
  37.4 18.3 %copy-start.4 = (s32[256]{0:T(256)S(1)}, s32[256]{0:T(256)}, u32[]{:S(2)}) copy-start(s32[256]{0:T(256)} %get-tuple-element.29) | copy-start | bytes 3076
  55.8 0.9 copy-start
  69.3 7.0 %collective-permute-start = (bf16[16,144,512]{2,1,0:T(8,128)(2,1)}, bf16[16,144,512]{2,1,0:T(8,128)(2,1)S(1)}, u32[]{:S(2)}, u32[]{:S(2)}) collective-permute-start(bf16[16,144,512]{2,1,0:T(8,128)(2,1)} %get-tuple-element.33), channel_id=1, source_target_pairs={{0,4},{4,0},{8,12},{12,8},{16,20},{20,16},{24,28},{28,24},{32,36},... | collective-permute-start | bytes 7077896 | tf_op jit(solution)/shard_map/ppermute | solution.py:357
  113.5 1.4 %copy-start.1 = (f32[512,512,1]{1,0,2:T(8,128)S(1)}, f32[512,512,1]{1,0,2:T(8,128)}, u32[]{:S(2)}) copy-start(f32[512,512,1]{1,0,2:T(8,128)} %constant.111) | copy-start | bytes 3145732

commit v19 on v18

--- a/solution.py
+++ b/solution.py
@@ -177,31 +177,32 @@
         loads[c].wait()
     core = core_ref[0]
     owner_rows = 2 * NSHELL
-    n_chip = give_hbm.shape[0]
+    chips_per_chunk = CHUNK // (2 * owner_rows)
     stores = []
-    for i in range(n_chip):
-        for h, target in enumerate((give_hbm, keep_hbm)):
-            owner = 2 * i + (1 - core if h == 0 else core)
-            r = pl.multiple_of(owner * owner_rows, owner_rows)
-            vol_half = volume_ref[owner]
-            vol = jnp.concatenate([vol_half, vol_half], axis=1)[:, None, :]
-            ref_part = ref_buf[pl.ds(r, owner_rows), :].astype(F32).reshape(2, NSHELL, -1)
-            acc_part = acc_ref[pl.ds(r, owner_rows), :].reshape(2, NSHELL, -1)
-            out_buf[pl.ds(r, owner_rows), :] = (
-                (acc_part - vol * ref_part).reshape(owner_rows, -1).astype(jnp.bfloat16)
-            )
-            slot = 2 * i + h
-            copy = pltpu.make_async_copy(
-                out_buf.at[pl.ds(r, owner_rows)], target.at[i, pl.ds(0, owner_rows)], out_sem.at[slot]
-            )
-            copy.start()
-            stores.append(copy)
-            copy = pltpu.make_async_copy(
-                extra_ref.at[owner], target.at[i, pl.ds(owner_rows, EXTRA)],
-                out_sem.at[2 * n_chip + slot],
-            )
-            copy.start()
-            stores.append(copy)
+    for c in range(n_ref):
+        vol_half = volume_ref[pl.ds(c * chunk_classes, chunk_classes), :]
+        vol = jnp.concatenate([vol_half, vol_half], axis=1)[:, None, :]
+        ref_part = ref_buf[rows(c)].astype(F32).reshape(chunk_classes, NSHELL, -1)
+        acc_part = acc_ref[rows(c)].reshape(chunk_classes, NSHELL, -1)
+        out_buf[rows(c)] = (acc_part - vol * ref_part).reshape(CHUNK, -1).astype(jnp.bfloat16)
+        for j in range(chips_per_chunk):
+            i = c * chips_per_chunk + j
+            for h, target in enumerate((give_hbm, keep_hbm)):
+                owner = 2 * i + (1 - core if h == 0 else core)
+                r = pl.multiple_of(owner * owner_rows, owner_rows)
+                slot = 2 * i + h
+                copy = pltpu.make_async_copy(
+                    out_buf.at[pl.ds(r, owner_rows)], target.at[i, pl.ds(0, owner_rows)],
+                    out_sem.at[slot],
+                )
+                copy.start()
+                stores.append(copy)
+                copy = pltpu.make_async_copy(
+                    extra_ref.at[owner], target.at[i, pl.ds(owner_rows, EXTRA)],
+                    out_sem.at[2 * give_hbm.shape[0] + slot],
+                )
+                copy.start()
+                stores.append(copy)
     for copy in stores:
         copy.wait()
 
@@ -351,7 +352,7 @@
         compiler_params=params,
     )(
         count_arr, ent_p, ent_k, ent_e, core.astype(jnp.int32).reshape(1), image_hat, coef,
-        ref_hat, volume.reshape(dp_count, per_owner, -1), extra,
+        ref_hat, volume, extra,
     )
 
     taken = lax.ppermute(give, "dp", perm=[(i, i ^ 1) for i in range(dp_count)])

time: 117 us -> 116 us (level)
    pallas_call x1, Pallas kernels: 12.6 us -> 11.4 us  [local(): pl.pallas_call(grad_kernel, out_shape=(half_shape, half_shape), in_specs=...]
where the time goes in v19:
time: 116 us; the launch traced here: 115 us
  blocking collectives  46.1 us (40%)
  Pallas kernels  30.8 us (27%)
  starting transfers between devices  9.96 us (9%)
  other arithmetic  8.66 us (7%)
  waiting for transfers between devices  7.95 us (7%)
  local copies, waits for them, and re-layouts  6.29 us (5%)
  matrix products  4.9 us (4%)
    all_to_all x1, blocking collectives, local(): lax.all_to_all(pair_sum, 'dp', split_axis=0, concat_axis=0, tiled=True, a...  35.6 us
    pallas_call x1, Pallas kernels, local(): pl.pallas_call(cross_kernel, out_shape=(jax.ShapeDtypeStruct((entries, ro...  19.4 us
    pallas_call x1, Pallas kernels, local(): pl.pallas_call(grad_kernel, out_shape=(half_shape, half_shape), in_specs=...  11.4 us
    all_gather x1, blocking collectives, local(): gathered = lax.all_gather(jnp.stack([top_local, total_local]), 'cls')  10.5 us
    all_to_all x1, starting transfers between devices, local(): lax.all_to_all(jnp.broadcast_to(packed[None], (dp_count,) + packed.shape)...  8.24 us
    ppermute x1, waiting for transfers between devices, local(): taken = lax.ppermute(give, 'dp', perm=[(i, i ^ 1) for i in range(dp_count)])  4.37 us
    all_to_all x1, waiting for transfers between devices, local(): lax.all_to_all(jnp.broadcast_to(packed[None], (dp_count,) + packed.shape)...  3.57 us
    convert_element_type x1, other arithmetic, local(): pair_sum = (keep.astype(F32) + taken.astype(F32)).astype(jnp.bfloat16)  2.4 us
  transfers between devices with their start and end apart: 2, of which 2 were waited for; matrix products, arithmetic and copies ran while one was open for 3% of the time, Pallas kernels for 0%

profile of v19, /device:TPU:0, one launch (start us, length us, event | category | flops | bytes accessed | tf_op | source)
XLA Modules:
  0.0 115.5 jit_solution(1288304447108992941)
XLA Ops:
  0.6 1.3 %broadcast_in_dim.107 = s32[32,2,128]{2,1,0:T(2,128)} broadcast(s32[2,128]{1,0:T(2,128)} %bitcast.38), dimensions={1,2} | broadcast | bytes 33792 | tf_op jit(solution)/shard_map/broadcast_in_dim | solution.py:242
  1.9 8.2 %all-to-all-start = ((s32[32,2,128]{2,1,0:T(2,128)}), s32[32,2,128]{2,1,0:T(2,128)S(1)}, u32[]{:S(2)}, u32[]{:S(2)}) async-start(s32[32,2,128]{2,1,0:T(2,128)} %broadcast_in_dim.107), calls=%async_computation | async-start | bytes 65536 | tf_op jit(solution)/shard_map/all_to_all | solution.py:241
  10.2 0.7 convert_log-plus-one_fusion
  10.8 0.7 and_select_fusion.3
  11.5 0.3 reduce_window_sum.11
  11.8 0.8 fusion.25
  12.7 1.3 %copy.19.wrow_ref = f32[64,1]{1,0:T(8,128)} copy(f32[64,1]{0,1:T(1,128)} %bitcast.41) | data formatting | bytes 512 | tf_op jit(solution)/shard_map/broadcast_in_dim | solution.py:246
  14.0 3.6 %all-to-all-done = s32[32,2,128]{2,1,0:T(2,128)S(1)} async-done(((s32[32,2,128]{2,1,0:T(2,128)}), s32[32,2,128]{2,1,0:T(2,128)S(1)}, u32[]{:S(2)}, u32[]{:S(2)}) %all-to-all-start) | async-done | bytes 32800 | tf_op jit(solution)/shard_map/all_to_all | solution.py:241
  17.6 0.6 copy-done.3
  18.2 19.4 %shard_map.104 = (f32[256,512]{1,0:T(8,128)}, bf16[8192,512]{1,0:T(8,128)(2,1)}, bf16[4096,512]{1,0:T(8,128)(2,1)}, s32[1]{0:T(128)}, s32[256]{0:T(256)}, /*index=5*/s32[256]{0:T(256)}, s32[256]{0:T(256)}, s32[256]{0:T(256)}) custom-call(s32[8192]{0:T(1024)} %bitcast.32, s32[128]{0:T(128)} %pose_ref.1, s32[1]{0:T(128)} %bitcast.2.column_ref, ...), custom_call_target="tpu_custom_call" | custom-call | tf_op jit(solution)/shard_map/pallas_call | solution.py:249
  37.6 0.7 compare_and_fusion.1
  38.3 0.6 broadcast_clamp_fusion
  39.0 0.1 select_reduce_fusion.1
  39.1 0.7 compare_and_fusion
  39.8 1.6 %fusion.27 = (f32[256]{0:T(256)S(1)}, f32[256,36]{0,1:T(8,128)S(1)}) fusion(f32[256]{0:T(256)S(1)} %select_reduce_fusion.1, f32[256,512]{1,0:T(8,128)} %get-tuple-element.30, f32[36,512]{1,0:T(8,128)S(1)} %copy-done.2, pred[256]{0:T(512)(128)(4,1)S(1)} %compare_and_fusion.1), kind=kOutput, calls=%fused_computation.64 | convolution fusion | flops 56650496 | bytes 637184 | tf_op jit(solution)/shard_map/dot_general | solution.py:286
  41.5 0.1 reduce_max.26
  41.6 0.1 reduce_max.27
  41.7 0.1 sub.50
  41.8 0.2 sub.51
  42.0 0.1 reduce_sum.99
  42.1 0.1 reduce_sum.100
  42.3 10.5 %all-gather.1 = f32[4,2,128]{2,1,0:T(2,128)S(1)} all-gather(f32[1,2,128]{2,1,0:T(2,128)S(1)} %maximum_bitcast_fusion), channel_id=2, replica_groups=mesh['dp'=32,'cls'=4] {'cls'}, dimensions={0}, use_global_device_ids=true | all-gather | bytes 5120 | tf_op jit(solution)/shard_map/all_gather | solution.py:294
  52.8 0.1 fusion.11
  52.9 0.1 div.34
  53.0 0.1 div.35
  53.2 0.1 sub.54
  53.2 0.2 sub.55
  53.4 0.1 fusion.14
  53.6 0.1 concatenate.9
  53.7 0.1 copy.21
  53.8 0.6 dynamic_update_slice.6
  54.4 0.9 scatter.4.extra_ref
  55.3 0.8 fusion.4.coef_ref
  56.2 0.9 fusion.2.volume_ref
  57.1 0.0 copy-done
  57.1 11.4 %shard_map.105 = (bf16[16,144,512]{2,1,0:T(8,128)(2,1)}, bf16[16,144,512]{2,1,0:T(8,128)(2,1)}) custom-call(s32[1]{0:T(128)} %get-tuple-element.24.count_ref, s32[256]{0:T(256)} %get-tuple-element.25.ent_p_ref, s32[256]{0:T(256)} %get-tuple-element.26.ent_k_ref, s32[256]{0:T(256)} %get-tuple-element.27.ent_e_ref, s32[1]{0:T(128)} %bitcast.6.core_ref, ...), custom_call_target="tpu_custom_call" | custom-call | tf_op jit(solution)/shard_map/pallas_call | solution.py:339
  68.5 1.7 %collective-permute-start = (bf16[16,144,512]{2,1,0:T(8,128)(2,1)}, bf16[16,144,512]{2,1,0:T(8,128)(2,1)S(1)}, u32[]{:S(2)}, u32[]{:S(2)}) collective-permute-start(bf16[16,144,512]{2,1,0:T(8,128)(2,1)} %get-tuple-element.33), channel_id=1, source_target_pairs={{0,4},{4,0},{8,12},{12,8},{16,20},{20,16},{24,28},{28,24},{32,36},... | collective-permute-start | bytes 7077896 | tf_op jit(solution)/shard_map/ppermute | solution.py:358
  70.2 4.4 %collective-permute-done = bf16[16,144,512]{2,1,0:T(8,128)(2,1)S(1)} collective-permute-done((bf16[16,144,512]{2,1,0:T(8,128)(2,1)}, bf16[16,144,512]{2,1,0:T(8,128)(2,1)S(1)}, u32[]{:S(2)}, u32[]{:S(2)}) %collective-permute-start) | collective-permute-done | bytes 2359328 | tf_op jit(solution)/shard_map/ppermute | solution.py:358
  74.6 2.4 %add_convert_fusion = bf16[16,144,512]{2,1,0:T(8,128)(2,1)S(1)} fusion(bf16[16,144,512]{2,1,0:T(8,128)(2,1)S(1)} %collective-permute-done, bf16[16,144,512]{2,1,0:T(8,128)(2,1)} %get-tuple-element.32), kind=kLoop, calls=%fused_computation | loop fusion | flops 4718592 | bytes 7077888 | tf_op jit(solution)/shard_map/convert_element_type | solution.py:359
  77.0 35.6 %all_to_all.10 = bf16[16,144,512]{2,1,0:T(8,128)(2,1)S(1)} all-to-all(bf16[16,144,512]{2,1,0:T(8,128)(2,1)S(1)} %add_convert_fusion), channel_id=1, replica_groups={{0,8,16,24,32,40,48,56,64,72,80,88,96,104,112,120},{4,12,20,28,36,44,52..., dimensions={0} | all-to-all | bytes 4718592 | tf_op jit(solution)/shard_map/all_to_all | solution.py:361
  112.6 0.1 reshape.176
  112.7 0.1 fusion.18
  112.8 0.1 fusion.26
  112.9 0.1 eq.115
  113.0 0.1 broadcast_in_dim.119
  113.1 0.6 select_reduce_fusion
  113.7 0.3 convert_reduce_fusion
  114.0 1.4 %fusion = f32[1,2,64,512]{3,2,1,0:T(8,128)} fusion(f32[2,64,512]{2,1,0:T(8,128)S(1)} %bitcast.31, f32[512,512,1]{1,0,2:T(8,128)S(1)} %copy-done.1, f32[2]{0:T(128)S(1)} %broadcast_add_fusion), kind=kOutput, calls=%fused_computation.3 | convolution fusion | flops 402718720 | bytes 1572872 | tf_op jit(solution)/shard_map/dot_general | solution.py:365
  (23 shorter events, 0.3 us)
Async XLA Ops:
  1.9 15.7 %all-to-all-start = ((s32[32,2,128]{2,1,0:T(2,128)}), s32[32,2,128]{2,1,0:T(2,128)S(1)}, u32[]{:S(2)}, u32[]{:S(2)}) async-start(s32[32,2,128]{2,1,0:T(2,128)} %broadcast_in_dim.107), calls=%async_computation | async-start | bytes 65536 | tf_op jit(solution)/shard_map/all_to_all | solution.py:241
  17.6 0.6 copy-start.3
  18.2 21.6 %copy-start.2 = (f32[36,512]{1,0:T(8,128)S(1)}, f32[36,512]{1,0:T(8,128)}, u32[]{:S(2)}) copy-start(f32[36,512]{1,0:T(8,128)} %param.14) | copy-start | bytes 221188
  37.6 18.6 %copy-start.4 = (s32[256]{0:T(256)S(1)}, s32[256]{0:T(256)}, u32[]{:S(2)}) copy-start(s32[256]{0:T(256)} %get-tuple-element.29) | copy-start | bytes 3076
  56.2 0.9 copy-start
  68.5 6.1 %collective-permute-start = (bf16[16,144,512]{2,1,0:T(8,128)(2,1)}, bf16[16,144,512]{2,1,0:T(8,128)(2,1)S(1)}, u32[]{:S(2)}, u32[]{:S(2)}) collective-permute-start(bf16[16,144,512]{2,1,0:T(8,128)(2,1)} %get-tuple-element.33), channel_id=1, source_target_pairs={{0,4},{4,0},{8,12},{12,8},{16,20},{20,16},{24,28},{28,24},{32,36},... | collective-permute-start | bytes 7077896 | tf_op jit(solution)/shard_map/ppermute | solution.py:358
  112.6 1.4 %copy-start.1 = (f32[512,512,1]{1,0,2:T(8,128)S(1)}, f32[512,512,1]{1,0,2:T(8,128)}, u32[]{:S(2)}) copy-start(f32[512,512,1]{1,0,2:T(8,128)} %constant.111) | copy-start | bytes 3145732

commit v20 on v19

--- a/solution.py
+++ b/solution.py
@@ -330,10 +330,16 @@
         [ev_hi, ev_lo, send_pos.astype(jnp.bfloat16), den_hi, den_lo], axis=1
     )
     slot_w = small.shape[1]
-    small_row = lax.dynamic_update_slice(
-        jnp.zeros((dp_count, row_width), jnp.bfloat16), small, (0, core * slot_w)
-    )
-    extra = jnp.zeros((dp_count, EXTRA, row_width), jnp.bfloat16).at[:, 0, :].set(small_row)
+    lane_gap = jnp.zeros((dp_count, row_width - 2 * slot_w), jnp.bfloat16)
+    slot_gap = jnp.zeros((dp_count, slot_w), jnp.bfloat16)
+    small_row = jnp.where(
+        core == 0,
+        jnp.concatenate([small, slot_gap, lane_gap], axis=1),
+        jnp.concatenate([slot_gap, small, lane_gap], axis=1),
+    )
+    extra = jnp.concatenate(
+        [small_row[:, None, :], jnp.zeros((dp_count, EXTRA - 1, row_width), jnp.bfloat16)], axis=1
+    )
     chunk_rows = per_owner * NSHELL
     half_shape = jax.ShapeDtypeStruct((dp_count // 2, chunk_rows + EXTRA, row_width), jnp.bfloat16)
     give, keep = pl.pallas_call(

time: 116 us -> 114 us (0.983)
  blocking collectives: 46.1 us -> 43.5 us
  starting transfers between devices: 9.96 us -> 8.33 us
  Pallas kernels: 30.8 us -> 32.1 us
    concatenate x1 -> x8, local copies, waits for them, and re-layouts: 0.13 us -> 2.47 us  [the longest x6 1.08 us: local(): jnp.concatenate([small, slot_gap, lane_gap], axis=1)]
    all_gather x1, blocking collectives: 10.5 us -> 8.4 us  [local(): gathered = lax.all_gather(jnp.stack([top_local, total_local]), 'cls')]
    ppermute x1, starting transfers between devices: 1.71 us -> 0.08 us  [local(): taken = lax.ppermute(give, 'dp', perm=[(i, i ^ 1) for i in range(dp_count)])]
where the time goes in v20:
time: 114 us
  blocking collectives  43.5 us (38%)
  Pallas kernels  32.1 us (28%)
  other arithmetic  8.77 us (8%)
  starting transfers between devices  8.33 us (7%)
  waiting for transfers between devices  8.31 us (7%)
  local copies, waits for them, and re-layouts  7.05 us (6%)
  matrix products  4.9 us (4%)
    all_to_all x1, blocking collectives, local(): lax.all_to_all(pair_sum, 'dp', split_axis=0, concat_axis=0, tiled=True, a...  35.1 us
    pallas_call x1, Pallas kernels, local(): pl.pallas_call(cross_kernel, out_shape=(jax.ShapeDtypeStruct((entries, ro...  20.1 us
    pallas_call x1, Pallas kernels, local(): pl.pallas_call(grad_kernel, out_shape=(half_shape, half_shape), in_specs=...  12.1 us
    all_gather x1, blocking collectives, local(): gathered = lax.all_gather(jnp.stack([top_local, total_local]), 'cls')  8.4 us
    all_to_all x1, starting transfers between devices, local(): lax.all_to_all(jnp.broadcast_to(packed[None], (dp_count,) + packed.shape)...  8.24 us
    ppermute x1, waiting for transfers between devices, local(): taken = lax.ppermute(give, 'dp', perm=[(i, i ^ 1) for i in range(dp_count)])  4.73 us
    all_to_all x1, waiting for transfers between devices, local(): lax.all_to_all(jnp.broadcast_to(packed[None], (dp_count,) + packed.shape)...  3.58 us
    convert_element_type x1, other arithmetic, local(): pair_sum = (keep.astype(F32) + taken.astype(F32)).astype(jnp.bfloat16)  2.4 us
  transfers between devices with their start and end apart: 2, of which 2 were waited for; matrix products, arithmetic and copies ran while one was open for 3% of the time, Pallas kernels for 0%

profile of v20, /device:TPU:0, one launch (start us, length us, event | category | flops | bytes accessed | tf_op | source)
XLA Modules:
  0.0 113.8 jit_solution(18130980477127372675)
XLA Ops:
  0.6 1.3 %broadcast_in_dim.111 = s32[32,2,128]{2,1,0:T(2,128)} broadcast(s32[2,128]{1,0:T(2,128)} %bitcast.48), dimensions={1,2} | broadcast | bytes 33792 | tf_op jit(solution)/shard_map/broadcast_in_dim | solution.py:242
  1.9 8.2 %all-to-all-start = ((s32[32,2,128]{2,1,0:T(2,128)}), s32[32,2,128]{2,1,0:T(2,128)S(1)}, u32[]{:S(2)}, u32[]{:S(2)}) async-start(s32[32,2,128]{2,1,0:T(2,128)} %broadcast_in_dim.111), calls=%async_computation | async-start | bytes 65536 | tf_op jit(solution)/shard_map/all_to_all | solution.py:241
  10.2 0.7 convert_log-plus-one_fusion
  10.8 0.7 and_select_fusion.3
  11.5 0.3 reduce_window_sum.11
  11.8 0.8 fusion.27
  12.7 1.3 %copy.47.wrow_ref = f32[64,1]{1,0:T(8,128)} copy(f32[64,1]{0,1:T(1,128)} %bitcast.51) | data formatting | bytes 512 | tf_op jit(solution)/shard_map/broadcast_in_dim | solution.py:246
  14.0 3.6 %all-to-all-done = s32[32,2,128]{2,1,0:T(2,128)S(1)} async-done(((s32[32,2,128]{2,1,0:T(2,128)}), s32[32,2,128]{2,1,0:T(2,128)S(1)}, u32[]{:S(2)}, u32[]{:S(2)}) %all-to-all-start) | async-done | bytes 32800 | tf_op jit(solution)/shard_map/all_to_all | solution.py:241
  17.6 0.6 copy-done.3
  18.2 20.1 %shard_map.104 = (f32[256,512]{1,0:T(8,128)}, bf16[8192,512]{1,0:T(8,128)(2,1)}, bf16[4096,512]{1,0:T(8,128)(2,1)}, s32[1]{0:T(128)}, s32[256]{0:T(256)}, /*index=5*/s32[256]{0:T(256)}, s32[256]{0:T(256)}, s32[256]{0:T(256)}) custom-call(s32[8192]{0:T(1024)} %bitcast.42, s32[128]{0:T(128)} %pose_ref.1, s32[1]{0:T(128)} %bitcast.2.column_ref, ...), custom_call_target="tpu_custom_call" | custom-call | tf_op jit(solution)/shard_map/pallas_call | solution.py:249
  38.3 0.7 compare_and_fusion.1
  39.0 0.6 broadcast_clamp_fusion
  39.6 0.1 select_reduce_fusion.1
  39.7 0.7 compare_and_fusion
  40.5 1.6 %fusion.29 = (f32[256]{0:T(256)S(1)}, f32[256,36]{0,1:T(8,128)S(1)}) fusion(f32[256]{0:T(256)S(1)} %select_reduce_fusion.1, f32[256,512]{1,0:T(8,128)} %get-tuple-element.18, f32[36,512]{1,0:T(8,128)S(1)} %copy-done.2, pred[256]{0:T(512)(128)(4,1)S(1)} %compare_and_fusion.1), kind=kOutput, calls=%fused_computation.70 | convolution fusion | flops 56650496 | bytes 637184 | tf_op jit(solution)/shard_map/dot_general | solution.py:286
  42.1 0.1 reduce_max.26
  42.3 0.1 reduce_max.27
  42.5 0.2 sub.60
  42.7 0.1 reduce_sum.99
  42.8 0.1 reduce_sum.100
  42.9 8.4 %all-gather.1 = f32[4,2,128]{2,1,0:T(2,128)S(1)} all-gather(f32[1,2,128]{2,1,0:T(2,128)S(1)} %maximum_bitcast_fusion), channel_id=2, replica_groups=mesh['dp'=32,'cls'=4] {'cls'}, dimensions={0}, use_global_device_ids=true | all-gather | bytes 5120 | tf_op jit(solution)/shard_map/all_gather | solution.py:294
  51.4 0.1 fusion.11
  51.5 0.1 copy.50
  51.6 0.1 copy.51
  51.7 0.1 copy.49
  51.9 0.1 div.35
  52.1 0.2 sub.64
  52.3 0.1 fusion.14
  52.5 0.2 copy.53
  52.7 0.1 copy.52
  52.8 0.5 concatenate.46
  53.3 0.5 concatenate.45
  53.8 0.1 broadcast_select_fusion
  53.9 0.9 concatenate.47.extra_ref
  54.8 0.8 fusion.4.coef_ref
  55.7 0.9 fusion.2.volume_ref
  56.6 12.1 %shard_map.105 = (bf16[16,144,512]{2,1,0:T(8,128)(2,1)}, bf16[16,144,512]{2,1,0:T(8,128)(2,1)}) custom-call(s32[1]{0:T(128)} %get-tuple-element.12.count_ref, s32[256]{0:T(256)} %get-tuple-element.13.ent_p_ref, s32[256]{0:T(256)} %get-tuple-element.14.ent_k_ref, s32[256]{0:T(256)} %get-tuple-element.15.ent_e_ref, s32[1]{0:T(128)} %bitcast.6.core_ref, ...), custom_call_target="tpu_custom_call" | custom-call | tf_op jit(solution)/shard_map/pallas_call | solution.py:345
  68.7 0.1 collective-permute-start
  68.7 4.7 %collective-permute-done = bf16[16,144,512]{2,1,0:T(8,128)(2,1)S(1)} collective-permute-done((bf16[16,144,512]{2,1,0:T(8,128)(2,1)}, bf16[16,144,512]{2,1,0:T(8,128)(2,1)S(1)}, u32[]{:S(2)}, u32[]{:S(2)}) %collective-permute-start) | collective-permute-done | bytes 2359328 | tf_op jit(solution)/shard_map/ppermute | solution.py:364
  73.5 2.4 %add_convert_fusion = bf16[16,144,512]{2,1,0:T(8,128)(2,1)S(1)} fusion(bf16[16,144,512]{2,1,0:T(8,128)(2,1)S(1)} %collective-permute-done, bf16[16,144,512]{2,1,0:T(8,128)(2,1)} %get-tuple-element.20), kind=kLoop, calls=%fused_computation | loop fusion | flops 4718592 | bytes 7077888 | tf_op jit(solution)/shard_map/convert_element_type | solution.py:365
  75.9 35.1 %all_to_all.10 = bf16[16,144,512]{2,1,0:T(8,128)(2,1)S(1)} all-to-all(bf16[16,144,512]{2,1,0:T(8,128)(2,1)S(1)} %add_convert_fusion), channel_id=1, replica_groups={{0,8,16,24,32,40,48,56,64,72,80,88,96,104,112,120},{4,12,20,28,36,44,52..., dimensions={0} | all-to-all | bytes 4718592 | tf_op jit(solution)/shard_map/all_to_all | solution.py:367
  111.0 0.1 fusion.18
  111.1 0.1 fusion.28
  111.2 0.1 eq.119
  111.3 0.1 broadcast_in_dim.124
  111.4 0.6 select_reduce_fusion
  112.1 0.3 convert_reduce_fusion
  112.4 1.4 %fusion = f32[1,2,64,512]{3,2,1,0:T(8,128)} fusion(f32[2,64,512]{2,1,0:T(8,128)S(1)} %bitcast.41, f32[512,512,1]{1,0,2:T(8,128)S(1)} %copy-done.1, f32[2]{0:T(128)S(1)} %broadcast_add_fusion), kind=kOutput, calls=%fused_computation.3 | convolution fusion | flops 402718720 | bytes 1572872 | tf_op jit(solution)/shard_map/dot_general | solution.py:371
  (29 shorter events, 0.6 us)
Async XLA Ops:
  1.9 15.7 %all-to-all-start = ((s32[32,2,128]{2,1,0:T(2,128)}), s32[32,2,128]{2,1,0:T(2,128)S(1)}, u32[]{:S(2)}, u32[]{:S(2)}) async-start(s32[32,2,128]{2,1,0:T(2,128)} %broadcast_in_dim.111), calls=%async_computation | async-start | bytes 65536 | tf_op jit(solution)/shard_map/all_to_all | solution.py:241
  17.6 0.6 copy-start.3
  18.2 22.3 %copy-start.2 = (f32[36,512]{1,0:T(8,128)S(1)}, f32[36,512]{1,0:T(8,128)}, u32[]{:S(2)}) copy-start(f32[36,512]{1,0:T(8,128)} %param.12) | copy-start | bytes 221188
  38.3 17.4 %copy-start.4 = (s32[256]{0:T(256)S(1)}, s32[256]{0:T(256)}, u32[]{:S(2)}) copy-start(s32[256]{0:T(256)} %get-tuple-element.17) | copy-start | bytes 3076
  55.7 0.9 copy-start
  68.7 4.8 %collective-permute-start = (bf16[16,144,512]{2,1,0:T(8,128)(2,1)}, bf16[16,144,512]{2,1,0:T(8,128)(2,1)S(1)}, u32[]{:S(2)}, u32[]{:S(2)}) collective-permute-start(bf16[16,144,512]{2,1,0:T(8,128)(2,1)} %get-tuple-element.21), channel_id=1, source_target_pairs={{0,4},{4,0},{8,12},{12,8},{16,20},{20,16},{24,28},{28,24},{32,36},... | collective-permute-start | bytes 7077896 | tf_op jit(solution)/shard_map/ppermute | solution.py:364
  110.9 1.4 %copy-start.1 = (f32[512,512,1]{1,0,2:T(8,128)S(1)}, f32[512,512,1]{1,0,2:T(8,128)}, u32[]{:S(2)}) copy-start(f32[512,512,1]{1,0,2:T(8,128)} %constant.80) | copy-start | bytes 3145732
